TPU v7x, 128 devices: a whole 4x4x4 slice. The times are simulated.
128 devices in a mesh: expert: 16 (over z, x), dp: 8 (over y, core).
Axes of the slice: x: 4, y: 4, z: 4, core: 2. Of those that a mesh axis runs over, the one named last changes fastest.
Arguments:
- tokens: bfloat16 [16, 480, 7168], P('expert', 'dp'), may hold values from -6 to 6
- cotangent: bfloat16 [16, 480, 7168], P('expert', 'dp'), may hold values from -1.5 to 1.5
- counts: int32 [16, 8], replicated, may hold values from 1 to 60, as said below
- w_gate: bfloat16 [16, 7168, 2048], P('expert', None, 'dp'), may hold values from -0.0625 to 0.0625
- w_up: bfloat16 [16, 7168, 2048], P('expert', None, 'dp'), may hold values from -0.0625 to 0.0625
- w_down: bfloat16 [16, 2048, 7168], P('expert', 'dp'), may hold values from -0.125 to 0.125
Outputs:
- outputs: bfloat16 [16, 480, 7168], P('expert', 'dp')
- input_grads: bfloat16 [16, 480, 7168], P('expert', 'dp')
- gate_grad: bfloat16 [16, 7168, 2048], P('expert', None, 'dp')
- up_grad: bfloat16 [16, 7168, 2048], P('expert', None, 'dp')
- down_grad: bfloat16 [16, 2048, 7168], P('expert', 'dp')
Inputs may be any that keep to these rules, and one draw needn't show every extreme that they name: For each expert e below 8, exactly one of experts e and e + 8 is hot: all its counts exceed 40 - 20 and one equals 60; every count of the other is at most 20 and one equals 20.
All inputs are finite; a program needn't handle non-finite values.
Results may differ from a plain program's by a relative error of at most 0.012.
Values may be sent and summed in bfloat16 or wider, within the bound.
No kernel may reach another device: no remote copies, remote signals or barrier semaphores. Data moves between devices by JAX's collectives and lax.ppermute only.
A program may use at most 192 MiB of HBM per device.

v0:
```python
import jax
import jax.numpy as jnp
from jax import lax
from jax.sharding import Mesh, PartitionSpec as P


def silu_slope(value):
    sigma = jax.nn.sigmoid(value)
    return sigma * (1.0 + value * (1.0 - sigma))


def contract_last(left, right):
    return lax.dot_general(
        left, right, (((1,), (1,)), ((), ())), preferred_element_type=jnp.float32
    )


def contract_first(left, right):
    return lax.dot_general(
        left, right, (((0,), (0,)), ((), ())), preferred_element_type=jnp.float32
    )


def expert_work(rows, cot_rows, gate_w, up_w, down_w):
    gate = jnp.dot(rows, gate_w, preferred_element_type=jnp.float32)
    up = jnp.dot(rows, up_w, preferred_element_type=jnp.float32)
    active = jax.nn.silu(gate)
    hidden = (active * up).astype(jnp.bfloat16)
    out_part = jnp.dot(hidden, down_w, preferred_element_type=jnp.float32).astype(jnp.bfloat16)
    out_part, hidden, gate, up = lax.optimization_barrier((out_part, hidden, gate, up))
    active = jax.nn.silu(gate)
    hidden_grad = contract_last(cot_rows, down_w)
    gate_act = (hidden_grad * up * silu_slope(gate)).astype(jnp.bfloat16)
    up_act = (hidden_grad * active).astype(jnp.bfloat16)
    in_part = contract_last(gate_act, gate_w) + contract_last(up_act, up_w)
    gate_term = contract_first(rows, gate_act)
    up_term = contract_first(rows, up_act)
    down_term = contract_first(hidden, cot_rows)
    return (out_part, in_part, gate_term, up_term, down_term)


def y_shift(value, distance):
    size = lax.axis_size("y")
    return lax.ppermute(value, "y", [(i, (i + distance) % size) for i in range(size)])


def core_swap(value):
    return lax.ppermute(value, "core", [(0, 1), (1, 0)])


def gather_rows(block, after=()):
    cut = block.shape[0] // 2
    block, _ = lax.optimization_barrier((block, after))
    from_prev = y_shift(block, 1)
    from_next = y_shift(block, -1)
    far = jnp.concatenate([y_shift(from_prev[:cut], 1), y_shift(from_next[cut:], -1)], axis=0)
    mine = jnp.concatenate([block, from_prev, from_next, far], axis=0)
    return jnp.concatenate([mine, core_swap(mine)], axis=0), (from_prev, from_next)


def scatter_rows(parts):
    half = parts.shape[0] // 2
    slots = half // 4
    cut = slots // 2
    acc = parts[:half].astype(jnp.float32) + core_swap(parts[half:]).astype(jnp.float32)
    own, prev, nxt, far = (acc[k * slots:(k + 1) * slots] for k in range(4))
    prev = prev + jnp.pad(
        y_shift(far[:cut].astype(jnp.bfloat16), -1).astype(jnp.float32), ((0, slots - cut), (0, 0))
    )
    nxt = nxt + jnp.pad(
        y_shift(far[cut:].astype(jnp.bfloat16), 1).astype(jnp.float32), ((cut, 0), (0, 0))
    )
    total = (
        own
        + y_shift(prev.astype(jnp.bfloat16), -1).astype(jnp.float32)
        + y_shift(nxt.astype(jnp.bfloat16), 1).astype(jnp.float32)
    )
    return total.astype(jnp.bfloat16)


def shards(tokens, cotangent, counts, w_gate, w_up, w_down):
    rows_in = tokens[0]
    cot_in = cotangent[0]
    gate_w = w_gate[0]
    up_w = w_up[0]
    down_w = w_down[0]
    expert_pos = lax.axis_index("expert")
    batch_pos = lax.axis_index("y") * lax.axis_size("core") + lax.axis_index("core")
    expert_ids = jnp.arange(counts.shape[0], dtype=jnp.int32)
    batch_ids = jnp.arange(counts.shape[1], dtype=jnp.int32)
    own_counts = jnp.sum(jnp.where(expert_ids[:, None] == expert_pos, counts, 0), axis=0)
    own_total = jnp.sum(jnp.where(batch_ids == batch_pos, own_counts, 0))
    slots = rows_in.shape[0]
    padded = -(-slots // 16) * 16
    valid = (jnp.arange(padded, dtype=jnp.int32) < jnp.minimum(own_total, slots))[:, None]
    grow = ((0, padded - slots), (0, 0))
    masked = jnp.where(valid, jnp.pad(rows_in, grow), 0).astype(rows_in.dtype)
    masked_cot = jnp.where(valid, jnp.pad(cot_in, grow), 0).astype(cot_in.dtype)
    all_rows, first_hop = gather_rows(masked)
    all_cot, _ = gather_rows(masked_cot, first_hop)
    out_part, in_part, gate_term, up_term, down_term = expert_work(
        all_rows, all_cot, gate_w, up_w, down_w
    )
    outputs = scatter_rows(out_part)[:slots]
    input_grads = scatter_rows(in_part.astype(jnp.bfloat16))[:slots]
    gate_grad = gate_term.astype(jnp.bfloat16)
    up_grad = up_term.astype(jnp.bfloat16)
    down_grad = down_term.astype(jnp.bfloat16)
    return (outputs[None], input_grads[None], gate_grad[None], up_grad[None], down_grad[None])


def solution(mesh):
    chips = mesh.shape["dp"] // 2
    split = Mesh(mesh.devices.reshape(mesh.shape["expert"], chips, 2), ("expert", "y", "core"))
    rows = P("expert", ("y", "core"), None)
    cols = P("expert", None, ("y", "core"))

    return jax.shard_map(
        shards,
        mesh=split,
        in_specs=(rows, rows, P(), cols, cols, rows),
        out_specs=(rows, rows, cols, cols, rows),
        check_vma=False,
    )
```

profile of v0, /device:TPU:1, one launch (start us, length us, event | category | flops | bytes accessed | tf_op | source)
XLA Modules:
  0.0 206.9 jit_solution(4562057448885560687)
XLA Ops:
  0.7 0.8 select_reduce_fusion
  1.5 0.6 fusion.23
  2.8 1.9 pad_select_fusion
  4.6 3.6 %collective-permute-start.1 = (bf16[64,7168]{1,0:T(8,128)(2,1)S(1)}, bf16[64,7168]{1,0:T(8,128)(2,1)S(1)}, u32[]{:S(2)}, u32[]{:S(2)}) collective-permute-start(bf16[64,7168]{1,0:T(8,128)(2,1)S(1)} %get-tuple-element.52), channel_id=1, source_target_pairs={{0,6},{2,0},{4,2},{6,4},{1,7},{3,1},{5,3},{7,5},{8,14},{10,8},{12,... | collective-permute-start | bytes 2752520 | tf_op jit(solution)/shard_map/ppermute | solution.py:44
  8.3 0.2 constant_dynamic-update-slice_fusion.4
  8.4 18.9 %collective-permute-done.1 = bf16[64,7168]{1,0:T(8,128)(2,1)S(1)} collective-permute-done((bf16[64,7168]{1,0:T(8,128)(2,1)S(1)}, bf16[64,7168]{1,0:T(8,128)(2,1)S(1)}, u32[]{:S(2)}, u32[]{:S(2)}) %collective-permute-start.1) | collective-permute-done | bytes 917536 | tf_op jit(solution)/shard_map/ppermute | solution.py:44
  27.3 3.1 %collective-permute-done = bf16[64,7168]{1,0:T(8,128)(2,1)S(1)} collective-permute-done((bf16[64,7168]{1,0:T(8,128)(2,1)S(1)}, bf16[64,7168]{1,0:T(8,128)(2,1)S(1)}, u32[]{:S(2)}, u32[]{:S(2)}) %collective-permute-start) | collective-permute-done | bytes 917536 | tf_op jit(solution)/shard_map/ppermute | solution.py:44
  30.4 0.3 collective-permute-start.11
  30.7 1.2 collective-permute-start.10
  31.9 0.2 constant_dynamic-update-slice_fusion.15
  32.1 1.6 collective-permute-start.3
  33.7 0.1 collective-permute-start.2
  33.8 0.2 constant_dynamic-update-slice_fusion.3
  34.0 0.2 constant_dynamic-update-slice_fusion.2
  34.2 27.7 %collective-permute-done.2 = bf16[32,7168]{1,0:T(8,128)(2,1)S(1)} collective-permute-done((bf16[32,7168]{1,0:T(8,128)(2,1)S(1)}, bf16[32,7168]{1,0:T(8,128)(2,1)S(1)}, u32[]{:S(2)}, u32[]{:S(2)}) %collective-permute-start.2) | collective-permute-done | bytes 458784 | tf_op jit(solution)/shard_map/ppermute | solution.py:44
  62.0 2.7 %collective-permute-start.4 = (bf16[256,7168]{1,0:T(8,128)(2,1)S(1)}, bf16[256,7168]{1,0:T(8,128)(2,1)S(1)}, u32[]{:S(2)}, u32[]{:S(2)}) collective-permute-start(bf16[256,7168]{1,0:T(8,128)(2,1)S(1)} %get-tuple-element.47), channel_id=1, source_target_pairs={{0,1},{1,0},{2,3},{3,2},{4,5},{5,4},{6,7},{7,6},{8,9},{9,8},{10,11... | collective-permute-start | bytes 11010056 | tf_op jit(solution)/shard_map/ppermute | solution.py:48
  64.8 0.1 collective-permute-start.13
  64.9 1.5 collective-permute-start.12
  66.4 0.2 constant_dynamic-update-slice_fusion.14
  66.6 0.2 constant_dynamic-update-slice_fusion.13
  66.8 11.3 %collective-permute-done.12 = bf16[32,7168]{1,0:T(8,128)(2,1)S(1)} collective-permute-done((bf16[32,7168]{1,0:T(8,128)(2,1)S(1)}, bf16[32,7168]{1,0:T(8,128)(2,1)S(1)}, u32[]{:S(2)}, u32[]{:S(2)}) %collective-permute-start.12) | collective-permute-done | bytes 458784 | tf_op jit(solution)/shard_map/ppermute | solution.py:44
  78.2 1.1 collective-permute-start.14
  79.4 0.2 constant_dynamic-update-slice_fusion.5
  79.6 1.8 copy-done.3
  81.4 2.1 fusion.11
  83.5 1.7 copy-done.4
  85.1 1.0 copy-done.1
  86.1 2.9 %multiply_convert_fusion.2 = (bf16[512,256]{1,0:T(8,128)(2,1)S(1)}, f32[512,256]{1,0:T(8,128)}) fusion(f32[512,256]{1,0:T(8,128)S(1)} %fusion.11, bf16[512,7168]{1,0:T(8,128)(2,1)S(1)} %constant_dynamic-update-slice_fusion.5, bf16[1,7168,256]{2,1,0:T(8,128)(2,1)S(1)} %copy-done.1), kind=kOutput, calls=%fused_computation.41 | convolution fusion | flops 1879834624 | bytes 12320768 | tf_op jit(solution)/shard_map/dot_general | solution.py:26
  88.9 2.1 %convolution_convert_fusion = bf16[512,7168]{1,0:T(8,128)(2,1)S(1)} fusion(bf16[512,256]{1,0:T(8,128)(2,1)S(1)} %get-tuple-element.14, bf16[1,256,7168]{2,1,0:T(8,128)(2,1)S(1)} %copy-done.2), kind=kOutput, calls=%fused_computation.1 | convolution fusion | flops 1882718208 | bytes 11272192 | tf_op jit(solution)/shard_map/dot_general | solution.py:29
  91.0 2.1 %slice.73 = bf16[256,7168]{1,0:T(8,128)(2,1)} slice(bf16[512,7168]{1,0:T(8,128)(2,1)S(1)} %convolution_convert_fusion), slice={[256:512], [0:7168]} | slice | bytes 7340032 | tf_op jit(solution)/shard_map/slice | solution.py:65
  93.2 0.2 constant_dynamic-update-slice_fusion.16
  93.4 0.8 copy-done.6
  94.2 0.2 copy-done.7
  94.4 2.2 %multiply_convert_fusion = (bf16[512,256]{1,0:T(8,128)(2,1)S(1)}, bf16[512,256]{1,0:T(8,128)(2,1)S(1)}) fusion(f32[512,256]{1,0:T(8,128)S(1)} %copy-done.6, f32[512,256]{1,0:T(8,128)S(1)} %copy-done.7, bf16[512,7168]{1,0:T(8,128)(2,1)S(1)} %constant_dynamic-update-slice_fusion.16, bf16[1,256,7168]{2,1,0:T(8,128)(2,1)S(1)} %copy-done.2), kind=kOutput, calls=%fused_computation.38 | convolution fusion | flops 1880752128 | bytes 12582912 | tf_op jit(solution)/shard_map/dot_general | solution.py:13
  96.5 0.8 copy-done
  97.3 7.3 %fusion.9 = f32[512,7168]{1,0:T(8,128)} fusion(bf16[512,256]{1,0:T(8,128)(2,1)S(1)} %get-tuple-element.30, bf16[1,7168,256]{2,1,0:T(8,128)(2,1)S(1)} %copy-done.3), kind=kOutput, calls=%fused_computation.16 | convolution fusion | flops 1879048192 | bytes 18612224 | tf_op jit(solution)/shard_map/dot_general | solution.py:13
  104.7 11.6 %add_convert_fusion = bf16[512,7168]{1,0:T(8,128)(2,1)} fusion(f32[512,7168]{1,0:T(8,128)} %fusion.9, bf16[512,256]{1,0:T(8,128)(2,1)S(1)} %get-tuple-element.29, bf16[1,7168,256]{2,1,0:T(8,128)(2,1)} %param.10), kind=kOutput, calls=%fused_computation | convolution fusion | flops 1886388224 | bytes 25952256 | tf_op jit(solution)/shard_map/dot_general | solution.py:13
  116.2 4.3 %slice.103 = bf16[256,7168]{1,0:T(8,128)(2,1)} slice(bf16[512,7168]{1,0:T(8,128)(2,1)} %add_convert_fusion), slice={[256:512], [0:7168]} | slice | bytes 7340032 | tf_op jit(solution)/shard_map/slice | solution.py:65
  120.6 0.5 collective-permute-start.15
  121.0 7.3 %fusion.1 = bf16[1,7168,256]{2,1,0:T(8,128)(2,1)} fusion(bf16[512,7168]{1,0:T(8,128)(2,1)} %copy-done.4, bf16[512,256]{1,0:T(8,128)(2,1)S(1)} %get-tuple-element.29), kind=kOutput, calls=%fused_computation.6 | convolution fusion | flops 1880883200 | bytes 11272192 | tf_op jit(solution)/shard_map/dot_general | solution.py:19
  128.4 4.0 %fusion = bf16[1,7168,256]{2,1,0:T(8,128)(2,1)} fusion(bf16[512,7168]{1,0:T(8,128)(2,1)S(1)} %bitcast.50, bf16[512,256]{1,0:T(8,128)(2,1)S(1)} %get-tuple-element.30), kind=kOutput, calls=%fused_computation.5 | convolution fusion | flops 1880883200 | bytes 11272192 | tf_op jit(solution)/shard_map/dot_general | solution.py:19
  132.3 4.0 %fusion.2 = bf16[1,256,7168]{2,1,0:T(8,128)(2,1)} fusion(bf16[512,256]{1,0:T(8,128)(2,1)S(1)} %get-tuple-element.14, bf16[512,7168]{1,0:T(8,128)(2,1)S(1)} %bitcast.46), kind=kOutput, calls=%fused_computation.7 | convolution fusion | flops 1880883200 | bytes 11272192 | tf_op jit(solution)/shard_map/dot_general | solution.py:19
  136.4 6.6 %fusion.24 = (bf16[256,7168]{1,0:T(8,128)(2,1)S(1)}, f32[256,7168]{1,0:T(8,128)}) fusion(bf16[256,7168]{1,0:T(8,128)(2,1)} %collective-permute-done.5, bf16[512,7168]{1,0:T(8,128)(2,1)S(1)} %convolution_convert_fusion), kind=kLoop, calls=%fused_computation.69 | loop fusion | flops 7340032 | bytes 18350080 | tf_op jit(solution)/shard_map/convert.11
  143.0 0.1 collective-permute-start.6
  143.1 1.5 collective-permute-start.8
  144.6 3.5 %fusion.25 = (bf16[256,7168]{1,0:T(8,128)(2,1)S(1)}, f32[256,7168]{1,0:T(8,128)S(1)}) fusion(bf16[256,7168]{1,0:T(8,128)(2,1)} %collective-permute-done.15, bf16[512,7168]{1,0:T(8,128)(2,1)S(1)} %bitcast.44), kind=kLoop, calls=%fused_computation.70 | loop fusion | flops 7340032 | bytes 18350080 | tf_op jit(solution)/shard_map/convert.9
  148.1 1.4 collective-permute-start.16
  149.5 0.2 collective-permute-start.18
  149.7 5.6 %collective-permute-done.6 = bf16[32,7168]{1,0:T(8,128)(2,1)} collective-permute-done((bf16[32,7168]{1,0:T(8,128)(2,1)S(1)}, bf16[32,7168]{1,0:T(8,128)(2,1)}, u32[]{:S(2)}, u32[]{:S(2)}) %collective-permute-start.6) | collective-permute-done | bytes 458784 | tf_op jit(solution)/shard_map/ppermute | solution.py:44
  155.3 1.3 collective-permute-done.8
  156.6 3.2 %fusion.20 = (bf16[64,7168]{1,0:T(8,128)(2,1)S(1)}, bf16[64,7168]{1,0:T(8,128)(2,1)S(1)}, f32[64,7168]{1,0:T(8,128)S(1)}) fusion(f32[256,7168]{1,0:T(8,128)} %get-tuple-element.18, bf16[32,7168]{1,0:T(8,128)(2,1)} %collective-permute-done.6, bf16[32,7168]{1,0:T(8,128)(2,1)} %collective-permute-done.8), kind=kLoop, calls=%fused_computation.33 | loop fusion | flops 2752512 | bytes 10092544 | tf_op jit(solution)/shard_map/convert_element_type | solution.py:75
  159.8 0.2 collective-permute-start.7
  160.0 1.3 collective-permute-start.9
  161.3 3.7 %collective-permute-done.16 = bf16[32,7168]{1,0:T(8,128)(2,1)S(1)} collective-permute-done((bf16[32,7168]{1,0:T(8,128)(2,1)S(1)}, bf16[32,7168]{1,0:T(8,128)(2,1)S(1)}, u32[]{:S(2)}, u32[]{:S(2)}) %collective-permute-start.16) | collective-permute-done | bytes 458784 | tf_op jit(solution)/shard_map/ppermute | solution.py:44
  165.0 1.3 collective-permute-done.18
  166.3 0.4 fusion.16
  166.7 0.2 collective-permute-start.17
  166.9 1.3 collective-permute-start.19
  168.2 16.4 %collective-permute-done.7 = bf16[64,7168]{1,0:T(8,128)(2,1)S(1)} collective-permute-done((bf16[64,7168]{1,0:T(8,128)(2,1)S(1)}, bf16[64,7168]{1,0:T(8,128)(2,1)S(1)}, u32[]{:S(2)}, u32[]{:S(2)}) %collective-permute-start.7) | collective-permute-done | bytes 917536 | tf_op jit(solution)/shard_map/ppermute | solution.py:44
  184.7 1.3 collective-permute-done.9
  186.0 1.2 fusion.21
  187.2 17.2 %collective-permute-done.17 = bf16[64,7168]{1,0:T(8,128)(2,1)S(1)} collective-permute-done((bf16[64,7168]{1,0:T(8,128)(2,1)S(1)}, bf16[64,7168]{1,0:T(8,128)(2,1)S(1)}, u32[]{:S(2)}, u32[]{:S(2)}) %collective-permute-start.17) | collective-permute-done | bytes 917536 | tf_op jit(solution)/shard_map/ppermute | solution.py:44
  204.3 1.3 collective-permute-done.19
  205.6 1.3 fusion.22
  (47 shorter events, 0.6 us)
Async XLA Ops:
  4.6 22.7 %collective-permute-start.1 = (bf16[64,7168]{1,0:T(8,128)(2,1)S(1)}, bf16[64,7168]{1,0:T(8,128)(2,1)S(1)}, u32[]{:S(2)}, u32[]{:S(2)}) collective-permute-start(bf16[64,7168]{1,0:T(8,128)(2,1)S(1)} %get-tuple-element.52), channel_id=1, source_target_pairs={{0,6},{2,0},{4,2},{6,4},{1,7},{3,1},{5,3},{7,5},{8,14},{10,8},{12,... | collective-permute-start | bytes 2752520 | tf_op jit(solution)/shard_map/ppermute | solution.py:44
  8.3 22.2 %collective-permute-start = (bf16[64,7168]{1,0:T(8,128)(2,1)S(1)}, bf16[64,7168]{1,0:T(8,128)(2,1)S(1)}, u32[]{:S(2)}, u32[]{:S(2)}) collective-permute-start(bf16[64,7168]{1,0:T(8,128)(2,1)S(1)} %get-tuple-element.52), channel_id=1, source_target_pairs={{0,2},{2,4},{4,6},{6,0},{1,3},{3,5},{5,7},{7,1},{8,10},{10,12},{12... | collective-permute-start | bytes 2752520 | tf_op jit(solution)/shard_map/ppermute | solution.py:44
  30.4 34.3 %collective-permute-start.11 = (bf16[64,7168]{1,0:T(8,128)(2,1)S(1)}, bf16[64,7168]{1,0:T(8,128)(2,1)S(1)}, u32[]{:S(2)}, u32[]{:S(2)}) collective-permute-start(bf16[64,7168]{1,0:T(8,128)(2,1)S(1)} %get-tuple-element.11), channel_id=1, source_target_pairs={{0,6},{2,0},{4,2},{6,4},{1,7},{3,1},{5,3},{7,5},{8,14},{10,8},{12,... | collective-permute-start | bytes 2752520 | tf_op jit(solution)/shard_map/ppermute | solution.py:44
  30.7 34.2 %collective-permute-start.10 = (bf16[64,7168]{1,0:T(8,128)(2,1)S(1)}, bf16[64,7168]{1,0:T(8,128)(2,1)S(1)}, u32[]{:S(2)}, u32[]{:S(2)}) collective-permute-start(bf16[64,7168]{1,0:T(8,128)(2,1)S(1)} %get-tuple-element.11), channel_id=1, source_target_pairs={{0,2},{2,4},{4,6},{6,0},{1,3},{3,5},{5,7},{7,1},{8,10},{10,12},{12... | collective-permute-start | bytes 2752520 | tf_op jit(solution)/shard_map/ppermute | solution.py:44
  32.1 29.8 %collective-permute-start.3 = (bf16[32,7168]{1,0:T(8,128)(2,1)S(1)}, bf16[32,7168]{1,0:T(8,128)(2,1)S(1)}, u32[]{:S(2)}, u32[]{:S(2)}) collective-permute-start(bf16[32,7168]{1,0:T(8,128)(2,1)S(1)} %slice.91), channel_id=1, source_target_pairs={{0,6},{2,0},{4,2},{6,4},{1,7},{3,1},{5,3},{7,5},{8,14},{10,8},{12,... | collective-permute-start | bytes 1376264 | tf_op jit(solution)/shard_map/ppermute | solution.py:44
  33.7 28.1 %collective-permute-start.2 = (bf16[32,7168]{1,0:T(8,128)(2,1)S(1)}, bf16[32,7168]{1,0:T(8,128)(2,1)S(1)}, u32[]{:S(2)}, u32[]{:S(2)}) collective-permute-start(bf16[32,7168]{1,0:T(8,128)(2,1)S(1)} %slice.90), channel_id=1, source_target_pairs={{0,2},{2,4},{4,6},{6,0},{1,3},{3,5},{5,7},{7,1},{8,10},{10,12},{12... | collective-permute-start | bytes 1376264 | tf_op jit(solution)/shard_map/ppermute | solution.py:44
  62.0 17.4 %collective-permute-start.4 = (bf16[256,7168]{1,0:T(8,128)(2,1)S(1)}, bf16[256,7168]{1,0:T(8,128)(2,1)S(1)}, u32[]{:S(2)}, u32[]{:S(2)}) collective-permute-start(bf16[256,7168]{1,0:T(8,128)(2,1)S(1)} %get-tuple-element.47), channel_id=1, source_target_pairs={{0,1},{1,0},{2,3},{3,2},{4,5},{5,4},{6,7},{7,6},{8,9},{9,8},{10,11... | collective-permute-start | bytes 11010056 | tf_op jit(solution)/shard_map/ppermute | solution.py:48
  64.8 13.4 %collective-permute-start.13 = (bf16[32,7168]{1,0:T(8,128)(2,1)S(1)}, bf16[32,7168]{1,0:T(8,128)(2,1)S(1)}, u32[]{:S(2)}, u32[]{:S(2)}) collective-permute-start(bf16[32,7168]{1,0:T(8,128)(2,1)S(1)} %slice.101), channel_id=1, source_target_pairs={{0,6},{2,0},{4,2},{6,4},{1,7},{3,1},{5,3},{7,5},{8,14},{10,8},{12,... | collective-permute-start | bytes 1376264 | tf_op jit(solution)/shard_map/ppermute | solution.py:44
  64.9 13.2 %collective-permute-start.12 = (bf16[32,7168]{1,0:T(8,128)(2,1)S(1)}, bf16[32,7168]{1,0:T(8,128)(2,1)S(1)}, u32[]{:S(2)}, u32[]{:S(2)}) collective-permute-start(bf16[32,7168]{1,0:T(8,128)(2,1)S(1)} %slice.100), channel_id=1, source_target_pairs={{0,2},{2,4},{4,6},{6,0},{1,3},{3,5},{5,7},{7,1},{8,10},{10,12},{12... | collective-permute-start | bytes 1376264 | tf_op jit(solution)/shard_map/ppermute | solution.py:44
  78.2 14.9 %collective-permute-start.14 = (bf16[256,7168]{1,0:T(8,128)(2,1)S(1)}, bf16[256,7168]{1,0:T(8,128)(2,1)S(1)}, u32[]{:S(2)}, u32[]{:S(2)}) collective-permute-start(bf16[256,7168]{1,0:T(8,128)(2,1)S(1)} %get-tuple-element.43), channel_id=1, source_target_pairs={{0,1},{1,0},{2,3},{3,2},{4,5},{5,4},{6,7},{7,6},{8,9},{9,8},{10,11... | collective-permute-start | bytes 11010056 | tf_op jit(solution)/shard_map/ppermute | solution.py:48
  79.4 2.0 copy-start.3
  81.4 3.7 %copy-start.4 = (bf16[512,7168]{1,0:T(8,128)(2,1)}, bf16[512,7168]{1,0:T(8,128)(2,1)S(1)}, u32[]{:S(2)}) copy-start(bf16[512,7168]{1,0:T(8,128)(2,1)S(1)} %constant_dynamic-update-slice_fusion.5) | copy-start | bytes 22020100
  81.4 4.7 %copy-start.1 = (bf16[1,7168,256]{2,1,0:T(8,128)(2,1)S(1)}, bf16[1,7168,256]{2,1,0:T(8,128)(2,1)}, u32[]{:S(2)}) copy-start(bf16[1,7168,256]{2,1,0:T(8,128)(2,1)} %param.10) | copy-start | bytes 11010052
  86.1 2.9 %copy-start.5 = (f32[512,256]{1,0:T(8,128)}, f32[512,256]{1,0:T(8,128)S(1)}, u32[]{:S(2)}) copy-start(f32[512,256]{1,0:T(8,128)S(1)} %fusion.11) | copy-start | bytes 1572868
  86.1 2.9 %copy-start.2 = (bf16[1,256,7168]{2,1,0:T(8,128)(2,1)S(1)}, bf16[1,256,7168]{2,1,0:T(8,128)(2,1)}, u32[]{:S(2)}) copy-start(bf16[1,256,7168]{2,1,0:T(8,128)(2,1)} %param.11) | copy-start | bytes 11010052
  93.1 43.2 %collective-permute-start.5 = (bf16[256,7168]{1,0:T(8,128)(2,1)}, bf16[256,7168]{1,0:T(8,128)(2,1)}, u32[]{:S(2)}, u32[]{:S(2)}) collective-permute-start(bf16[256,7168]{1,0:T(8,128)(2,1)} %slice.73), channel_id=1, source_target_pairs={{0,1},{1,0},{2,3},{3,2},{4,5},{5,4},{6,7},{7,6},{8,9},{9,8},{10,11... | collective-permute-start | bytes 11010056 | tf_op jit(solution)/shard_map/ppermute | solution.py:48
  93.2 1.0 copy-start.6
  93.2 1.2 copy-start.7
  94.4 3.0 %copy-start = (bf16[512,7168]{1,0:T(8,128)(2,1)}, bf16[512,7168]{1,0:T(8,128)(2,1)S(1)}, u32[]{:S(2)}) copy-start(bf16[512,7168]{1,0:T(8,128)(2,1)S(1)} %constant_dynamic-update-slice_fusion.16) | copy-start | bytes 22020100
  116.2 12.1 %slice-start.4 = ((s8[7340032]{0:T(1024)(128)(4,1)}), s8[4194304]{0:T(1024)(128)(4,1)S(1)}, s32[]{:S(2)}) async-start(s8[7340032]{0:T(1024)(128)(4,1)} %bitcast.49), calls=%async_computation.4 | async-start | bytes 8388608
  120.6 7.8 %slice-start.5 = ((s8[7340032]{0:T(1024)(128)(4,1)}), s8[3145728]{0:T(1024)(128)(4,1)S(1)}, s32[]{:S(2)}) async-start(s8[7340032]{0:T(1024)(128)(4,1)} %bitcast.49), calls=%async_computation.5 | async-start | bytes 6291456
  120.6 24.0 %collective-permute-start.15 = (bf16[256,7168]{1,0:T(8,128)(2,1)}, bf16[256,7168]{1,0:T(8,128)(2,1)}, u32[]{:S(2)}, u32[]{:S(2)}) collective-permute-start(bf16[256,7168]{1,0:T(8,128)(2,1)} %slice.103), channel_id=1, source_target_pairs={{0,1},{1,0},{2,3},{3,2},{4,5},{5,4},{6,7},{7,6},{8,9},{9,8},{10,11... | collective-permute-start | bytes 11010056 | tf_op jit(solution)/shard_map/ppermute | solution.py:48
  121.0 11.3 %slice-start.2 = ((s8[7340032]{0:T(1024)(128)(4,1)}), s8[4194304]{0:T(1024)(128)(4,1)S(1)}, s32[]{:S(2)}) async-start(s8[7340032]{0:T(1024)(128)(4,1)} %bitcast.45), calls=%async_computation.2 | async-start | bytes 8388608
  128.4 4.0 %slice-start.3 = ((s8[7340032]{0:T(1024)(128)(4,1)}), s8[3145728]{0:T(1024)(128)(4,1)S(1)}, s32[]{:S(2)}) async-start(s8[7340032]{0:T(1024)(128)(4,1)} %bitcast.45), calls=%async_computation.3 | async-start | bytes 6291456
  132.3 12.2 %slice-start = ((s8[7340032]{0:T(1024)(128)(4,1)}), s8[4194304]{0:T(1024)(128)(4,1)S(1)}, s32[]{:S(2)}) async-start(s8[7340032]{0:T(1024)(128)(4,1)} %bitcast.43), calls=%async_computation | async-start | bytes 8388608
  136.4 8.2 %slice-start.1 = ((s8[7340032]{0:T(1024)(128)(4,1)}), s8[3145728]{0:T(1024)(128)(4,1)S(1)}, s32[]{:S(2)}) async-start(s8[7340032]{0:T(1024)(128)(4,1)} %bitcast.43), calls=%async_computation.1 | async-start | bytes 6291456
  143.0 12.3 %collective-permute-start.6 = (bf16[32,7168]{1,0:T(8,128)(2,1)S(1)}, bf16[32,7168]{1,0:T(8,128)(2,1)}, u32[]{:S(2)}, u32[]{:S(2)}) collective-permute-start(bf16[32,7168]{1,0:T(8,128)(2,1)S(1)} %get-tuple-element.27), channel_id=1, source_target_pairs={{0,6},{2,0},{4,2},{6,4},{1,7},{3,1},{5,3},{7,5},{8,14},{10,8},{12,... | collective-permute-start | bytes 1376264 | tf_op jit(solution)/shard_map/ppermute | solution.py:44
  143.1 13.5 %collective-permute-start.8 = (bf16[32,7168]{1,0:T(8,128)(2,1)S(1)}, bf16[32,7168]{1,0:T(8,128)(2,1)}, u32[]{:S(2)}, u32[]{:S(2)}) collective-permute-start(bf16[32,7168]{1,0:T(8,128)(2,1)S(1)} %get-tuple-element.28), channel_id=1, source_target_pairs={{0,2},{2,4},{4,6},{6,0},{1,3},{3,5},{5,7},{7,1},{8,10},{10,12},{12... | collective-permute-start | bytes 1376264 | tf_op jit(solution)/shard_map/ppermute | solution.py:44
  148.1 16.9 %collective-permute-start.16 = (bf16[32,7168]{1,0:T(8,128)(2,1)S(1)}, bf16[32,7168]{1,0:T(8,128)(2,1)S(1)}, u32[]{:S(2)}, u32[]{:S(2)}) collective-permute-start(bf16[32,7168]{1,0:T(8,128)(2,1)S(1)} %get-tuple-element.25), channel_id=1, source_target_pairs={{0,6},{2,0},{4,2},{6,4},{1,7},{3,1},{5,3},{7,5},{8,14},{10,8},{12,... | collective-permute-start | bytes 1376264 | tf_op jit(solution)/shard_map/ppermute | solution.py:44
  149.5 16.8 %collective-permute-start.18 = (bf16[32,7168]{1,0:T(8,128)(2,1)S(1)}, bf16[32,7168]{1,0:T(8,128)(2,1)S(1)}, u32[]{:S(2)}, u32[]{:S(2)}) collective-permute-start(bf16[32,7168]{1,0:T(8,128)(2,1)S(1)} %get-tuple-element.26), channel_id=1, source_target_pairs={{0,2},{2,4},{4,6},{6,0},{1,3},{3,5},{5,7},{7,1},{8,10},{10,12},{12... | collective-permute-start | bytes 1376264 | tf_op jit(solution)/shard_map/ppermute | solution.py:44
  159.8 24.9 %collective-permute-start.7 = (bf16[64,7168]{1,0:T(8,128)(2,1)S(1)}, bf16[64,7168]{1,0:T(8,128)(2,1)S(1)}, u32[]{:S(2)}, u32[]{:S(2)}) collective-permute-start(bf16[64,7168]{1,0:T(8,128)(2,1)S(1)} %get-tuple-element.22), channel_id=1, source_target_pairs={{0,6},{2,0},{4,2},{6,4},{1,7},{3,1},{5,3},{7,5},{8,14},{10,8},{12,... | collective-permute-start | bytes 2752520 | tf_op jit(solution)/shard_map/ppermute | solution.py:44
  160.0 26.0 %collective-permute-start.9 = (bf16[64,7168]{1,0:T(8,128)(2,1)S(1)}, bf16[64,7168]{1,0:T(8,128)(2,1)S(1)}, u32[]{:S(2)}, u32[]{:S(2)}) collective-permute-start(bf16[64,7168]{1,0:T(8,128)(2,1)S(1)} %get-tuple-element.23), channel_id=1, source_target_pairs={{0,2},{2,4},{4,6},{6,0},{1,3},{3,5},{5,7},{7,1},{8,10},{10,12},{12... | collective-permute-start | bytes 2752520 | tf_op jit(solution)/shard_map/ppermute | solution.py:44
  166.7 37.6 %collective-permute-start.17 = (bf16[64,7168]{1,0:T(8,128)(2,1)S(1)}, bf16[64,7168]{1,0:T(8,128)(2,1)S(1)}, u32[]{:S(2)}, u32[]{:S(2)}) collective-permute-start(bf16[64,7168]{1,0:T(8,128)(2,1)S(1)} %get-tuple-element.19), channel_id=1, source_target_pairs={{0,6},{2,0},{4,2},{6,4},{1,7},{3,1},{5,3},{7,5},{8,14},{10,8},{12,... | collective-permute-start | bytes 2752520 | tf_op jit(solution)/shard_map/ppermute | solution.py:44
  166.9 38.7 %collective-permute-start.19 = (bf16[64,7168]{1,0:T(8,128)(2,1)S(1)}, bf16[64,7168]{1,0:T(8,128)(2,1)S(1)}, u32[]{:S(2)}, u32[]{:S(2)}) collective-permute-start(bf16[64,7168]{1,0:T(8,128)(2,1)S(1)} %get-tuple-element.20), channel_id=1, source_target_pairs={{0,2},{2,4},{4,6},{6,0},{1,3},{3,5},{5,7},{7,1},{8,10},{10,12},{12... | collective-permute-start | bytes 2752520 | tf_op jit(solution)/shard_map/ppermute | solution.py:44
where the time goes:
time: 207 us
  waiting for transfers between devices  109 us (53%)
  matrix products  43.3 us (21%)
  other arithmetic  19.4 us (9%)
  starting transfers between devices  18.8 us (9%)
  local copies, waits for them, and re-layouts  14.6 us (7%)
    ppermute x16, waiting for transfers between devices, y_shift(): lax.ppermute(value, 'y', [(i, (i + distance) % size) for i in range(size)])  109 us
    dot_general x3, matrix products, contract_last(): lax.dot_general(left, right, (((1,), (1,)), ((), ())), preferred_element_...  21.1 us
    dot_general x3, matrix products, contract_first(): lax.dot_general(left, right, (((0,), (0,)), ((), ())), preferred_element_...  15.3 us
    ppermute x16, starting transfers between devices, y_shift(): lax.ppermute(value, 'y', [(i, (i + distance) % size) for i in range(size)])  14.4 us
    another operation x2, other arithmetic  10.1 us
    unnamed x36, local copies, waits for them, and re-layouts  7.38 us
    slice x2, local copies, waits for them, and re-layouts, scatter_rows(): parts[half:]  6.4 us
    ppermute x4, starting transfers between devices, core_swap(): return lax.ppermute(value, 'core', [(0, 1), (1, 0)])  4.39 us
  transfers between devices with their start and end apart: 20, of which 12 were waited for; matrix products, arithmetic and copies ran while one was open for 32% of the time, Pallas kernels for 0%

commit v1 on v0

--- a/solution.py
+++ b/solution.py
@@ -64,17 +64,13 @@
     cut = slots // 2
     acc = parts[:half].astype(jnp.float32) + core_swap(parts[half:]).astype(jnp.float32)
     own, prev, nxt, far = (acc[k * slots:(k + 1) * slots] for k in range(4))
-    prev = prev + jnp.pad(
-        y_shift(far[:cut].astype(jnp.bfloat16), -1).astype(jnp.float32), ((0, slots - cut), (0, 0))
-    )
-    nxt = nxt + jnp.pad(
-        y_shift(far[cut:].astype(jnp.bfloat16), 1).astype(jnp.float32), ((cut, 0), (0, 0))
-    )
-    total = (
-        own
-        + y_shift(prev.astype(jnp.bfloat16), -1).astype(jnp.float32)
-        + y_shift(nxt.astype(jnp.bfloat16), 1).astype(jnp.float32)
-    )
+    back_prev = y_shift(far[:cut].astype(jnp.bfloat16), -1)
+    back_next = y_shift(far[cut:].astype(jnp.bfloat16), 1)
+    prev = prev + jnp.pad(back_prev.astype(jnp.float32), ((0, slots - cut), (0, 0)))
+    nxt = nxt + jnp.pad(back_next.astype(jnp.float32), ((cut, 0), (0, 0)))
+    from_next = y_shift(prev.astype(jnp.bfloat16), -1)
+    from_prev = y_shift(nxt.astype(jnp.bfloat16), 1)
+    total = own + from_next.astype(jnp.float32) + from_prev.astype(jnp.float32)
     return total.astype(jnp.bfloat16)
 
 

time: 207 us -> 207 us (level)
  no operation moved by 1% of the time
where the time goes in v1:
time: 207 us
  waiting for transfers between devices  109 us (53%)
  matrix products  43.3 us (21%)
  other arithmetic  19.4 us (9%)
  starting transfers between devices  18.8 us (9%)
  local copies, waits for them, and re-layouts  14.6 us (7%)
    ppermute x16, waiting for transfers between devices, y_shift(): lax.ppermute(value, 'y', [(i, (i + distance) % size) for i in range(size)])  109 us
    dot_general x3, matrix products, contract_last(): lax.dot_general(left, right, (((1,), (1,)), ((), ())), preferred_element_...  21.1 us
    dot_general x3, matrix products, contract_first(): lax.dot_general(left, right, (((0,), (0,)), ((), ())), preferred_element_...  15.3 us
    ppermute x16, starting transfers between devices, y_shift(): lax.ppermute(value, 'y', [(i, (i + distance) % size) for i in range(size)])  14.4 us
    another operation x2, other arithmetic  10.1 us
    unnamed x36, local copies, waits for them, and re-layouts  7.38 us
    slice x2, local copies, waits for them, and re-layouts, scatter_rows(): parts[half:]  6.4 us
    ppermute x4, starting transfers between devices, core_swap(): return lax.ppermute(value, 'core', [(0, 1), (1, 0)])  4.39 us
  transfers between devices with their start and end apart: 20, of which 12 were waited for; matrix products, arithmetic and copies ran while one was open for 32% of the time, Pallas kernels for 0%

profile of v1, /device:TPU:1, one launch (start us, length us, event | category | flops | bytes accessed | tf_op | source)
XLA Modules:
  0.0 206.9 jit_solution(4562057448885560687)
XLA Ops:
  0.7 0.8 select_reduce_fusion
  1.5 0.6 fusion.23
  2.8 1.9 pad_select_fusion
  4.6 3.6 %collective-permute-start.1 = (bf16[64,7168]{1,0:T(8,128)(2,1)S(1)}, bf16[64,7168]{1,0:T(8,128)(2,1)S(1)}, u32[]{:S(2)}, u32[]{:S(2)}) collective-permute-start(bf16[64,7168]{1,0:T(8,128)(2,1)S(1)} %get-tuple-element.52), channel_id=1, source_target_pairs={{0,6},{2,0},{4,2},{6,4},{1,7},{3,1},{5,3},{7,5},{8,14},{10,8},{12,... | collective-permute-start | bytes 2752520 | tf_op jit(solution)/shard_map/ppermute | solution.py:44
  8.3 0.2 constant_dynamic-update-slice_fusion.4
  8.4 18.9 %collective-permute-done.1 = bf16[64,7168]{1,0:T(8,128)(2,1)S(1)} collective-permute-done((bf16[64,7168]{1,0:T(8,128)(2,1)S(1)}, bf16[64,7168]{1,0:T(8,128)(2,1)S(1)}, u32[]{:S(2)}, u32[]{:S(2)}) %collective-permute-start.1) | collective-permute-done | bytes 917536 | tf_op jit(solution)/shard_map/ppermute | solution.py:44
  27.3 3.1 %collective-permute-done = bf16[64,7168]{1,0:T(8,128)(2,1)S(1)} collective-permute-done((bf16[64,7168]{1,0:T(8,128)(2,1)S(1)}, bf16[64,7168]{1,0:T(8,128)(2,1)S(1)}, u32[]{:S(2)}, u32[]{:S(2)}) %collective-permute-start) | collective-permute-done | bytes 917536 | tf_op jit(solution)/shard_map/ppermute | solution.py:44
  30.4 0.3 collective-permute-start.11
  30.7 1.2 collective-permute-start.10
  31.9 0.2 constant_dynamic-update-slice_fusion.15
  32.1 1.6 collective-permute-start.3
  33.7 0.1 collective-permute-start.2
  33.8 0.2 constant_dynamic-update-slice_fusion.3
  34.0 0.2 constant_dynamic-update-slice_fusion.2
  34.2 27.7 %collective-permute-done.2 = bf16[32,7168]{1,0:T(8,128)(2,1)S(1)} collective-permute-done((bf16[32,7168]{1,0:T(8,128)(2,1)S(1)}, bf16[32,7168]{1,0:T(8,128)(2,1)S(1)}, u32[]{:S(2)}, u32[]{:S(2)}) %collective-permute-start.2) | collective-permute-done | bytes 458784 | tf_op jit(solution)/shard_map/ppermute | solution.py:44
  62.0 2.7 %collective-permute-start.4 = (bf16[256,7168]{1,0:T(8,128)(2,1)S(1)}, bf16[256,7168]{1,0:T(8,128)(2,1)S(1)}, u32[]{:S(2)}, u32[]{:S(2)}) collective-permute-start(bf16[256,7168]{1,0:T(8,128)(2,1)S(1)} %get-tuple-element.47), channel_id=1, source_target_pairs={{0,1},{1,0},{2,3},{3,2},{4,5},{5,4},{6,7},{7,6},{8,9},{9,8},{10,11... | collective-permute-start | bytes 11010056 | tf_op jit(solution)/shard_map/ppermute | solution.py:48
  64.8 0.1 collective-permute-start.13
  64.9 1.5 collective-permute-start.12
  66.4 0.2 constant_dynamic-update-slice_fusion.14
  66.6 0.2 constant_dynamic-update-slice_fusion.13
  66.8 11.3 %collective-permute-done.12 = bf16[32,7168]{1,0:T(8,128)(2,1)S(1)} collective-permute-done((bf16[32,7168]{1,0:T(8,128)(2,1)S(1)}, bf16[32,7168]{1,0:T(8,128)(2,1)S(1)}, u32[]{:S(2)}, u32[]{:S(2)}) %collective-permute-start.12) | collective-permute-done | bytes 458784 | tf_op jit(solution)/shard_map/ppermute | solution.py:44
  78.2 1.1 collective-permute-start.14
  79.4 0.2 constant_dynamic-update-slice_fusion.5
  79.6 1.8 copy-done.3
  81.4 2.1 fusion.11
  83.5 1.7 copy-done.4
  85.1 1.0 copy-done.1
  86.1 2.9 %multiply_convert_fusion.2 = (bf16[512,256]{1,0:T(8,128)(2,1)S(1)}, f32[512,256]{1,0:T(8,128)}) fusion(f32[512,256]{1,0:T(8,128)S(1)} %fusion.11, bf16[512,7168]{1,0:T(8,128)(2,1)S(1)} %constant_dynamic-update-slice_fusion.5, bf16[1,7168,256]{2,1,0:T(8,128)(2,1)S(1)} %copy-done.1), kind=kOutput, calls=%fused_computation.41 | convolution fusion | flops 1879834624 | bytes 12320768 | tf_op jit(solution)/shard_map/dot_general | solution.py:26
  88.9 2.1 %convolution_convert_fusion = bf16[512,7168]{1,0:T(8,128)(2,1)S(1)} fusion(bf16[512,256]{1,0:T(8,128)(2,1)S(1)} %get-tuple-element.14, bf16[1,256,7168]{2,1,0:T(8,128)(2,1)S(1)} %copy-done.2), kind=kOutput, calls=%fused_computation.1 | convolution fusion | flops 1882718208 | bytes 11272192 | tf_op jit(solution)/shard_map/dot_general | solution.py:29
  91.0 2.1 %slice.73 = bf16[256,7168]{1,0:T(8,128)(2,1)} slice(bf16[512,7168]{1,0:T(8,128)(2,1)S(1)} %convolution_convert_fusion), slice={[256:512], [0:7168]} | slice | bytes 7340032 | tf_op jit(solution)/shard_map/slice | solution.py:65
  93.2 0.2 constant_dynamic-update-slice_fusion.16
  93.4 0.8 copy-done.6
  94.2 0.2 copy-done.7
  94.4 2.2 %multiply_convert_fusion = (bf16[512,256]{1,0:T(8,128)(2,1)S(1)}, bf16[512,256]{1,0:T(8,128)(2,1)S(1)}) fusion(f32[512,256]{1,0:T(8,128)S(1)} %copy-done.6, f32[512,256]{1,0:T(8,128)S(1)} %copy-done.7, bf16[512,7168]{1,0:T(8,128)(2,1)S(1)} %constant_dynamic-update-slice_fusion.16, bf16[1,256,7168]{2,1,0:T(8,128)(2,1)S(1)} %copy-done.2), kind=kOutput, calls=%fused_computation.38 | convolution fusion | flops 1880752128 | bytes 12582912 | tf_op jit(solution)/shard_map/dot_general | solution.py:13
  96.5 0.8 copy-done
  97.3 7.3 %fusion.9 = f32[512,7168]{1,0:T(8,128)} fusion(bf16[512,256]{1,0:T(8,128)(2,1)S(1)} %get-tuple-element.30, bf16[1,7168,256]{2,1,0:T(8,128)(2,1)S(1)} %copy-done.3), kind=kOutput, calls=%fused_computation.16 | convolution fusion | flops 1879048192 | bytes 18612224 | tf_op jit(solution)/shard_map/dot_general | solution.py:13
  104.7 11.6 %add_convert_fusion = bf16[512,7168]{1,0:T(8,128)(2,1)} fusion(f32[512,7168]{1,0:T(8,128)} %fusion.9, bf16[512,256]{1,0:T(8,128)(2,1)S(1)} %get-tuple-element.29, bf16[1,7168,256]{2,1,0:T(8,128)(2,1)} %param.10), kind=kOutput, calls=%fused_computation | convolution fusion | flops 1886388224 | bytes 25952256 | tf_op jit(solution)/shard_map/dot_general | solution.py:13
  116.2 4.3 %slice.103 = bf16[256,7168]{1,0:T(8,128)(2,1)} slice(bf16[512,7168]{1,0:T(8,128)(2,1)} %add_convert_fusion), slice={[256:512], [0:7168]} | slice | bytes 7340032 | tf_op jit(solution)/shard_map/slice | solution.py:65
  120.6 0.5 collective-permute-start.15
  121.0 7.3 %fusion.1 = bf16[1,7168,256]{2,1,0:T(8,128)(2,1)} fusion(bf16[512,7168]{1,0:T(8,128)(2,1)} %copy-done.4, bf16[512,256]{1,0:T(8,128)(2,1)S(1)} %get-tuple-element.29), kind=kOutput, calls=%fused_computation.6 | convolution fusion | flops 1880883200 | bytes 11272192 | tf_op jit(solution)/shard_map/dot_general | solution.py:19
  128.4 4.0 %fusion = bf16[1,7168,256]{2,1,0:T(8,128)(2,1)} fusion(bf16[512,7168]{1,0:T(8,128)(2,1)S(1)} %bitcast.50, bf16[512,256]{1,0:T(8,128)(2,1)S(1)} %get-tuple-element.30), kind=kOutput, calls=%fused_computation.5 | convolution fusion | flops 1880883200 | bytes 11272192 | tf_op jit(solution)/shard_map/dot_general | solution.py:19
  132.3 4.0 %fusion.2 = bf16[1,256,7168]{2,1,0:T(8,128)(2,1)} fusion(bf16[512,256]{1,0:T(8,128)(2,1)S(1)} %get-tuple-element.14, bf16[512,7168]{1,0:T(8,128)(2,1)S(1)} %bitcast.46), kind=kOutput, calls=%fused_computation.7 | convolution fusion | flops 1880883200 | bytes 11272192 | tf_op jit(solution)/shard_map/dot_general | solution.py:19
  136.4 6.6 %fusion.24 = (bf16[256,7168]{1,0:T(8,128)(2,1)S(1)}, f32[256,7168]{1,0:T(8,128)}) fusion(bf16[256,7168]{1,0:T(8,128)(2,1)} %collective-permute-done.5, bf16[512,7168]{1,0:T(8,128)(2,1)S(1)} %convolution_convert_fusion), kind=kLoop, calls=%fused_computation.69 | loop fusion | flops 7340032 | bytes 18350080 | tf_op jit(solution)/shard_map/convert.11
  143.0 0.1 collective-permute-start.6
  143.1 1.5 collective-permute-start.8
  144.6 3.5 %fusion.25 = (bf16[256,7168]{1,0:T(8,128)(2,1)S(1)}, f32[256,7168]{1,0:T(8,128)S(1)}) fusion(bf16[256,7168]{1,0:T(8,128)(2,1)} %collective-permute-done.15, bf16[512,7168]{1,0:T(8,128)(2,1)S(1)} %bitcast.44), kind=kLoop, calls=%fused_computation.70 | loop fusion | flops 7340032 | bytes 18350080 | tf_op jit(solution)/shard_map/convert.9
  148.1 1.4 collective-permute-start.16
  149.5 0.2 collective-permute-start.18
  149.7 5.6 %collective-permute-done.6 = bf16[32,7168]{1,0:T(8,128)(2,1)} collective-permute-done((bf16[32,7168]{1,0:T(8,128)(2,1)S(1)}, bf16[32,7168]{1,0:T(8,128)(2,1)}, u32[]{:S(2)}, u32[]{:S(2)}) %collective-permute-start.6) | collective-permute-done | bytes 458784 | tf_op jit(solution)/shard_map/ppermute | solution.py:44
  155.3 1.3 collective-permute-done.8
  156.6 3.2 %fusion.20 = (bf16[64,7168]{1,0:T(8,128)(2,1)S(1)}, bf16[64,7168]{1,0:T(8,128)(2,1)S(1)}, f32[64,7168]{1,0:T(8,128)S(1)}) fusion(f32[256,7168]{1,0:T(8,128)} %get-tuple-element.18, bf16[32,7168]{1,0:T(8,128)(2,1)} %collective-permute-done.6, bf16[32,7168]{1,0:T(8,128)(2,1)} %collective-permute-done.8), kind=kLoop, calls=%fused_computation.33 | loop fusion | flops 2752512 | bytes 10092544 | tf_op jit(solution)/shard_map/convert_element_type | solution.py:71
  159.8 0.2 collective-permute-start.7
  160.0 1.3 collective-permute-start.9
  161.3 3.7 %collective-permute-done.16 = bf16[32,7168]{1,0:T(8,128)(2,1)S(1)} collective-permute-done((bf16[32,7168]{1,0:T(8,128)(2,1)S(1)}, bf16[32,7168]{1,0:T(8,128)(2,1)S(1)}, u32[]{:S(2)}, u32[]{:S(2)}) %collective-permute-start.16) | collective-permute-done | bytes 458784 | tf_op jit(solution)/shard_map/ppermute | solution.py:44
  165.0 1.3 collective-permute-done.18
  166.3 0.4 fusion.16
  166.7 0.2 collective-permute-start.17
  166.9 1.3 collective-permute-start.19
  168.2 16.4 %collective-permute-done.7 = bf16[64,7168]{1,0:T(8,128)(2,1)S(1)} collective-permute-done((bf16[64,7168]{1,0:T(8,128)(2,1)S(1)}, bf16[64,7168]{1,0:T(8,128)(2,1)S(1)}, u32[]{:S(2)}, u32[]{:S(2)}) %collective-permute-start.7) | collective-permute-done | bytes 917536 | tf_op jit(solution)/shard_map/ppermute | solution.py:44
  184.7 1.3 collective-permute-done.9
  186.0 1.2 fusion.21
  187.2 17.2 %collective-permute-done.17 = bf16[64,7168]{1,0:T(8,128)(2,1)S(1)} collective-permute-done((bf16[64,7168]{1,0:T(8,128)(2,1)S(1)}, bf16[64,7168]{1,0:T(8,128)(2,1)S(1)}, u32[]{:S(2)}, u32[]{:S(2)}) %collective-permute-start.17) | collective-permute-done | bytes 917536 | tf_op jit(solution)/shard_map/ppermute | solution.py:44
  204.3 1.3 collective-permute-done.19
  205.6 1.3 fusion.22
  (47 shorter events, 0.6 us)
Async XLA Ops:
  4.6 22.7 %collective-permute-start.1 = (bf16[64,7168]{1,0:T(8,128)(2,1)S(1)}, bf16[64,7168]{1,0:T(8,128)(2,1)S(1)}, u32[]{:S(2)}, u32[]{:S(2)}) collective-permute-start(bf16[64,7168]{1,0:T(8,128)(2,1)S(1)} %get-tuple-element.52), channel_id=1, source_target_pairs={{0,6},{2,0},{4,2},{6,4},{1,7},{3,1},{5,3},{7,5},{8,14},{10,8},{12,... | collective-permute-start | bytes 2752520 | tf_op jit(solution)/shard_map/ppermute | solution.py:44
  8.3 22.2 %collective-permute-start = (bf16[64,7168]{1,0:T(8,128)(2,1)S(1)}, bf16[64,7168]{1,0:T(8,128)(2,1)S(1)}, u32[]{:S(2)}, u32[]{:S(2)}) collective-permute-start(bf16[64,7168]{1,0:T(8,128)(2,1)S(1)} %get-tuple-element.52), channel_id=1, source_target_pairs={{0,2},{2,4},{4,6},{6,0},{1,3},{3,5},{5,7},{7,1},{8,10},{10,12},{12... | collective-permute-start | bytes 2752520 | tf_op jit(solution)/shard_map/ppermute | solution.py:44
  30.4 34.3 %collective-permute-start.11 = (bf16[64,7168]{1,0:T(8,128)(2,1)S(1)}, bf16[64,7168]{1,0:T(8,128)(2,1)S(1)}, u32[]{:S(2)}, u32[]{:S(2)}) collective-permute-start(bf16[64,7168]{1,0:T(8,128)(2,1)S(1)} %get-tuple-element.11), channel_id=1, source_target_pairs={{0,6},{2,0},{4,2},{6,4},{1,7},{3,1},{5,3},{7,5},{8,14},{10,8},{12,... | collective-permute-start | bytes 2752520 | tf_op jit(solution)/shard_map/ppermute | solution.py:44
  30.7 34.2 %collective-permute-start.10 = (bf16[64,7168]{1,0:T(8,128)(2,1)S(1)}, bf16[64,7168]{1,0:T(8,128)(2,1)S(1)}, u32[]{:S(2)}, u32[]{:S(2)}) collective-permute-start(bf16[64,7168]{1,0:T(8,128)(2,1)S(1)} %get-tuple-element.11), channel_id=1, source_target_pairs={{0,2},{2,4},{4,6},{6,0},{1,3},{3,5},{5,7},{7,1},{8,10},{10,12},{12... | collective-permute-start | bytes 2752520 | tf_op jit(solution)/shard_map/ppermute | solution.py:44
  32.1 29.8 %collective-permute-start.3 = (bf16[32,7168]{1,0:T(8,128)(2,1)S(1)}, bf16[32,7168]{1,0:T(8,128)(2,1)S(1)}, u32[]{:S(2)}, u32[]{:S(2)}) collective-permute-start(bf16[32,7168]{1,0:T(8,128)(2,1)S(1)} %slice.91), channel_id=1, source_target_pairs={{0,6},{2,0},{4,2},{6,4},{1,7},{3,1},{5,3},{7,5},{8,14},{10,8},{12,... | collective-permute-start | bytes 1376264 | tf_op jit(solution)/shard_map/ppermute | solution.py:44
  33.7 28.1 %collective-permute-start.2 = (bf16[32,7168]{1,0:T(8,128)(2,1)S(1)}, bf16[32,7168]{1,0:T(8,128)(2,1)S(1)}, u32[]{:S(2)}, u32[]{:S(2)}) collective-permute-start(bf16[32,7168]{1,0:T(8,128)(2,1)S(1)} %slice.90), channel_id=1, source_target_pairs={{0,2},{2,4},{4,6},{6,0},{1,3},{3,5},{5,7},{7,1},{8,10},{10,12},{12... | collective-permute-start | bytes 1376264 | tf_op jit(solution)/shard_map/ppermute | solution.py:44
  62.0 17.4 %collective-permute-start.4 = (bf16[256,7168]{1,0:T(8,128)(2,1)S(1)}, bf16[256,7168]{1,0:T(8,128)(2,1)S(1)}, u32[]{:S(2)}, u32[]{:S(2)}) collective-permute-start(bf16[256,7168]{1,0:T(8,128)(2,1)S(1)} %get-tuple-element.47), channel_id=1, source_target_pairs={{0,1},{1,0},{2,3},{3,2},{4,5},{5,4},{6,7},{7,6},{8,9},{9,8},{10,11... | collective-permute-start | bytes 11010056 | tf_op jit(solution)/shard_map/ppermute | solution.py:48
  64.8 13.4 %collective-permute-start.13 = (bf16[32,7168]{1,0:T(8,128)(2,1)S(1)}, bf16[32,7168]{1,0:T(8,128)(2,1)S(1)}, u32[]{:S(2)}, u32[]{:S(2)}) collective-permute-start(bf16[32,7168]{1,0:T(8,128)(2,1)S(1)} %slice.101), channel_id=1, source_target_pairs={{0,6},{2,0},{4,2},{6,4},{1,7},{3,1},{5,3},{7,5},{8,14},{10,8},{12,... | collective-permute-start | bytes 1376264 | tf_op jit(solution)/shard_map/ppermute | solution.py:44
  64.9 13.2 %collective-permute-start.12 = (bf16[32,7168]{1,0:T(8,128)(2,1)S(1)}, bf16[32,7168]{1,0:T(8,128)(2,1)S(1)}, u32[]{:S(2)}, u32[]{:S(2)}) collective-permute-start(bf16[32,7168]{1,0:T(8,128)(2,1)S(1)} %slice.100), channel_id=1, source_target_pairs={{0,2},{2,4},{4,6},{6,0},{1,3},{3,5},{5,7},{7,1},{8,10},{10,12},{12... | collective-permute-start | bytes 1376264 | tf_op jit(solution)/shard_map/ppermute | solution.py:44
  78.2 14.9 %collective-permute-start.14 = (bf16[256,7168]{1,0:T(8,128)(2,1)S(1)}, bf16[256,7168]{1,0:T(8,128)(2,1)S(1)}, u32[]{:S(2)}, u32[]{:S(2)}) collective-permute-start(bf16[256,7168]{1,0:T(8,128)(2,1)S(1)} %get-tuple-element.43), channel_id=1, source_target_pairs={{0,1},{1,0},{2,3},{3,2},{4,5},{5,4},{6,7},{7,6},{8,9},{9,8},{10,11... | collective-permute-start | bytes 11010056 | tf_op jit(solution)/shard_map/ppermute | solution.py:48
  79.4 2.0 copy-start.3
  81.4 3.7 %copy-start.4 = (bf16[512,7168]{1,0:T(8,128)(2,1)}, bf16[512,7168]{1,0:T(8,128)(2,1)S(1)}, u32[]{:S(2)}) copy-start(bf16[512,7168]{1,0:T(8,128)(2,1)S(1)} %constant_dynamic-update-slice_fusion.5) | copy-start | bytes 22020100
  81.4 4.7 %copy-start.1 = (bf16[1,7168,256]{2,1,0:T(8,128)(2,1)S(1)}, bf16[1,7168,256]{2,1,0:T(8,128)(2,1)}, u32[]{:S(2)}) copy-start(bf16[1,7168,256]{2,1,0:T(8,128)(2,1)} %param.10) | copy-start | bytes 11010052
  86.1 2.9 %copy-start.5 = (f32[512,256]{1,0:T(8,128)}, f32[512,256]{1,0:T(8,128)S(1)}, u32[]{:S(2)}) copy-start(f32[512,256]{1,0:T(8,128)S(1)} %fusion.11) | copy-start | bytes 1572868
  86.1 2.9 %copy-start.2 = (bf16[1,256,7168]{2,1,0:T(8,128)(2,1)S(1)}, bf16[1,256,7168]{2,1,0:T(8,128)(2,1)}, u32[]{:S(2)}) copy-start(bf16[1,256,7168]{2,1,0:T(8,128)(2,1)} %param.11) | copy-start | bytes 11010052
  93.1 43.2 %collective-permute-start.5 = (bf16[256,7168]{1,0:T(8,128)(2,1)}, bf16[256,7168]{1,0:T(8,128)(2,1)}, u32[]{:S(2)}, u32[]{:S(2)}) collective-permute-start(bf16[256,7168]{1,0:T(8,128)(2,1)} %slice.73), channel_id=1, source_target_pairs={{0,1},{1,0},{2,3},{3,2},{4,5},{5,4},{6,7},{7,6},{8,9},{9,8},{10,11... | collective-permute-start | bytes 11010056 | tf_op jit(solution)/shard_map/ppermute | solution.py:48
  93.2 1.0 copy-start.6
  93.2 1.2 copy-start.7
  94.4 3.0 %copy-start = (bf16[512,7168]{1,0:T(8,128)(2,1)}, bf16[512,7168]{1,0:T(8,128)(2,1)S(1)}, u32[]{:S(2)}) copy-start(bf16[512,7168]{1,0:T(8,128)(2,1)S(1)} %constant_dynamic-update-slice_fusion.16) | copy-start | bytes 22020100
  116.2 12.1 %slice-start.4 = ((s8[7340032]{0:T(1024)(128)(4,1)}), s8[4194304]{0:T(1024)(128)(4,1)S(1)}, s32[]{:S(2)}) async-start(s8[7340032]{0:T(1024)(128)(4,1)} %bitcast.49), calls=%async_computation.4 | async-start | bytes 8388608
  120.6 7.8 %slice-start.5 = ((s8[7340032]{0:T(1024)(128)(4,1)}), s8[3145728]{0:T(1024)(128)(4,1)S(1)}, s32[]{:S(2)}) async-start(s8[7340032]{0:T(1024)(128)(4,1)} %bitcast.49), calls=%async_computation.5 | async-start | bytes 6291456
  120.6 24.0 %collective-permute-start.15 = (bf16[256,7168]{1,0:T(8,128)(2,1)}, bf16[256,7168]{1,0:T(8,128)(2,1)}, u32[]{:S(2)}, u32[]{:S(2)}) collective-permute-start(bf16[256,7168]{1,0:T(8,128)(2,1)} %slice.103), channel_id=1, source_target_pairs={{0,1},{1,0},{2,3},{3,2},{4,5},{5,4},{6,7},{7,6},{8,9},{9,8},{10,11... | collective-permute-start | bytes 11010056 | tf_op jit(solution)/shard_map/ppermute | solution.py:48
  121.0 11.3 %slice-start.2 = ((s8[7340032]{0:T(1024)(128)(4,1)}), s8[4194304]{0:T(1024)(128)(4,1)S(1)}, s32[]{:S(2)}) async-start(s8[7340032]{0:T(1024)(128)(4,1)} %bitcast.45), calls=%async_computation.2 | async-start | bytes 8388608
  128.4 4.0 %slice-start.3 = ((s8[7340032]{0:T(1024)(128)(4,1)}), s8[3145728]{0:T(1024)(128)(4,1)S(1)}, s32[]{:S(2)}) async-start(s8[7340032]{0:T(1024)(128)(4,1)} %bitcast.45), calls=%async_computation.3 | async-start | bytes 6291456
  132.3 12.2 %slice-start = ((s8[7340032]{0:T(1024)(128)(4,1)}), s8[4194304]{0:T(1024)(128)(4,1)S(1)}, s32[]{:S(2)}) async-start(s8[7340032]{0:T(1024)(128)(4,1)} %bitcast.43), calls=%async_computation | async-start | bytes 8388608
  136.4 8.2 %slice-start.1 = ((s8[7340032]{0:T(1024)(128)(4,1)}), s8[3145728]{0:T(1024)(128)(4,1)S(1)}, s32[]{:S(2)}) async-start(s8[7340032]{0:T(1024)(128)(4,1)} %bitcast.43), calls=%async_computation.1 | async-start | bytes 6291456
  143.0 12.3 %collective-permute-start.6 = (bf16[32,7168]{1,0:T(8,128)(2,1)S(1)}, bf16[32,7168]{1,0:T(8,128)(2,1)}, u32[]{:S(2)}, u32[]{:S(2)}) collective-permute-start(bf16[32,7168]{1,0:T(8,128)(2,1)S(1)} %get-tuple-element.27), channel_id=1, source_target_pairs={{0,6},{2,0},{4,2},{6,4},{1,7},{3,1},{5,3},{7,5},{8,14},{10,8},{12,... | collective-permute-start | bytes 1376264 | tf_op jit(solution)/shard_map/ppermute | solution.py:44
  143.1 13.5 %collective-permute-start.8 = (bf16[32,7168]{1,0:T(8,128)(2,1)S(1)}, bf16[32,7168]{1,0:T(8,128)(2,1)}, u32[]{:S(2)}, u32[]{:S(2)}) collective-permute-start(bf16[32,7168]{1,0:T(8,128)(2,1)S(1)} %get-tuple-element.28), channel_id=1, source_target_pairs={{0,2},{2,4},{4,6},{6,0},{1,3},{3,5},{5,7},{7,1},{8,10},{10,12},{12... | collective-permute-start | bytes 1376264 | tf_op jit(solution)/shard_map/ppermute | solution.py:44
  148.1 16.9 %collective-permute-start.16 = (bf16[32,7168]{1,0:T(8,128)(2,1)S(1)}, bf16[32,7168]{1,0:T(8,128)(2,1)S(1)}, u32[]{:S(2)}, u32[]{:S(2)}) collective-permute-start(bf16[32,7168]{1,0:T(8,128)(2,1)S(1)} %get-tuple-element.25), channel_id=1, source_target_pairs={{0,6},{2,0},{4,2},{6,4},{1,7},{3,1},{5,3},{7,5},{8,14},{10,8},{12,... | collective-permute-start | bytes 1376264 | tf_op jit(solution)/shard_map/ppermute | solution.py:44
  149.5 16.8 %collective-permute-start.18 = (bf16[32,7168]{1,0:T(8,128)(2,1)S(1)}, bf16[32,7168]{1,0:T(8,128)(2,1)S(1)}, u32[]{:S(2)}, u32[]{:S(2)}) collective-permute-start(bf16[32,7168]{1,0:T(8,128)(2,1)S(1)} %get-tuple-element.26), channel_id=1, source_target_pairs={{0,2},{2,4},{4,6},{6,0},{1,3},{3,5},{5,7},{7,1},{8,10},{10,12},{12... | collective-permute-start | bytes 1376264 | tf_op jit(solution)/shard_map/ppermute | solution.py:44
  159.8 24.9 %collective-permute-start.7 = (bf16[64,7168]{1,0:T(8,128)(2,1)S(1)}, bf16[64,7168]{1,0:T(8,128)(2,1)S(1)}, u32[]{:S(2)}, u32[]{:S(2)}) collective-permute-start(bf16[64,7168]{1,0:T(8,128)(2,1)S(1)} %get-tuple-element.22), channel_id=1, source_target_pairs={{0,6},{2,0},{4,2},{6,4},{1,7},{3,1},{5,3},{7,5},{8,14},{10,8},{12,... | collective-permute-start | bytes 2752520 | tf_op jit(solution)/shard_map/ppermute | solution.py:44
  160.0 26.0 %collective-permute-start.9 = (bf16[64,7168]{1,0:T(8,128)(2,1)S(1)}, bf16[64,7168]{1,0:T(8,128)(2,1)S(1)}, u32[]{:S(2)}, u32[]{:S(2)}) collective-permute-start(bf16[64,7168]{1,0:T(8,128)(2,1)S(1)} %get-tuple-element.23), channel_id=1, source_target_pairs={{0,2},{2,4},{4,6},{6,0},{1,3},{3,5},{5,7},{7,1},{8,10},{10,12},{12... | collective-permute-start | bytes 2752520 | tf_op jit(solution)/shard_map/ppermute | solution.py:44
  166.7 37.6 %collective-permute-start.17 = (bf16[64,7168]{1,0:T(8,128)(2,1)S(1)}, bf16[64,7168]{1,0:T(8,128)(2,1)S(1)}, u32[]{:S(2)}, u32[]{:S(2)}) collective-permute-start(bf16[64,7168]{1,0:T(8,128)(2,1)S(1)} %get-tuple-element.19), channel_id=1, source_target_pairs={{0,6},{2,0},{4,2},{6,4},{1,7},{3,1},{5,3},{7,5},{8,14},{10,8},{12,... | collective-permute-start | bytes 2752520 | tf_op jit(solution)/shard_map/ppermute | solution.py:44
  166.9 38.7 %collective-permute-start.19 = (bf16[64,7168]{1,0:T(8,128)(2,1)S(1)}, bf16[64,7168]{1,0:T(8,128)(2,1)S(1)}, u32[]{:S(2)}, u32[]{:S(2)}) collective-permute-start(bf16[64,7168]{1,0:T(8,128)(2,1)S(1)} %get-tuple-element.20), channel_id=1, source_target_pairs={{0,2},{2,4},{4,6},{6,0},{1,3},{3,5},{5,7},{7,1},{8,10},{10,12},{12... | collective-permute-start | bytes 2752520 | tf_op jit(solution)/shard_map/ppermute | solution.py:44

commit v2 on v1

--- a/solution.py
+++ b/solution.py
@@ -48,16 +48,6 @@
     return lax.ppermute(value, "core", [(0, 1), (1, 0)])
 
 
-def gather_rows(block, after=()):
-    cut = block.shape[0] // 2
-    block, _ = lax.optimization_barrier((block, after))
-    from_prev = y_shift(block, 1)
-    from_next = y_shift(block, -1)
-    far = jnp.concatenate([y_shift(from_prev[:cut], 1), y_shift(from_next[cut:], -1)], axis=0)
-    mine = jnp.concatenate([block, from_prev, from_next, far], axis=0)
-    return jnp.concatenate([mine, core_swap(mine)], axis=0), (from_prev, from_next)
-
-
 def scatter_rows(parts):
     half = parts.shape[0] // 2
     slots = half // 4
@@ -92,8 +82,18 @@
     grow = ((0, padded - slots), (0, 0))
     masked = jnp.where(valid, jnp.pad(rows_in, grow), 0).astype(rows_in.dtype)
     masked_cot = jnp.where(valid, jnp.pad(cot_in, grow), 0).astype(cot_in.dtype)
-    all_rows, first_hop = gather_rows(masked)
-    all_cot, _ = gather_rows(masked_cot, first_hop)
+    cut = masked.shape[0] // 2
+    tok_prev = y_shift(masked, 1)
+    tok_next = y_shift(masked, -1)
+    got_prev = y_shift(jnp.concatenate([tok_prev[:cut], masked_cot], axis=0), 1)
+    got_next = y_shift(jnp.concatenate([tok_next[cut:], masked_cot], axis=0), -1)
+    tok_far_a, cot_prev = got_prev[:cut], got_prev[cut:]
+    tok_far_b, cot_next = got_next[:cut], got_next[cut:]
+    tok_mine = jnp.concatenate([masked, tok_prev, tok_next, tok_far_a, tok_far_b], axis=0)
+    all_rows = jnp.concatenate([tok_mine, core_swap(tok_mine)], axis=0)
+    cot_far = jnp.concatenate([y_shift(cot_prev[:cut], 1), y_shift(cot_next[cut:], -1)], axis=0)
+    cot_mine = jnp.concatenate([masked_cot, cot_prev, cot_next, cot_far], axis=0)
+    all_cot = jnp.concatenate([cot_mine, core_swap(cot_mine)], axis=0)
     out_part, in_part, gate_term, up_term, down_term = expert_work(
         all_rows, all_cot, gate_w, up_w, down_w
     )

time: 207 us -> 205 us (level)
  waiting for transfers between devices: 109 us -> 105 us
    ppermute x16 -> x14, waiting for transfers between devices: 109 us -> 105 us  [y_shift(): lax.ppermute(value, 'y', [(i, (i + distance) % size) for i in range(size)])]
    ppermute x4, starting transfers between devices: 4.39 us -> 7.34 us  [core_swap(): return lax.ppermute(value, 'core', [(0, 1), (1, 0)])]
    ppermute x16 -> x14, starting transfers between devices: 14.4 us -> 12.8 us  [y_shift(): lax.ppermute(value, 'y', [(i, (i + distance) % size) for i in range(size)])]
    unnamed x36 -> x34, local copies, waits for them, and re-layouts: 7.38 us -> 7.13 us
  transfers between devices with their start and end apart: 20 -> 18, of which waited for: 12 -> 12; matrix products, arithmetic and copies ran while one was open for 32% -> 32% of each run, Pallas kernels for 0% -> 0%
where the time goes in v2:
time: 205 us
  waiting for transfers between devices  105 us (51%)
  matrix products  43.3 us (21%)
  starting transfers between devices  20.2 us (10%)
  other arithmetic  19.9 us (10%)
  local copies, waits for them, and re-layouts  14.4 us (7%)
    ppermute x14, waiting for transfers between devices, y_shift(): lax.ppermute(value, 'y', [(i, (i + distance) % size) for i in range(size)])  105 us
    dot_general x3, matrix products, contract_last(): lax.dot_general(left, right, (((1,), (1,)), ((), ())), preferred_element_...  21.1 us
    dot_general x3, matrix products, contract_first(): lax.dot_general(left, right, (((0,), (0,)), ((), ())), preferred_element_...  15.3 us
    ppermute x14, starting transfers between devices, y_shift(): lax.ppermute(value, 'y', [(i, (i + distance) % size) for i in range(size)])  12.8 us
    another operation x2, other arithmetic  10.1 us
    ppermute x4, starting transfers between devices, core_swap(): return lax.ppermute(value, 'core', [(0, 1), (1, 0)])  7.34 us
    unnamed x34, local copies, waits for them, and re-layouts  7.13 us
    slice x2, local copies, waits for them, and re-layouts, scatter_rows(): parts[half:]  6.38 us
  transfers between devices with their start and end apart: 18, of which 12 were waited for; matrix products, arithmetic and copies ran while one was open for 32% of the time, Pallas kernels for 0%

profile of v2, /device:TPU:1, one launch (start us, length us, event | category | flops | bytes accessed | tf_op | source)
XLA Modules:
  0.0 204.8 jit_solution(8818172373566033891)
XLA Ops:
  0.7 0.8 select_reduce_fusion
  1.5 0.6 fusion.23
  2.8 2.0 constant_dynamic-update-slice_fusion.9
  4.8 3.6 %collective-permute-start.1 = (bf16[64,7168]{1,0:T(8,128)(2,1)S(1)}, bf16[64,7168]{1,0:T(8,128)(2,1)S(1)}, u32[]{:S(2)}, u32[]{:S(2)}) collective-permute-start(bf16[64,7168]{1,0:T(8,128)(2,1)S(1)} %get-tuple-element.54), channel_id=1, source_target_pairs={{0,6},{2,0},{4,2},{6,4},{1,7},{3,1},{5,3},{7,5},{8,14},{10,8},{12,... | collective-permute-start | bytes 2752520 | tf_op jit(solution)/shard_map/ppermute | solution.py:44
  8.4 0.1 constant_dynamic-update-slice_fusion.6
  8.6 18.9 %collective-permute-done.1 = bf16[64,7168]{1,0:T(8,128)(2,1)S(1)} collective-permute-done((bf16[64,7168]{1,0:T(8,128)(2,1)S(1)}, bf16[64,7168]{1,0:T(8,128)(2,1)S(1)}, u32[]{:S(2)}, u32[]{:S(2)}) %collective-permute-start.1) | collective-permute-done | bytes 917536 | tf_op jit(solution)/shard_map/ppermute | solution.py:44
  27.5 3.1 %collective-permute-done = bf16[64,7168]{1,0:T(8,128)(2,1)S(1)} collective-permute-done((bf16[64,7168]{1,0:T(8,128)(2,1)S(1)}, bf16[64,7168]{1,0:T(8,128)(2,1)S(1)}, u32[]{:S(2)}, u32[]{:S(2)}) %collective-permute-start) | collective-permute-done | bytes 917536 | tf_op jit(solution)/shard_map/ppermute | solution.py:44
  30.6 0.3 pad_maximum_fusion
  31.0 0.4 collective-permute-start.3
  31.4 1.1 collective-permute-start.2
  32.5 0.2 constant_dynamic-update-slice_fusion.1
  32.7 0.2 constant_dynamic-update-slice_fusion
  32.9 29.6 %collective-permute-done.2 = bf16[96,7168]{1,0:T(8,128)(2,1)S(1)} collective-permute-done((bf16[96,7168]{1,0:T(8,128)(2,1)S(1)}, bf16[96,7168]{1,0:T(8,128)(2,1)S(1)}, u32[]{:S(2)}, u32[]{:S(2)}) %collective-permute-start.2) | collective-permute-done | bytes 1376288 | tf_op jit(solution)/shard_map/ppermute | solution.py:44
  62.5 0.1 fusion.29
  62.6 0.1 fusion.28
  62.7 0.2 collective-permute-start.11
  62.9 1.3 collective-permute-start.10
  64.3 3.2 %collective-permute-start.4 = (bf16[256,7168]{1,0:T(8,128)(2,1)S(1)}, bf16[256,7168]{1,0:T(8,128)(2,1)S(1)}, u32[]{:S(2)}, u32[]{:S(2)}) collective-permute-start(bf16[256,7168]{1,0:T(8,128)(2,1)S(1)} %get-tuple-element.37), channel_id=1, source_target_pairs={{0,1},{1,0},{2,3},{3,2},{4,5},{5,4},{6,7},{7,6},{8,9},{9,8},{10,11... | collective-permute-start | bytes 11010056 | tf_op jit(solution)/shard_map/ppermute | solution.py:48
  67.5 0.2 slice_dynamic-update-slice_fusion.3
  67.7 0.2 slice_dynamic-update-slice_fusion.1
  67.9 5.7 %collective-permute-done.10 = bf16[32,7168]{1,0:T(8,128)(2,1)S(1)} collective-permute-done((bf16[32,7168]{1,0:T(8,128)(2,1)S(1)}, bf16[32,7168]{1,0:T(8,128)(2,1)S(1)}, u32[]{:S(2)}, u32[]{:S(2)}) %collective-permute-start.10) | collective-permute-done | bytes 458784 | tf_op jit(solution)/shard_map/ppermute | solution.py:44
  73.7 3.6 %collective-permute-start.12 = (bf16[256,7168]{1,0:T(8,128)(2,1)S(1)}, bf16[256,7168]{1,0:T(8,128)(2,1)S(1)}, u32[]{:S(2)}, u32[]{:S(2)}) collective-permute-start(bf16[256,7168]{1,0:T(8,128)(2,1)S(1)} %get-tuple-element.49), channel_id=1, source_target_pairs={{0,1},{1,0},{2,3},{3,2},{4,5},{5,4},{6,7},{7,6},{8,9},{9,8},{10,11... | collective-permute-start | bytes 11010056 | tf_op jit(solution)/shard_map/ppermute | solution.py:48
  77.3 0.2 constant_dynamic-update-slice_fusion.3
  77.6 1.8 copy-done.3
  79.4 2.1 %fusion.11 = f32[512,256]{1,0:T(8,128)S(1)} fusion(bf16[512,7168]{1,0:T(8,128)(2,1)S(1)} %constant_dynamic-update-slice_fusion.3, bf16[1,7168,256]{2,1,0:T(8,128)(2,1)S(1)} %copy-done.3), kind=kOutput, calls=%fused_computation.18 | convolution fusion | flops 1879048192 | bytes 11534336 | tf_op jit(solution)/shard_map/dot_general | solution.py:25
  81.4 1.7 copy-done.4
  83.1 1.0 copy-done.1
  84.0 2.9 %multiply_convert_fusion.2 = (bf16[512,256]{1,0:T(8,128)(2,1)S(1)}, f32[512,256]{1,0:T(8,128)}) fusion(f32[512,256]{1,0:T(8,128)S(1)} %fusion.11, bf16[512,7168]{1,0:T(8,128)(2,1)S(1)} %constant_dynamic-update-slice_fusion.3, bf16[1,7168,256]{2,1,0:T(8,128)(2,1)S(1)} %copy-done.1), kind=kOutput, calls=%fused_computation.47 | convolution fusion | flops 1879834624 | bytes 12320768 | tf_op jit(solution)/shard_map/dot_general | solution.py:26
  86.9 2.1 %convolution_convert_fusion = bf16[512,7168]{1,0:T(8,128)(2,1)S(1)} fusion(bf16[512,256]{1,0:T(8,128)(2,1)S(1)} %get-tuple-element.12, bf16[1,256,7168]{2,1,0:T(8,128)(2,1)S(1)} %copy-done.2), kind=kOutput, calls=%fused_computation.1 | convolution fusion | flops 1882718208 | bytes 11272192 | tf_op jit(solution)/shard_map/dot_general | solution.py:29
  89.0 2.1 %slice.89 = bf16[256,7168]{1,0:T(8,128)(2,1)} slice(bf16[512,7168]{1,0:T(8,128)(2,1)S(1)} %convolution_convert_fusion), slice={[256:512], [0:7168]} | slice | bytes 7340032 | tf_op jit(solution)/shard_map/slice | solution.py:55
  91.1 0.2 constant_dynamic-update-slice_fusion.10
  91.3 0.8 copy-done.6
  92.1 0.2 copy-done.7
  92.3 2.2 %multiply_convert_fusion = (bf16[512,256]{1,0:T(8,128)(2,1)S(1)}, bf16[512,256]{1,0:T(8,128)(2,1)S(1)}) fusion(f32[512,256]{1,0:T(8,128)S(1)} %copy-done.6, f32[512,256]{1,0:T(8,128)S(1)} %copy-done.7, bf16[512,7168]{1,0:T(8,128)(2,1)S(1)} %constant_dynamic-update-slice_fusion.10, bf16[1,256,7168]{2,1,0:T(8,128)(2,1)S(1)} %copy-done.2), kind=kOutput, calls=%fused_computation.44 | convolution fusion | flops 1880752128 | bytes 12582912 | tf_op jit(solution)/shard_map/dot_general | solution.py:13
  94.5 0.8 copy-done
  95.3 7.3 %fusion.9 = f32[512,7168]{1,0:T(8,128)} fusion(bf16[512,256]{1,0:T(8,128)(2,1)S(1)} %get-tuple-element.42, bf16[1,7168,256]{2,1,0:T(8,128)(2,1)S(1)} %copy-done.3), kind=kOutput, calls=%fused_computation.16 | convolution fusion | flops 1879048192 | bytes 18612224 | tf_op jit(solution)/shard_map/dot_general | solution.py:13
  102.6 11.6 %add_convert_fusion = bf16[512,7168]{1,0:T(8,128)(2,1)} fusion(f32[512,7168]{1,0:T(8,128)} %fusion.9, bf16[512,256]{1,0:T(8,128)(2,1)S(1)} %get-tuple-element.41, bf16[1,7168,256]{2,1,0:T(8,128)(2,1)} %param.10), kind=kOutput, calls=%fused_computation | convolution fusion | flops 1886388224 | bytes 25952256 | tf_op jit(solution)/shard_map/dot_general | solution.py:13
  114.2 4.3 %slice.125 = bf16[256,7168]{1,0:T(8,128)(2,1)} slice(bf16[512,7168]{1,0:T(8,128)(2,1)} %add_convert_fusion), slice={[256:512], [0:7168]} | slice | bytes 7340032 | tf_op jit(solution)/shard_map/slice | solution.py:55
  118.5 0.5 collective-permute-start.13
  119.0 7.3 %fusion.1 = bf16[1,7168,256]{2,1,0:T(8,128)(2,1)} fusion(bf16[512,7168]{1,0:T(8,128)(2,1)} %copy-done.4, bf16[512,256]{1,0:T(8,128)(2,1)S(1)} %get-tuple-element.41), kind=kOutput, calls=%fused_computation.6 | convolution fusion | flops 1880883200 | bytes 11272192 | tf_op jit(solution)/shard_map/dot_general | solution.py:19
  126.3 4.0 %fusion = bf16[1,7168,256]{2,1,0:T(8,128)(2,1)} fusion(bf16[512,7168]{1,0:T(8,128)(2,1)S(1)} %bitcast.50, bf16[512,256]{1,0:T(8,128)(2,1)S(1)} %get-tuple-element.42), kind=kOutput, calls=%fused_computation.5 | convolution fusion | flops 1880883200 | bytes 11272192 | tf_op jit(solution)/shard_map/dot_general | solution.py:19
  130.3 4.0 %fusion.2 = bf16[1,256,7168]{2,1,0:T(8,128)(2,1)} fusion(bf16[512,256]{1,0:T(8,128)(2,1)S(1)} %get-tuple-element.12, bf16[512,7168]{1,0:T(8,128)(2,1)S(1)} %bitcast.46), kind=kOutput, calls=%fused_computation.7 | convolution fusion | flops 1880883200 | bytes 11272192 | tf_op jit(solution)/shard_map/dot_general | solution.py:19
  134.3 6.6 %fusion.24 = (bf16[256,7168]{1,0:T(8,128)(2,1)S(1)}, f32[256,7168]{1,0:T(8,128)}) fusion(bf16[256,7168]{1,0:T(8,128)(2,1)} %collective-permute-done.5, bf16[512,7168]{1,0:T(8,128)(2,1)S(1)} %convolution_convert_fusion), kind=kLoop, calls=%fused_computation.71 | loop fusion | flops 7340032 | bytes 18350080 | tf_op jit(solution)/shard_map/convert.11
  141.0 0.1 collective-permute-start.6
  141.0 1.5 collective-permute-start.8
  142.5 3.5 %fusion.25 = (bf16[256,7168]{1,0:T(8,128)(2,1)S(1)}, f32[256,7168]{1,0:T(8,128)S(1)}) fusion(bf16[256,7168]{1,0:T(8,128)(2,1)} %collective-permute-done.13, bf16[512,7168]{1,0:T(8,128)(2,1)S(1)} %bitcast.44), kind=kLoop, calls=%fused_computation.72 | loop fusion | flops 7340032 | bytes 18350080 | tf_op jit(solution)/shard_map/convert.9
  146.1 1.4 collective-permute-start.14
  147.5 0.2 collective-permute-start.16
  147.6 5.6 %collective-permute-done.6 = bf16[32,7168]{1,0:T(8,128)(2,1)} collective-permute-done((bf16[32,7168]{1,0:T(8,128)(2,1)S(1)}, bf16[32,7168]{1,0:T(8,128)(2,1)}, u32[]{:S(2)}, u32[]{:S(2)}) %collective-permute-start.6) | collective-permute-done | bytes 458784 | tf_op jit(solution)/shard_map/ppermute | solution.py:44
  153.3 1.2 collective-permute-done.8
  154.5 3.2 %fusion.20 = (bf16[64,7168]{1,0:T(8,128)(2,1)S(1)}, bf16[64,7168]{1,0:T(8,128)(2,1)S(1)}, f32[64,7168]{1,0:T(8,128)S(1)}) fusion(f32[256,7168]{1,0:T(8,128)} %get-tuple-element.20, bf16[32,7168]{1,0:T(8,128)(2,1)} %collective-permute-done.6, bf16[32,7168]{1,0:T(8,128)(2,1)} %collective-permute-done.8), kind=kLoop, calls=%fused_computation.33 | loop fusion | flops 2752512 | bytes 10092544 | tf_op jit(solution)/shard_map/convert_element_type | solution.py:61
  157.6 0.2 collective-permute-start.7
  157.8 1.3 collective-permute-start.9
  159.2 3.8 %collective-permute-done.14 = bf16[32,7168]{1,0:T(8,128)(2,1)S(1)} collective-permute-done((bf16[32,7168]{1,0:T(8,128)(2,1)S(1)}, bf16[32,7168]{1,0:T(8,128)(2,1)S(1)}, u32[]{:S(2)}, u32[]{:S(2)}) %collective-permute-start.14) | collective-permute-done | bytes 458784 | tf_op jit(solution)/shard_map/ppermute | solution.py:44
  163.0 1.2 collective-permute-done.16
  164.2 0.4 fusion.16
  164.6 0.2 collective-permute-start.15
  164.8 1.3 collective-permute-start.17
  166.1 16.5 %collective-permute-done.7 = bf16[64,7168]{1,0:T(8,128)(2,1)S(1)} collective-permute-done((bf16[64,7168]{1,0:T(8,128)(2,1)S(1)}, bf16[64,7168]{1,0:T(8,128)(2,1)S(1)}, u32[]{:S(2)}, u32[]{:S(2)}) %collective-permute-start.7) | collective-permute-done | bytes 917536 | tf_op jit(solution)/shard_map/ppermute | solution.py:44
  182.6 1.2 collective-permute-done.9
  183.8 1.2 fusion.21
  185.0 17.3 %collective-permute-done.15 = bf16[64,7168]{1,0:T(8,128)(2,1)S(1)} collective-permute-done((bf16[64,7168]{1,0:T(8,128)(2,1)S(1)}, bf16[64,7168]{1,0:T(8,128)(2,1)S(1)}, u32[]{:S(2)}, u32[]{:S(2)}) %collective-permute-start.15) | collective-permute-done | bytes 917536 | tf_op jit(solution)/shard_map/ppermute | solution.py:44
  202.3 1.2 collective-permute-done.17
  203.5 1.3 fusion.22
  (41 shorter events, 0.4 us)
Async XLA Ops:
  4.8 22.7 %collective-permute-start.1 = (bf16[64,7168]{1,0:T(8,128)(2,1)S(1)}, bf16[64,7168]{1,0:T(8,128)(2,1)S(1)}, u32[]{:S(2)}, u32[]{:S(2)}) collective-permute-start(bf16[64,7168]{1,0:T(8,128)(2,1)S(1)} %get-tuple-element.54), channel_id=1, source_target_pairs={{0,6},{2,0},{4,2},{6,4},{1,7},{3,1},{5,3},{7,5},{8,14},{10,8},{12,... | collective-permute-start | bytes 2752520 | tf_op jit(solution)/shard_map/ppermute | solution.py:44
  8.4 22.2 %collective-permute-start = (bf16[64,7168]{1,0:T(8,128)(2,1)S(1)}, bf16[64,7168]{1,0:T(8,128)(2,1)S(1)}, u32[]{:S(2)}, u32[]{:S(2)}) collective-permute-start(bf16[64,7168]{1,0:T(8,128)(2,1)S(1)} %get-tuple-element.54), channel_id=1, source_target_pairs={{0,2},{2,4},{4,6},{6,0},{1,3},{3,5},{5,7},{7,1},{8,10},{10,12},{12... | collective-permute-start | bytes 2752520 | tf_op jit(solution)/shard_map/ppermute | solution.py:44
  31.0 31.7 %collective-permute-start.3 = (bf16[96,7168]{1,0:T(8,128)(2,1)S(1)}, bf16[96,7168]{1,0:T(8,128)(2,1)S(1)}, u32[]{:S(2)}, u32[]{:S(2)}) collective-permute-start(bf16[96,7168]{1,0:T(8,128)(2,1)S(1)} %get-tuple-element.47), channel_id=1, source_target_pairs={{0,6},{2,0},{4,2},{6,4},{1,7},{3,1},{5,3},{7,5},{8,14},{10,8},{12,... | collective-permute-start | bytes 4128776 | tf_op jit(solution)/shard_map/ppermute | solution.py:44
  31.4 31.1 %collective-permute-start.2 = (bf16[96,7168]{1,0:T(8,128)(2,1)S(1)}, bf16[96,7168]{1,0:T(8,128)(2,1)S(1)}, u32[]{:S(2)}, u32[]{:S(2)}) collective-permute-start(bf16[96,7168]{1,0:T(8,128)(2,1)S(1)} %get-tuple-element.48), channel_id=1, source_target_pairs={{0,2},{2,4},{4,6},{6,0},{1,3},{3,5},{5,7},{7,1},{8,10},{10,12},{12... | collective-permute-start | bytes 4128776 | tf_op jit(solution)/shard_map/ppermute | solution.py:44
  62.7 10.9 %collective-permute-start.11 = (bf16[32,7168]{1,0:T(8,128)(2,1)S(1)}, bf16[32,7168]{1,0:T(8,128)(2,1)S(1)}, u32[]{:S(2)}, u32[]{:S(2)}) collective-permute-start(bf16[32,7168]{1,0:T(8,128)(2,1)S(1)} %get-tuple-element.35), channel_id=1, source_target_pairs={{0,6},{2,0},{4,2},{6,4},{1,7},{3,1},{5,3},{7,5},{8,14},{10,8},{12,... | collective-permute-start | bytes 1376264 | tf_op jit(solution)/shard_map/ppermute | solution.py:44
  62.9 10.6 %collective-permute-start.10 = (bf16[32,7168]{1,0:T(8,128)(2,1)S(1)}, bf16[32,7168]{1,0:T(8,128)(2,1)S(1)}, u32[]{:S(2)}, u32[]{:S(2)}) collective-permute-start(bf16[32,7168]{1,0:T(8,128)(2,1)S(1)} %get-tuple-element.38), channel_id=1, source_target_pairs={{0,2},{2,4},{4,6},{6,0},{1,3},{3,5},{5,7},{7,1},{8,10},{10,12},{12... | collective-permute-start | bytes 1376264 | tf_op jit(solution)/shard_map/ppermute | solution.py:44
  64.3 13.0 %collective-permute-start.4 = (bf16[256,7168]{1,0:T(8,128)(2,1)S(1)}, bf16[256,7168]{1,0:T(8,128)(2,1)S(1)}, u32[]{:S(2)}, u32[]{:S(2)}) collective-permute-start(bf16[256,7168]{1,0:T(8,128)(2,1)S(1)} %get-tuple-element.37), channel_id=1, source_target_pairs={{0,1},{1,0},{2,3},{3,2},{4,5},{5,4},{6,7},{7,6},{8,9},{9,8},{10,11... | collective-permute-start | bytes 11010056 | tf_op jit(solution)/shard_map/ppermute | solution.py:48
  73.7 17.4 %collective-permute-start.12 = (bf16[256,7168]{1,0:T(8,128)(2,1)S(1)}, bf16[256,7168]{1,0:T(8,128)(2,1)S(1)}, u32[]{:S(2)}, u32[]{:S(2)}) collective-permute-start(bf16[256,7168]{1,0:T(8,128)(2,1)S(1)} %get-tuple-element.49), channel_id=1, source_target_pairs={{0,1},{1,0},{2,3},{3,2},{4,5},{5,4},{6,7},{7,6},{8,9},{9,8},{10,11... | collective-permute-start | bytes 11010056 | tf_op jit(solution)/shard_map/ppermute | solution.py:48
  77.3 2.0 copy-start.3
  79.4 3.7 %copy-start.4 = (bf16[512,7168]{1,0:T(8,128)(2,1)}, bf16[512,7168]{1,0:T(8,128)(2,1)S(1)}, u32[]{:S(2)}) copy-start(bf16[512,7168]{1,0:T(8,128)(2,1)S(1)} %constant_dynamic-update-slice_fusion.3) | copy-start | bytes 22020100
  79.4 4.7 %copy-start.1 = (bf16[1,7168,256]{2,1,0:T(8,128)(2,1)S(1)}, bf16[1,7168,256]{2,1,0:T(8,128)(2,1)}, u32[]{:S(2)}) copy-start(bf16[1,7168,256]{2,1,0:T(8,128)(2,1)} %param.10) | copy-start | bytes 11010052
  84.0 2.9 %copy-start.5 = (f32[512,256]{1,0:T(8,128)}, f32[512,256]{1,0:T(8,128)S(1)}, u32[]{:S(2)}) copy-start(f32[512,256]{1,0:T(8,128)S(1)} %fusion.11) | copy-start | bytes 1572868
  84.0 2.9 %copy-start.2 = (bf16[1,256,7168]{2,1,0:T(8,128)(2,1)S(1)}, bf16[1,256,7168]{2,1,0:T(8,128)(2,1)}, u32[]{:S(2)}) copy-start(bf16[1,256,7168]{2,1,0:T(8,128)(2,1)} %param.11) | copy-start | bytes 11010052
  91.1 43.2 %collective-permute-start.5 = (bf16[256,7168]{1,0:T(8,128)(2,1)}, bf16[256,7168]{1,0:T(8,128)(2,1)}, u32[]{:S(2)}, u32[]{:S(2)}) collective-permute-start(bf16[256,7168]{1,0:T(8,128)(2,1)} %slice.89), channel_id=1, source_target_pairs={{0,1},{1,0},{2,3},{3,2},{4,5},{5,4},{6,7},{7,6},{8,9},{9,8},{10,11... | collective-permute-start | bytes 11010056 | tf_op jit(solution)/shard_map/ppermute | solution.py:48
  91.1 1.0 copy-start.6
  91.1 1.2 copy-start.7
  92.3 3.0 %copy-start = (bf16[512,7168]{1,0:T(8,128)(2,1)}, bf16[512,7168]{1,0:T(8,128)(2,1)S(1)}, u32[]{:S(2)}) copy-start(bf16[512,7168]{1,0:T(8,128)(2,1)S(1)} %constant_dynamic-update-slice_fusion.10) | copy-start | bytes 22020100
  114.2 12.1 %slice-start.4 = ((s8[7340032]{0:T(1024)(128)(4,1)}), s8[4194304]{0:T(1024)(128)(4,1)S(1)}, s32[]{:S(2)}) async-start(s8[7340032]{0:T(1024)(128)(4,1)} %bitcast.49), calls=%async_computation.4 | async-start | bytes 8388608
  118.5 7.8 %slice-start.5 = ((s8[7340032]{0:T(1024)(128)(4,1)}), s8[3145728]{0:T(1024)(128)(4,1)S(1)}, s32[]{:S(2)}) async-start(s8[7340032]{0:T(1024)(128)(4,1)} %bitcast.49), calls=%async_computation.5 | async-start | bytes 6291456
  118.5 24.0 %collective-permute-start.13 = (bf16[256,7168]{1,0:T(8,128)(2,1)}, bf16[256,7168]{1,0:T(8,128)(2,1)}, u32[]{:S(2)}, u32[]{:S(2)}) collective-permute-start(bf16[256,7168]{1,0:T(8,128)(2,1)} %slice.125), channel_id=1, source_target_pairs={{0,1},{1,0},{2,3},{3,2},{4,5},{5,4},{6,7},{7,6},{8,9},{9,8},{10,11... | collective-permute-start | bytes 11010056 | tf_op jit(solution)/shard_map/ppermute | solution.py:48
  119.0 11.3 %slice-start.2 = ((s8[7340032]{0:T(1024)(128)(4,1)}), s8[4194304]{0:T(1024)(128)(4,1)S(1)}, s32[]{:S(2)}) async-start(s8[7340032]{0:T(1024)(128)(4,1)} %bitcast.45), calls=%async_computation.2 | async-start | bytes 8388608
  126.3 4.0 %slice-start.3 = ((s8[7340032]{0:T(1024)(128)(4,1)}), s8[3145728]{0:T(1024)(128)(4,1)S(1)}, s32[]{:S(2)}) async-start(s8[7340032]{0:T(1024)(128)(4,1)} %bitcast.45), calls=%async_computation.3 | async-start | bytes 6291456
  130.3 12.2 %slice-start = ((s8[7340032]{0:T(1024)(128)(4,1)}), s8[4194304]{0:T(1024)(128)(4,1)S(1)}, s32[]{:S(2)}) async-start(s8[7340032]{0:T(1024)(128)(4,1)} %bitcast.43), calls=%async_computation | async-start | bytes 8388608
  134.3 8.2 %slice-start.1 = ((s8[7340032]{0:T(1024)(128)(4,1)}), s8[3145728]{0:T(1024)(128)(4,1)S(1)}, s32[]{:S(2)}) async-start(s8[7340032]{0:T(1024)(128)(4,1)} %bitcast.43), calls=%async_computation.1 | async-start | bytes 6291456
  141.0 12.3 %collective-permute-start.6 = (bf16[32,7168]{1,0:T(8,128)(2,1)S(1)}, bf16[32,7168]{1,0:T(8,128)(2,1)}, u32[]{:S(2)}, u32[]{:S(2)}) collective-permute-start(bf16[32,7168]{1,0:T(8,128)(2,1)S(1)} %get-tuple-element.29), channel_id=1, source_target_pairs={{0,6},{2,0},{4,2},{6,4},{1,7},{3,1},{5,3},{7,5},{8,14},{10,8},{12,... | collective-permute-start | bytes 1376264 | tf_op jit(solution)/shard_map/ppermute | solution.py:44
  141.0 13.4 %collective-permute-start.8 = (bf16[32,7168]{1,0:T(8,128)(2,1)S(1)}, bf16[32,7168]{1,0:T(8,128)(2,1)}, u32[]{:S(2)}, u32[]{:S(2)}) collective-permute-start(bf16[32,7168]{1,0:T(8,128)(2,1)S(1)} %get-tuple-element.30), channel_id=1, source_target_pairs={{0,2},{2,4},{4,6},{6,0},{1,3},{3,5},{5,7},{7,1},{8,10},{10,12},{12... | collective-permute-start | bytes 1376264 | tf_op jit(solution)/shard_map/ppermute | solution.py:44
  146.1 16.9 %collective-permute-start.14 = (bf16[32,7168]{1,0:T(8,128)(2,1)S(1)}, bf16[32,7168]{1,0:T(8,128)(2,1)S(1)}, u32[]{:S(2)}, u32[]{:S(2)}) collective-permute-start(bf16[32,7168]{1,0:T(8,128)(2,1)S(1)} %get-tuple-element.27), channel_id=1, source_target_pairs={{0,6},{2,0},{4,2},{6,4},{1,7},{3,1},{5,3},{7,5},{8,14},{10,8},{12,... | collective-permute-start | bytes 1376264 | tf_op jit(solution)/shard_map/ppermute | solution.py:44
  147.5 16.7 %collective-permute-start.16 = (bf16[32,7168]{1,0:T(8,128)(2,1)S(1)}, bf16[32,7168]{1,0:T(8,128)(2,1)S(1)}, u32[]{:S(2)}, u32[]{:S(2)}) collective-permute-start(bf16[32,7168]{1,0:T(8,128)(2,1)S(1)} %get-tuple-element.28), channel_id=1, source_target_pairs={{0,2},{2,4},{4,6},{6,0},{1,3},{3,5},{5,7},{7,1},{8,10},{10,12},{12... | collective-permute-start | bytes 1376264 | tf_op jit(solution)/shard_map/ppermute | solution.py:44
  157.6 25.0 %collective-permute-start.7 = (bf16[64,7168]{1,0:T(8,128)(2,1)S(1)}, bf16[64,7168]{1,0:T(8,128)(2,1)S(1)}, u32[]{:S(2)}, u32[]{:S(2)}) collective-permute-start(bf16[64,7168]{1,0:T(8,128)(2,1)S(1)} %get-tuple-element.24), channel_id=1, source_target_pairs={{0,6},{2,0},{4,2},{6,4},{1,7},{3,1},{5,3},{7,5},{8,14},{10,8},{12,... | collective-permute-start | bytes 2752520 | tf_op jit(solution)/shard_map/ppermute | solution.py:44
  157.8 26.0 %collective-permute-start.9 = (bf16[64,7168]{1,0:T(8,128)(2,1)S(1)}, bf16[64,7168]{1,0:T(8,128)(2,1)S(1)}, u32[]{:S(2)}, u32[]{:S(2)}) collective-permute-start(bf16[64,7168]{1,0:T(8,128)(2,1)S(1)} %get-tuple-element.25), channel_id=1, source_target_pairs={{0,2},{2,4},{4,6},{6,0},{1,3},{3,5},{5,7},{7,1},{8,10},{10,12},{12... | collective-permute-start | bytes 2752520 | tf_op jit(solution)/shard_map/ppermute | solution.py:44
  164.6 37.7 %collective-permute-start.15 = (bf16[64,7168]{1,0:T(8,128)(2,1)S(1)}, bf16[64,7168]{1,0:T(8,128)(2,1)S(1)}, u32[]{:S(2)}, u32[]{:S(2)}) collective-permute-start(bf16[64,7168]{1,0:T(8,128)(2,1)S(1)} %get-tuple-element.21), channel_id=1, source_target_pairs={{0,6},{2,0},{4,2},{6,4},{1,7},{3,1},{5,3},{7,5},{8,14},{10,8},{12,... | collective-permute-start | bytes 2752520 | tf_op jit(solution)/shard_map/ppermute | solution.py:44
  164.8 38.7 %collective-permute-start.17 = (bf16[64,7168]{1,0:T(8,128)(2,1)S(1)}, bf16[64,7168]{1,0:T(8,128)(2,1)S(1)}, u32[]{:S(2)}, u32[]{:S(2)}) collective-permute-start(bf16[64,7168]{1,0:T(8,128)(2,1)S(1)} %get-tuple-element.22), channel_id=1, source_target_pairs={{0,2},{2,4},{4,6},{6,0},{1,3},{3,5},{5,7},{7,1},{8,10},{10,12},{12... | collective-permute-start | bytes 2752520 | tf_op jit(solution)/shard_map/ppermute | solution.py:44

commit v3 on v2

--- a/solution.py
+++ b/solution.py
@@ -32,7 +32,13 @@
     hidden_grad = contract_last(cot_rows, down_w)
     gate_act = (hidden_grad * up * silu_slope(gate)).astype(jnp.bfloat16)
     up_act = (hidden_grad * active).astype(jnp.bfloat16)
-    in_part = contract_last(gate_act, gate_w) + contract_last(up_act, up_w)
+    half = rows.shape[0] // 2
+    in_part = tuple(
+        (
+            contract_last(gate_act[pick], gate_w) + contract_last(up_act[pick], up_w)
+        ).astype(jnp.bfloat16)
+        for pick in (slice(half, None), slice(None, half))
+    )
     gate_term = contract_first(rows, gate_act)
     up_term = contract_first(rows, up_act)
     down_term = contract_first(hidden, cot_rows)
@@ -48,12 +54,15 @@
     return lax.ppermute(value, "core", [(0, 1), (1, 0)])
 
 
-def scatter_rows(parts):
-    half = parts.shape[0] // 2
-    slots = half // 4
+def scatter_rows(other, mine):
+    slots = mine.shape[0] // 4
     cut = slots // 2
-    acc = parts[:half].astype(jnp.float32) + core_swap(parts[half:]).astype(jnp.float32)
-    own, prev, nxt, far = (acc[k * slots:(k + 1) * slots] for k in range(4))
+    got = core_swap(other)
+    own, prev, nxt, far = (
+        mine[k * slots:(k + 1) * slots].astype(jnp.float32)
+        + got[k * slots:(k + 1) * slots].astype(jnp.float32)
+        for k in range(4)
+    )
     back_prev = y_shift(far[:cut].astype(jnp.bfloat16), -1)
     back_next = y_shift(far[cut:].astype(jnp.bfloat16), 1)
     prev = prev + jnp.pad(back_prev.astype(jnp.float32), ((0, slots - cut), (0, 0)))
@@ -97,8 +106,9 @@
     out_part, in_part, gate_term, up_term, down_term = expert_work(
         all_rows, all_cot, gate_w, up_w, down_w
     )
-    outputs = scatter_rows(out_part)[:slots]
-    input_grads = scatter_rows(in_part.astype(jnp.bfloat16))[:slots]
+    half = out_part.shape[0] // 2
+    outputs = scatter_rows(out_part[half:], out_part[:half])[:slots]
+    input_grads = scatter_rows(*in_part)[:slots]
     gate_grad = gate_term.astype(jnp.bfloat16)
     up_grad = up_term.astype(jnp.bfloat16)
     down_grad = down_term.astype(jnp.bfloat16)

time: 205 us -> 199 us (0.971)
  other arithmetic: 19.9 us -> 14.4 us
  waiting for transfers between devices: 105 us -> 99.6 us
  local copies, waits for them, and re-layouts: 14.4 us -> 17.4 us
  matrix products: 43.3 us -> 45.7 us
    dot_general x3 -> x5, matrix products: 21.1 us -> 11.5 us  [contract_last(): lax.dot_general(left, right, (((1,), (1,)), ((), ())), preferred_element_...]
    another operation x2, other arithmetic: 10.1 us -> 2.78 us
    ppermute x14, waiting for transfers between devices: 105 us -> 99.6 us  [y_shift(): lax.ppermute(value, 'y', [(i, (i + distance) % size) for i in range(size)])]
    dot_general x3, matrix products: 15.3 us -> 19.6 us  [contract_first(): lax.dot_general(left, right, (((0,), (0,)), ((), ())), preferred_element_...]
    dot_general x1, matrix products: 2.05 us -> 5.29 us  [expert_work(): gate = jnp.dot(rows, gate_w, preferred_element_type=jnp.float32)]
    dot_general x1, matrix products: 2.85 us -> 5.14 us  [expert_work(): up = jnp.dot(rows, up_w, preferred_element_type=jnp.float32)]
    slice x2 -> x7, local copies, waits for them, and re-layouts: 6.38 us -> 4.75 us  [the longest x2 2.48 us: scatter_rows(): got[k * slots:(k + 1) * slots].astype(jnp.float32)]
    unnamed x34 -> x20, local copies, waits for them, and re-layouts: 7.13 us -> 7.46 us
  transfers between devices with their start and end apart: 18 -> 18, of which waited for: 12 -> 12; matrix products, arithmetic and copies ran while one was open for 32% -> 35% of each run, Pallas kernels for 0% -> 0%
where the time goes in v3:
time: 199 us
  waiting for transfers between devices  99.6 us (50%)
  matrix products  45.7 us (23%)
  starting transfers between devices  20.2 us (10%)
  local copies, waits for them, and re-layouts  17.4 us (9%)
  other arithmetic  14.4 us (7%)
    ppermute x14, waiting for transfers between devices, y_shift(): lax.ppermute(value, 'y', [(i, (i + distance) % size) for i in range(size)])  99.6 us
    dot_general x3, matrix products, contract_first(): lax.dot_general(left, right, (((0,), (0,)), ((), ())), preferred_element_...  19.6 us
    ppermute x14, starting transfers between devices, y_shift(): lax.ppermute(value, 'y', [(i, (i + distance) % size) for i in range(size)])  12.7 us
    dot_general x5, matrix products, contract_last(): lax.dot_general(left, right, (((1,), (1,)), ((), ())), preferred_element_...  11.5 us
    ppermute x4, starting transfers between devices, core_swap(): return lax.ppermute(value, 'core', [(0, 1), (1, 0)])  7.5 us
    unnamed x20, local copies, waits for them, and re-layouts  7.46 us
    dot_general x1, matrix products, expert_work(): gate = jnp.dot(rows, gate_w, preferred_element_type=jnp.float32)  5.29 us
    dot_general x1, matrix products, expert_work(): up = jnp.dot(rows, up_w, preferred_element_type=jnp.float32)  5.14 us
  transfers between devices with their start and end apart: 18, of which 12 were waited for; matrix products, arithmetic and copies ran while one was open for 35% of the time, Pallas kernels for 0%

profile of v3, /device:TPU:1, one launch (start us, length us, event | category | flops | bytes accessed | tf_op | source)
XLA Modules:
  0.0 198.8 jit_solution(8854930053450554384)
XLA Ops:
  0.7 0.8 select_reduce_fusion
  1.5 0.6 fusion.24
  2.8 2.9 %constant_dynamic-update-slice_fusion.9 = (bf16[256,7168]{1,0:T(8,128)(2,1)}, bf16[64,7168]{1,0:T(8,128)(2,1)S(1)}, bf16[256,7168]{1,0:T(8,128)(2,1)S(1)}, bf16[64,7168]{1,0:T(8,128)(2,1)S(1)}) fusion(bf16[60,7168]{1,0:T(8,128)(2,1)} %bitcast.47, pred[64]{0:T(512)(128)(4,1)S(1)} %iota_compare_fusion.1, bf16[60,7168]{1,0:T(8,128)(2,1)} %bitcast.48), kind=kLoop, calls=%fused_computation.63 | loop fusion | flops 917502 | bytes 5390400
  5.7 3.6 %collective-permute-start.1 = (bf16[64,7168]{1,0:T(8,128)(2,1)S(1)}, bf16[64,7168]{1,0:T(8,128)(2,1)S(1)}, u32[]{:S(2)}, u32[]{:S(2)}) collective-permute-start(bf16[64,7168]{1,0:T(8,128)(2,1)S(1)} %get-tuple-element.48), channel_id=1, source_target_pairs={{0,6},{2,0},{4,2},{6,4},{1,7},{3,1},{5,3},{7,5},{8,14},{10,8},{12,... | collective-permute-start | bytes 2752520 | tf_op jit(solution)/shard_map/ppermute | solution.py:50
  9.2 1.0 constant_dynamic-update-slice_fusion.6
  10.3 18.0 %collective-permute-done.1 = bf16[64,7168]{1,0:T(8,128)(2,1)S(1)} collective-permute-done((bf16[64,7168]{1,0:T(8,128)(2,1)S(1)}, bf16[64,7168]{1,0:T(8,128)(2,1)S(1)}, u32[]{:S(2)}, u32[]{:S(2)}) %collective-permute-start.1) | collective-permute-done | bytes 917536 | tf_op jit(solution)/shard_map/ppermute | solution.py:50
  28.3 3.1 %collective-permute-done = bf16[64,7168]{1,0:T(8,128)(2,1)S(1)} collective-permute-done((bf16[64,7168]{1,0:T(8,128)(2,1)S(1)}, bf16[64,7168]{1,0:T(8,128)(2,1)S(1)}, u32[]{:S(2)}, u32[]{:S(2)}) %collective-permute-start) | collective-permute-done | bytes 917536 | tf_op jit(solution)/shard_map/ppermute | solution.py:50
  31.4 0.3 pad_maximum_fusion
  31.7 0.4 collective-permute-start.3
  32.1 1.1 collective-permute-start.2
  33.3 1.1 constant_dynamic-update-slice_fusion.1
  34.4 1.1 constant_dynamic-update-slice_fusion
  35.5 27.8 %collective-permute-done.2 = bf16[96,7168]{1,0:T(8,128)(2,1)S(1)} collective-permute-done((bf16[96,7168]{1,0:T(8,128)(2,1)S(1)}, bf16[96,7168]{1,0:T(8,128)(2,1)S(1)}, u32[]{:S(2)}, u32[]{:S(2)}) %collective-permute-start.2) | collective-permute-done | bytes 1376288 | tf_op jit(solution)/shard_map/ppermute | solution.py:50
  63.3 0.9 fusion.26
  64.2 0.9 fusion.25
  65.1 1.5 collective-permute-start.10
  66.5 3.2 %collective-permute-start.4 = (bf16[256,7168]{1,0:T(8,128)(2,1)S(1)}, bf16[256,7168]{1,0:T(8,128)(2,1)S(1)}, u32[]{:S(2)}, u32[]{:S(2)}) collective-permute-start(bf16[256,7168]{1,0:T(8,128)(2,1)S(1)} %get-tuple-element.27), channel_id=1, source_target_pairs={{0,1},{1,0},{2,3},{3,2},{4,5},{5,4},{6,7},{7,6},{8,9},{9,8},{10,11... | collective-permute-start | bytes 11010056 | tf_op jit(solution)/shard_map/ppermute | solution.py:54
  69.8 1.1 slice_dynamic-update-slice_fusion.3
  70.8 1.1 slice_dynamic-update-slice_fusion.1
  71.9 3.8 %collective-permute-done.10 = bf16[32,7168]{1,0:T(8,128)(2,1)S(1)} collective-permute-done((bf16[32,7168]{1,0:T(8,128)(2,1)S(1)}, bf16[32,7168]{1,0:T(8,128)(2,1)S(1)}, u32[]{:S(2)}, u32[]{:S(2)}) %collective-permute-start.10) | collective-permute-done | bytes 458784 | tf_op jit(solution)/shard_map/ppermute | solution.py:50
  75.7 0.8 constant_dynamic-update-slice_fusion.8
  76.5 0.8 constant_dynamic-update-slice_fusion.7
  77.4 3.5 %collective-permute-start.12 = (bf16[256,7168]{1,0:T(8,128)(2,1)}, bf16[256,7168]{1,0:T(8,128)(2,1)S(1)}, u32[]{:S(2)}, u32[]{:S(2)}) collective-permute-start(bf16[256,7168]{1,0:T(8,128)(2,1)} %get-tuple-element.43), channel_id=1, source_target_pairs={{0,1},{1,0},{2,3},{3,2},{4,5},{5,4},{6,7},{7,6},{8,9},{9,8},{10,11... | collective-permute-start | bytes 11010056 | tf_op jit(solution)/shard_map/ppermute | solution.py:54
  80.9 2.1 %constant_dynamic-update-slice_fusion.3 = bf16[512,7168]{1,0:T(8,128)(2,1)} fusion(bf16[512,7168]{1,0:T(8,128)(2,1)} %get-tuple-element.26, bf16[256,7168]{1,0:T(8,128)(2,1)S(1)} %collective-permute-done.4), kind=kLoop, calls=%fused_computation.57 | loop fusion | bytes 7340032 | tf_op jit(solution)/shard_map/concatenate | solution.py:102
  83.0 1.3 copy-done.3
  84.2 5.3 %fusion.16 = f32[512,256]{1,0:T(8,128)S(1)} fusion(bf16[512,7168]{1,0:T(8,128)(2,1)} %constant_dynamic-update-slice_fusion.3, bf16[1,7168,256]{2,1,0:T(8,128)(2,1)S(1)} %copy-done.3), kind=kOutput, calls=%fused_computation.22 | convolution fusion | flops 1879048192 | bytes 11534336 | tf_op jit(solution)/shard_map/dot_general | solution.py:25
  89.6 5.1 %multiply_convert_fusion.2 = (bf16[512,256]{1,0:T(8,128)(2,1)S(1)}, f32[512,256]{1,0:T(8,128)S(1)}) fusion(f32[512,256]{1,0:T(8,128)S(1)} %fusion.16, bf16[512,7168]{1,0:T(8,128)(2,1)} %constant_dynamic-update-slice_fusion.3, bf16[1,7168,256]{2,1,0:T(8,128)(2,1)S(1)} %copy-done.1), kind=kOutput, calls=%fused_computation.45 | convolution fusion | flops 1879834624 | bytes 12320768 | tf_op jit(solution)/shard_map/dot_general | solution.py:26
  94.7 4.1 %convolution_convert_fusion = bf16[512,7168]{1,0:T(8,128)(2,1)S(1)} fusion(bf16[512,256]{1,0:T(8,128)(2,1)S(1)} %get-tuple-element.12, bf16[1,256,7168]{2,1,0:T(8,128)(2,1)} %param.11), kind=kOutput, calls=%fused_computation | convolution fusion | flops 1882718208 | bytes 11272192 | tf_op jit(solution)/shard_map/dot_general | solution.py:29
  98.8 2.3 %slice.121 = bf16[256,7168]{1,0:T(8,128)(2,1)} slice(bf16[512,7168]{1,0:T(8,128)(2,1)S(1)} %convolution_convert_fusion), slice={[256:512], [0:7168]} | slice | bytes 7340032 | tf_op jit(solution)/shard_map/slice | solution.py:110
  101.1 0.2 constant_dynamic-update-slice_fusion.10
  101.4 6.9 %multiply_convert_fusion = (bf16[512,256]{1,0:T(8,128)(2,1)S(1)}, bf16[512,256]{1,0:T(8,128)(2,1)S(1)}) fusion(f32[512,256]{1,0:T(8,128)S(1)} %fusion.16, f32[512,256]{1,0:T(8,128)S(1)} %get-tuple-element.10, bf16[512,7168]{1,0:T(8,128)(2,1)S(1)} %constant_dynamic-update-slice_fusion.10, bf16[1,256,7168]{2,1,0:T(8,128)(2,1)} %param.11), kind=kOutput, calls=%fused_computation.42 | convolution fusion | flops 1880752128 | bytes 12582912 | tf_op jit(solution)/shard_map/dot_general | solution.py:13
  108.3 1.2 fusion.12
  109.4 1.2 fusion.1
  110.6 0.8 collective-permute-start.13
  111.4 1.1 fusion.14
  112.5 1.2 fusion
  113.7 8.4 %fusion.3 = bf16[1,7168,256]{2,1,0:T(8,128)(2,1)} fusion(bf16[512,7168]{1,0:T(8,128)(2,1)} %constant_dynamic-update-slice_fusion.3, bf16[512,256]{1,0:T(8,128)(2,1)S(1)} %get-tuple-element.31), kind=kOutput, calls=%fused_computation.9 | convolution fusion | flops 1880883200 | bytes 11272192 | tf_op jit(solution)/shard_map/dot_general | solution.py:19
  122.1 7.2 %fusion.2 = bf16[1,7168,256]{2,1,0:T(8,128)(2,1)} fusion(bf16[512,7168]{1,0:T(8,128)(2,1)} %constant_dynamic-update-slice_fusion.3, bf16[512,256]{1,0:T(8,128)(2,1)S(1)} %get-tuple-element.32), kind=kOutput, calls=%fused_computation.8 | convolution fusion | flops 1880883200 | bytes 11272192 | tf_op jit(solution)/shard_map/dot_general | solution.py:19
  129.3 4.0 %fusion.4 = bf16[1,256,7168]{2,1,0:T(8,128)(2,1)} fusion(bf16[512,256]{1,0:T(8,128)(2,1)S(1)} %get-tuple-element.12, bf16[512,7168]{1,0:T(8,128)(2,1)S(1)} %bitcast.46), kind=kOutput, calls=%fused_computation.10 | convolution fusion | flops 1880883200 | bytes 11272192 | tf_op jit(solution)/shard_map/dot_general | solution.py:19
  133.3 1.4 add_convert_fusion.7
  134.7 0.1 fusion.28
  134.8 0.1 collective-permute-start.6
  134.9 1.5 collective-permute-start.8
  136.3 1.2 slice.155
  137.6 1.4 add_convert_fusion.3
  139.0 1.4 collective-permute-start.14
  140.4 0.2 collective-permute-start.16
  140.6 1.2 slice.174
  141.8 5.1 %collective-permute-done.6 = bf16[32,7168]{1,0:T(8,128)(2,1)S(1)} collective-permute-done((bf16[32,7168]{1,0:T(8,128)(2,1)S(1)}, bf16[32,7168]{1,0:T(8,128)(2,1)S(1)}, u32[]{:S(2)}, u32[]{:S(2)}) %collective-permute-start.6) | collective-permute-done | bytes 458784 | tf_op jit(solution)/shard_map/ppermute | solution.py:50
  146.9 1.3 collective-permute-done.8
  148.2 2.1 %add_convert_fusion.6 = (bf16[64,7168]{1,0:T(8,128)(2,1)S(1)}, bf16[64,7168]{1,0:T(8,128)(2,1)S(1)}) fusion(bf16[256,7168]{1,0:T(8,128)(2,1)} %collective-permute-done.5, bf16[32,7168]{1,0:T(8,128)(2,1)S(1)} %collective-permute-done.6, bf16[512,7168]{1,0:T(8,128)(2,1)S(1)} %convolution_convert_fusion, bf16[32,7168]{1,0:T(8,128)(2,1)S(1)} %collective-permute-done.8), kind=kLoop, calls=%fused_computation.30 | loop fusion | flops 5505024 | bytes 6422528 | tf_op jit(solution)/shard_map/convert_element_type | solution.py:70
  150.3 0.3 collective-permute-start.7
  150.6 1.3 collective-permute-start.9
  151.9 4.9 %collective-permute-done.14 = bf16[32,7168]{1,0:T(8,128)(2,1)S(1)} collective-permute-done((bf16[32,7168]{1,0:T(8,128)(2,1)S(1)}, bf16[32,7168]{1,0:T(8,128)(2,1)S(1)}, u32[]{:S(2)}, u32[]{:S(2)}) %collective-permute-start.14) | collective-permute-done | bytes 458784 | tf_op jit(solution)/shard_map/ppermute | solution.py:50
  156.8 1.3 collective-permute-done.16
  158.1 2.1 %add_convert_fusion.2 = (bf16[64,7168]{1,0:T(8,128)(2,1)S(1)}, bf16[64,7168]{1,0:T(8,128)(2,1)S(1)}) fusion(bf16[256,7168]{1,0:T(8,128)(2,1)} %collective-permute-done.13, bf16[256,7168]{1,0:T(8,128)(2,1)S(1)} %fusion, bf16[32,7168]{1,0:T(8,128)(2,1)S(1)} %collective-permute-done.14, bf16[32,7168]{1,0:T(8,128)(2,1)S(1)} %collective-permute-done.16), kind=kLoop, calls=%fused_computation.26 | loop fusion | flops 5505024 | bytes 6422528 | tf_op jit(solution)/shard_map/convert_element_type | solution.py:70
  160.1 0.3 collective-permute-start.15
  160.4 1.3 collective-permute-start.17
  161.7 14.7 %collective-permute-done.7 = bf16[64,7168]{1,0:T(8,128)(2,1)S(1)} collective-permute-done((bf16[64,7168]{1,0:T(8,128)(2,1)S(1)}, bf16[64,7168]{1,0:T(8,128)(2,1)S(1)}, u32[]{:S(2)}, u32[]{:S(2)}) %collective-permute-start.7) | collective-permute-done | bytes 917536 | tf_op jit(solution)/shard_map/ppermute | solution.py:50
  176.4 1.3 collective-permute-done.9
  177.7 1.4 fusion.18
  179.1 17.0 %collective-permute-done.15 = bf16[64,7168]{1,0:T(8,128)(2,1)S(1)} collective-permute-done((bf16[64,7168]{1,0:T(8,128)(2,1)S(1)}, bf16[64,7168]{1,0:T(8,128)(2,1)S(1)}, u32[]{:S(2)}, u32[]{:S(2)}) %collective-permute-start.15) | collective-permute-done | bytes 917536 | tf_op jit(solution)/shard_map/ppermute | solution.py:50
  196.1 1.3 collective-permute-done.17
  197.4 1.4 fusion.19
  (32 shorter events, 0.2 us)
Async XLA Ops:
  5.7 22.6 %collective-permute-start.1 = (bf16[64,7168]{1,0:T(8,128)(2,1)S(1)}, bf16[64,7168]{1,0:T(8,128)(2,1)S(1)}, u32[]{:S(2)}, u32[]{:S(2)}) collective-permute-start(bf16[64,7168]{1,0:T(8,128)(2,1)S(1)} %get-tuple-element.48), channel_id=1, source_target_pairs={{0,6},{2,0},{4,2},{6,4},{1,7},{3,1},{5,3},{7,5},{8,14},{10,8},{12,... | collective-permute-start | bytes 2752520 | tf_op jit(solution)/shard_map/ppermute | solution.py:50
  9.2 22.2 %collective-permute-start = (bf16[64,7168]{1,0:T(8,128)(2,1)S(1)}, bf16[64,7168]{1,0:T(8,128)(2,1)S(1)}, u32[]{:S(2)}, u32[]{:S(2)}) collective-permute-start(bf16[64,7168]{1,0:T(8,128)(2,1)S(1)} %get-tuple-element.48), channel_id=1, source_target_pairs={{0,2},{2,4},{4,6},{6,0},{1,3},{3,5},{5,7},{7,1},{8,10},{10,12},{12... | collective-permute-start | bytes 2752520 | tf_op jit(solution)/shard_map/ppermute | solution.py:50
  31.7 32.5 %collective-permute-start.3 = (bf16[96,7168]{1,0:T(8,128)(2,1)S(1)}, bf16[96,7168]{1,0:T(8,128)(2,1)S(1)}, u32[]{:S(2)}, u32[]{:S(2)}) collective-permute-start(bf16[96,7168]{1,0:T(8,128)(2,1)S(1)} %get-tuple-element.41), channel_id=1, source_target_pairs={{0,6},{2,0},{4,2},{6,4},{1,7},{3,1},{5,3},{7,5},{8,14},{10,8},{12,... | collective-permute-start | bytes 4128776 | tf_op jit(solution)/shard_map/ppermute | solution.py:50
  32.1 31.1 %collective-permute-start.2 = (bf16[96,7168]{1,0:T(8,128)(2,1)S(1)}, bf16[96,7168]{1,0:T(8,128)(2,1)S(1)}, u32[]{:S(2)}, u32[]{:S(2)}) collective-permute-start(bf16[96,7168]{1,0:T(8,128)(2,1)S(1)} %get-tuple-element.42), channel_id=1, source_target_pairs={{0,2},{2,4},{4,6},{6,0},{1,3},{3,5},{5,7},{7,1},{8,10},{10,12},{12... | collective-permute-start | bytes 4128776 | tf_op jit(solution)/shard_map/ppermute | solution.py:50
  65.1 11.5 %collective-permute-start.11 = (bf16[32,7168]{1,0:T(8,128)(2,1)S(1)}, bf16[32,7168]{1,0:T(8,128)(2,1)S(1)}, u32[]{:S(2)}, u32[]{:S(2)}) collective-permute-start(bf16[32,7168]{1,0:T(8,128)(2,1)S(1)} %get-tuple-element.25), channel_id=1, source_target_pairs={{0,6},{2,0},{4,2},{6,4},{1,7},{3,1},{5,3},{7,5},{8,14},{10,8},{12,... | collective-permute-start | bytes 1376264 | tf_op jit(solution)/shard_map/ppermute | solution.py:50
  65.1 10.6 %collective-permute-start.10 = (bf16[32,7168]{1,0:T(8,128)(2,1)S(1)}, bf16[32,7168]{1,0:T(8,128)(2,1)S(1)}, u32[]{:S(2)}, u32[]{:S(2)}) collective-permute-start(bf16[32,7168]{1,0:T(8,128)(2,1)S(1)} %get-tuple-element.28), channel_id=1, source_target_pairs={{0,2},{2,4},{4,6},{6,0},{1,3},{3,5},{5,7},{7,1},{8,10},{10,12},{12... | collective-permute-start | bytes 1376264 | tf_op jit(solution)/shard_map/ppermute | solution.py:50
  66.5 14.3 %collective-permute-start.4 = (bf16[256,7168]{1,0:T(8,128)(2,1)S(1)}, bf16[256,7168]{1,0:T(8,128)(2,1)S(1)}, u32[]{:S(2)}, u32[]{:S(2)}) collective-permute-start(bf16[256,7168]{1,0:T(8,128)(2,1)S(1)} %get-tuple-element.27), channel_id=1, source_target_pairs={{0,1},{1,0},{2,3},{3,2},{4,5},{5,4},{6,7},{7,6},{8,9},{9,8},{10,11... | collective-permute-start | bytes 11010056 | tf_op jit(solution)/shard_map/ppermute | solution.py:54
  77.4 23.8 %collective-permute-start.12 = (bf16[256,7168]{1,0:T(8,128)(2,1)}, bf16[256,7168]{1,0:T(8,128)(2,1)S(1)}, u32[]{:S(2)}, u32[]{:S(2)}) collective-permute-start(bf16[256,7168]{1,0:T(8,128)(2,1)} %get-tuple-element.43), channel_id=1, source_target_pairs={{0,1},{1,0},{2,3},{3,2},{4,5},{5,4},{6,7},{7,6},{8,9},{9,8},{10,11... | collective-permute-start | bytes 11010056 | tf_op jit(solution)/shard_map/ppermute | solution.py:54
  80.9 3.4 %copy-start.3 = (bf16[1,7168,256]{2,1,0:T(8,128)(2,1)S(1)}, bf16[1,7168,256]{2,1,0:T(8,128)(2,1)}, u32[]{:S(2)}) copy-start(bf16[1,7168,256]{2,1,0:T(8,128)(2,1)} %param.9) | copy-start | bytes 11010052
  84.2 5.3 %copy-start.1 = (bf16[1,7168,256]{2,1,0:T(8,128)(2,1)S(1)}, bf16[1,7168,256]{2,1,0:T(8,128)(2,1)}, u32[]{:S(2)}) copy-start(bf16[1,7168,256]{2,1,0:T(8,128)(2,1)} %param.10) | copy-start | bytes 11010052
  98.8 49.4 %copy-start = (bf16[512,7168]{1,0:T(8,128)(2,1)}, bf16[512,7168]{1,0:T(8,128)(2,1)S(1)}, u32[]{:S(2)}) copy-start(bf16[512,7168]{1,0:T(8,128)(2,1)S(1)} %convolution_convert_fusion) | copy-start | bytes 22020100
  101.1 32.2 %collective-permute-start.5 = (bf16[256,7168]{1,0:T(8,128)(2,1)}, bf16[256,7168]{1,0:T(8,128)(2,1)}, u32[]{:S(2)}, u32[]{:S(2)}) collective-permute-start(bf16[256,7168]{1,0:T(8,128)(2,1)} %slice.121), channel_id=1, source_target_pairs={{0,1},{1,0},{2,3},{3,2},{4,5},{5,4},{6,7},{7,6},{8,9},{9,8},{10,11... | collective-permute-start | bytes 11010056 | tf_op jit(solution)/shard_map/ppermute | solution.py:54
  101.4 6.9 %copy-start.4 = (bf16[512,7168]{1,0:T(8,128)(2,1)}, bf16[512,7168]{1,0:T(8,128)(2,1)S(1)}, u32[]{:S(2)}) copy-start(bf16[512,7168]{1,0:T(8,128)(2,1)S(1)} %constant_dynamic-update-slice_fusion.10) | copy-start | bytes 22020100
  110.6 27.0 %collective-permute-start.13 = (bf16[256,7168]{1,0:T(8,128)(2,1)S(1)}, bf16[256,7168]{1,0:T(8,128)(2,1)}, u32[]{:S(2)}, u32[]{:S(2)}) collective-permute-start(bf16[256,7168]{1,0:T(8,128)(2,1)S(1)} %fusion.1), channel_id=1, source_target_pairs={{0,1},{1,0},{2,3},{3,2},{4,5},{5,4},{6,7},{7,6},{8,9},{9,8},{10,11... | collective-permute-start | bytes 11010056 | tf_op jit(solution)/shard_map/ppermute | solution.py:54
  113.7 44.4 %copy-start.2 = (bf16[256,7168]{1,0:T(8,128)(2,1)}, bf16[256,7168]{1,0:T(8,128)(2,1)S(1)}, u32[]{:S(2)}) copy-start(bf16[256,7168]{1,0:T(8,128)(2,1)S(1)} %fusion) | copy-start | bytes 11010052
  113.7 15.6 %slice-start.2 = ((s8[7340032]{0:T(1024)(128)(4,1)}), s8[4194304]{0:T(1024)(128)(4,1)S(1)}, s32[]{:S(2)}) async-start(s8[7340032]{0:T(1024)(128)(4,1)} %bitcast.45), calls=%async_computation.2 | async-start | bytes 8388608
  122.1 7.2 %slice-start.3 = ((s8[7340032]{0:T(1024)(128)(4,1)}), s8[3145728]{0:T(1024)(128)(4,1)S(1)}, s32[]{:S(2)}) async-start(s8[7340032]{0:T(1024)(128)(4,1)} %bitcast.45), calls=%async_computation.3 | async-start | bytes 6291456
  134.8 12.1 %collective-permute-start.6 = (bf16[32,7168]{1,0:T(8,128)(2,1)S(1)}, bf16[32,7168]{1,0:T(8,128)(2,1)S(1)}, u32[]{:S(2)}, u32[]{:S(2)}) collective-permute-start(bf16[32,7168]{1,0:T(8,128)(2,1)S(1)} %get-tuple-element.35), channel_id=1, source_target_pairs={{0,6},{2,0},{4,2},{6,4},{1,7},{3,1},{5,3},{7,5},{8,14},{10,8},{12,... | collective-permute-start | bytes 1376264 | tf_op jit(solution)/shard_map/ppermute | solution.py:50
  134.9 13.3 %collective-permute-start.8 = (bf16[32,7168]{1,0:T(8,128)(2,1)S(1)}, bf16[32,7168]{1,0:T(8,128)(2,1)S(1)}, u32[]{:S(2)}, u32[]{:S(2)}) collective-permute-start(bf16[32,7168]{1,0:T(8,128)(2,1)S(1)} %get-tuple-element.36), channel_id=1, source_target_pairs={{0,2},{2,4},{4,6},{6,0},{1,3},{3,5},{5,7},{7,1},{8,10},{10,12},{12... | collective-permute-start | bytes 1376264 | tf_op jit(solution)/shard_map/ppermute | solution.py:50
  139.0 17.7 %collective-permute-start.14 = (bf16[32,7168]{1,0:T(8,128)(2,1)S(1)}, bf16[32,7168]{1,0:T(8,128)(2,1)S(1)}, u32[]{:S(2)}, u32[]{:S(2)}) collective-permute-start(bf16[32,7168]{1,0:T(8,128)(2,1)S(1)} %get-tuple-element.33), channel_id=1, source_target_pairs={{0,6},{2,0},{4,2},{6,4},{1,7},{3,1},{5,3},{7,5},{8,14},{10,8},{12,... | collective-permute-start | bytes 1376264 | tf_op jit(solution)/shard_map/ppermute | solution.py:50
  140.4 17.6 %collective-permute-start.16 = (bf16[32,7168]{1,0:T(8,128)(2,1)S(1)}, bf16[32,7168]{1,0:T(8,128)(2,1)S(1)}, u32[]{:S(2)}, u32[]{:S(2)}) collective-permute-start(bf16[32,7168]{1,0:T(8,128)(2,1)S(1)} %get-tuple-element.34), channel_id=1, source_target_pairs={{0,2},{2,4},{4,6},{6,0},{1,3},{3,5},{5,7},{7,1},{8,10},{10,12},{12... | collective-permute-start | bytes 1376264 | tf_op jit(solution)/shard_map/ppermute | solution.py:50
  150.3 27.4 %slice-start = ((bf16[512,7168]{1,0:T(8,128)(2,1)}), bf16[64,7168]{1,0:T(8,128)(2,1)S(1)}, s32[]{:S(2)}) async-start(bf16[512,7168]{1,0:T(8,128)(2,1)} %copy-done), calls=%async_computation | async-start | bytes 1835008 | tf_op jit(solution)/shard_map/slice | solution.py:62
  150.3 26.1 %collective-permute-start.7 = (bf16[64,7168]{1,0:T(8,128)(2,1)S(1)}, bf16[64,7168]{1,0:T(8,128)(2,1)S(1)}, u32[]{:S(2)}, u32[]{:S(2)}) collective-permute-start(bf16[64,7168]{1,0:T(8,128)(2,1)S(1)} %get-tuple-element.17), channel_id=1, source_target_pairs={{0,6},{2,0},{4,2},{6,4},{1,7},{3,1},{5,3},{7,5},{8,14},{10,8},{12,... | collective-permute-start | bytes 2752520 | tf_op jit(solution)/shard_map/ppermute | solution.py:50
  150.6 27.1 %collective-permute-start.9 = (bf16[64,7168]{1,0:T(8,128)(2,1)S(1)}, bf16[64,7168]{1,0:T(8,128)(2,1)S(1)}, u32[]{:S(2)}, u32[]{:S(2)}) collective-permute-start(bf16[64,7168]{1,0:T(8,128)(2,1)S(1)} %get-tuple-element.18), channel_id=1, source_target_pairs={{0,2},{2,4},{4,6},{6,0},{1,3},{3,5},{5,7},{7,1},{8,10},{10,12},{12... | collective-permute-start | bytes 2752520 | tf_op jit(solution)/shard_map/ppermute | solution.py:50
  160.1 37.2 %slice-start.1 = ((bf16[256,7168]{1,0:T(8,128)(2,1)}), bf16[64,7168]{1,0:T(8,128)(2,1)S(1)}, s32[]{:S(2)}) async-start(bf16[256,7168]{1,0:T(8,128)(2,1)} %copy-done.2), calls=%async_computation.1 | async-start | bytes 1835008 | tf_op jit(solution)/shard_map/slice | solution.py:62
  160.1 35.9 %collective-permute-start.15 = (bf16[64,7168]{1,0:T(8,128)(2,1)S(1)}, bf16[64,7168]{1,0:T(8,128)(2,1)S(1)}, u32[]{:S(2)}, u32[]{:S(2)}) collective-permute-start(bf16[64,7168]{1,0:T(8,128)(2,1)S(1)} %get-tuple-element.19), channel_id=1, source_target_pairs={{0,6},{2,0},{4,2},{6,4},{1,7},{3,1},{5,3},{7,5},{8,14},{10,8},{12,... | collective-permute-start | bytes 2752520 | tf_op jit(solution)/shard_map/ppermute | solution.py:50
  160.4 37.0 %collective-permute-start.17 = (bf16[64,7168]{1,0:T(8,128)(2,1)S(1)}, bf16[64,7168]{1,0:T(8,128)(2,1)S(1)}, u32[]{:S(2)}, u32[]{:S(2)}) collective-permute-start(bf16[64,7168]{1,0:T(8,128)(2,1)S(1)} %get-tuple-element.20), channel_id=1, source_target_pairs={{0,2},{2,4},{4,6},{6,0},{1,3},{3,5},{5,7},{7,1},{8,10},{10,12},{12... | collective-permute-start | bytes 2752520 | tf_op jit(solution)/shard_map/ppermute | solution.py:50

commit v4 on v3

--- a/solution.py
+++ b/solution.py
@@ -54,22 +54,22 @@
     return lax.ppermute(value, "core", [(0, 1), (1, 0)])
 
 
-def scatter_rows(other, mine):
-    slots = mine.shape[0] // 4
-    cut = slots // 2
+def scatter_rows(other, mine, slots):
+    block = mine.shape[0] // 4
+    cut = block // 2
     got = core_swap(other)
     own, prev, nxt, far = (
-        mine[k * slots:(k + 1) * slots].astype(jnp.float32)
-        + got[k * slots:(k + 1) * slots].astype(jnp.float32)
+        mine[k * block:(k + 1) * block].astype(jnp.float32)
+        + got[k * block:(k + 1) * block].astype(jnp.float32)
         for k in range(4)
     )
     back_prev = y_shift(far[:cut].astype(jnp.bfloat16), -1)
-    back_next = y_shift(far[cut:].astype(jnp.bfloat16), 1)
-    prev = prev + jnp.pad(back_prev.astype(jnp.float32), ((0, slots - cut), (0, 0)))
-    nxt = nxt + jnp.pad(back_next.astype(jnp.float32), ((cut, 0), (0, 0)))
+    back_next = y_shift(far[cut:slots].astype(jnp.bfloat16), 1)
+    prev = prev[:slots] + jnp.pad(back_prev.astype(jnp.float32), ((0, slots - cut), (0, 0)))
+    nxt = nxt[:slots] + jnp.pad(back_next.astype(jnp.float32), ((cut, 0), (0, 0)))
     from_next = y_shift(prev.astype(jnp.bfloat16), -1)
     from_prev = y_shift(nxt.astype(jnp.bfloat16), 1)
-    total = own + from_next.astype(jnp.float32) + from_prev.astype(jnp.float32)
+    total = own[:slots] + from_next.astype(jnp.float32) + from_prev.astype(jnp.float32)
     return total.astype(jnp.bfloat16)
 
 
@@ -91,24 +91,31 @@
     grow = ((0, padded - slots), (0, 0))
     masked = jnp.where(valid, jnp.pad(rows_in, grow), 0).astype(rows_in.dtype)
     masked_cot = jnp.where(valid, jnp.pad(cot_in, grow), 0).astype(cot_in.dtype)
-    cut = masked.shape[0] // 2
-    tok_prev = y_shift(masked, 1)
-    tok_next = y_shift(masked, -1)
-    got_prev = y_shift(jnp.concatenate([tok_prev[:cut], masked_cot], axis=0), 1)
-    got_next = y_shift(jnp.concatenate([tok_next[cut:], masked_cot], axis=0), -1)
-    tok_far_a, cot_prev = got_prev[:cut], got_prev[cut:]
-    tok_far_b, cot_next = got_next[:cut], got_next[cut:]
-    tok_mine = jnp.concatenate([masked, tok_prev, tok_next, tok_far_a, tok_far_b], axis=0)
+    block = masked.shape[0]
+    cut = block // 2
+    send_tok = masked[:slots]
+    send_cot = masked_cot[:slots]
+
+    def fill(rows):
+        return jnp.pad(rows, ((0, block - rows.shape[0]), (0, 0)))
+
+    tok_prev = y_shift(send_tok, 1)
+    tok_next = y_shift(send_tok, -1)
+    got_prev = y_shift(jnp.concatenate([send_cot, tok_prev[:cut]], axis=0), 1)
+    got_next = y_shift(jnp.concatenate([send_cot, tok_next[cut:]], axis=0), -1)
+    cot_prev, cot_next = got_prev[:slots], got_next[:slots]
+    tok_far = jnp.concatenate([got_prev[slots:], got_next[slots:]], axis=0)
+    tok_mine = jnp.concatenate([masked, fill(tok_prev), fill(tok_next), fill(tok_far)], axis=0)
     all_rows = jnp.concatenate([tok_mine, core_swap(tok_mine)], axis=0)
     cot_far = jnp.concatenate([y_shift(cot_prev[:cut], 1), y_shift(cot_next[cut:], -1)], axis=0)
-    cot_mine = jnp.concatenate([masked_cot, cot_prev, cot_next, cot_far], axis=0)
+    cot_mine = jnp.concatenate([masked_cot, fill(cot_prev), fill(cot_next), fill(cot_far)], axis=0)
     all_cot = jnp.concatenate([cot_mine, core_swap(cot_mine)], axis=0)
     out_part, in_part, gate_term, up_term, down_term = expert_work(
         all_rows, all_cot, gate_w, up_w, down_w
     )
     half = out_part.shape[0] // 2
-    outputs = scatter_rows(out_part[half:], out_part[:half])[:slots]
-    input_grads = scatter_rows(*in_part)[:slots]
+    outputs = scatter_rows(out_part[half:], out_part[:half], slots)
+    input_grads = scatter_rows(*in_part, slots)
     gate_grad = gate_term.astype(jnp.bfloat16)
     up_grad = up_term.astype(jnp.bfloat16)
     down_grad = down_term.astype(jnp.bfloat16)

time: 199 us -> 199 us (level); the launches traced: 199 us -> 196 us
  matrix products: 45.7 us -> 37.8 us
  starting transfers between devices: 20.2 us -> 23.8 us
  waiting for transfers between devices: 99.6 us -> 103 us
  other arithmetic: 14.4 us -> 11.5 us
    ppermute x14, starting transfers between devices: 12.7 us -> 16.6 us  [y_shift(): lax.ppermute(value, 'y', [(i, (i + distance) % size) for i in range(size)])]
    convert_element_type x2, other arithmetic: 4.15 us -> 0.55 us  [scatter_rows(): from_next = y_shift(prev.astype(jnp.bfloat16), -1)]
    ppermute x14, waiting for transfers between devices: 99.6 us -> 103 us  [y_shift(): lax.ppermute(value, 'y', [(i, (i + distance) % size) for i in range(size)])]
    slice x9, local copies, waits for them, and re-layouts: 4.81 us -> 7.67 us  [the longest x2 3.82 us: scatter_rows(): got[k * block:(k + 1) * block].astype(jnp.float32)]
    unnamed x20 -> x30, local copies, waits for them, and re-layouts: 7.46 us -> 5.15 us
    dot_general x1, matrix products: 5.14 us -> 2.85 us  [expert_work(): up = jnp.dot(rows, up_w, preferred_element_type=jnp.float32)]
    dot_general x5, matrix products: 11.5 us -> 9.4 us  [contract_last(): lax.dot_general(left, right, (((1,), (1,)), ((), ())), preferred_element_...]
    concatenate x1, local copies, waits for them, and re-layouts: 0.24 us -> 2.32 us  [shards(): all_cot = jnp.concatenate([cot_mine, core_swap(cot_mine)], axis=0)]
  transfers between devices with their start and end apart: 18 -> 18, of which waited for: 12 -> 10; matrix products, arithmetic and copies ran while one was open for 35% -> 29% of each run, Pallas kernels for 0% -> 0%
where the time goes in v4:
time: 199 us; the launch traced here: 196 us
  waiting for transfers between devices  103 us (52%)
  matrix products  37.8 us (19%)
  starting transfers between devices  23.8 us (12%)
  local copies, waits for them, and re-layouts  17.8 us (9%)
  other arithmetic  11.5 us (6%)
    ppermute x14, waiting for transfers between devices, y_shift(): lax.ppermute(value, 'y', [(i, (i + distance) % size) for i in range(size)])  103 us
    dot_general x3, matrix products, contract_first(): lax.dot_general(left, right, (((0,), (0,)), ((), ())), preferred_element_...  18.2 us
    ppermute x14, starting transfers between devices, y_shift(): lax.ppermute(value, 'y', [(i, (i + distance) % size) for i in range(size)])  16.6 us
    dot_general x5, matrix products, contract_last(): lax.dot_general(left, right, (((1,), (1,)), ((), ())), preferred_element_...  9.4 us
    ppermute x4, starting transfers between devices, core_swap(): return lax.ppermute(value, 'core', [(0, 1), (1, 0)])  7.19 us
    dot_general x1, matrix products, expert_work(): gate = jnp.dot(rows, gate_w, preferred_element_type=jnp.float32)  5.33 us
    unnamed x30, local copies, waits for them, and re-layouts  5.15 us
  transfers between devices with their start and end apart: 18, of which 10 were waited for; matrix products, arithmetic and copies ran while one was open for 29% of the time, Pallas kernels for 0%

profile of v4, /device:TPU:1, one launch (start us, length us, event | category | flops | bytes accessed | tf_op | source)
XLA Modules:
  0.0 195.7 jit_solution(1772583684956215041)
XLA Ops:
  0.7 0.8 select_reduce_fusion
  1.5 0.6 fusion.30
  2.8 1.8 constant_dynamic-update-slice_fusion.9
  4.6 3.6 %collective-permute-start.1 = (bf16[60,7168]{1,0:T(8,128)(2,1)S(1)}, bf16[60,7168]{1,0:T(8,128)(2,1)S(1)}, u32[]{:S(2)}, u32[]{:S(2)}) collective-permute-start(bf16[60,7168]{1,0:T(8,128)(2,1)S(1)} %bitcast.49), channel_id=1, source_target_pairs={{0,6},{2,0},{4,2},{6,4},{1,7},{3,1},{5,3},{7,5},{8,14},{10,8},{12,... | collective-permute-start | bytes 2580488 | tf_op jit(solution)/shard_map/ppermute | solution.py:50
  8.2 19.0 %collective-permute-done.1 = bf16[60,7168]{1,0:T(8,128)(2,1)S(1)} collective-permute-done((bf16[60,7168]{1,0:T(8,128)(2,1)S(1)}, bf16[60,7168]{1,0:T(8,128)(2,1)S(1)}, u32[]{:S(2)}, u32[]{:S(2)}) %collective-permute-start.1) | collective-permute-done | bytes 860192 | tf_op jit(solution)/shard_map/ppermute | solution.py:50
  27.3 0.1 pad_maximum_fusion.3
  27.4 3.0 %collective-permute-done = bf16[60,7168]{1,0:T(8,128)(2,1)S(1)} collective-permute-done((bf16[60,7168]{1,0:T(8,128)(2,1)S(1)}, bf16[60,7168]{1,0:T(8,128)(2,1)S(1)}, u32[]{:S(2)}, u32[]{:S(2)}) %collective-permute-start) | collective-permute-done | bytes 860192 | tf_op jit(solution)/shard_map/ppermute | solution.py:50
  30.4 0.1 pad_maximum_fusion.2
  30.6 0.5 collective-permute-start.3
  31.1 1.0 collective-permute-start.2
  32.1 0.1 fusion.37
  32.3 0.1 fusion.38
  32.4 25.7 %collective-permute-done.3 = bf16[88,7168]{1,0:T(8,128)(2,1)S(1)} collective-permute-done((bf16[88,7168]{1,0:T(8,128)(2,1)S(1)}, bf16[88,7168]{1,0:T(8,128)(2,1)S(1)}, u32[]{:S(2)}, u32[]{:S(2)}) %collective-permute-start.3) | collective-permute-done | bytes 1261600 | tf_op jit(solution)/shard_map/ppermute | solution.py:50
  58.2 2.0 %collective-permute-start.11 = (bf16[28,7168]{1,0:T(8,128)(2,1)S(1)}, bf16[28,7168]{1,0:T(8,128)(2,1)S(1)}, u32[]{:S(2)}, u32[]{:S(2)}) collective-permute-start(bf16[28,7168]{1,0:T(8,128)(2,1)S(1)} %get-tuple-element.35), channel_id=1, source_target_pairs={{0,6},{2,0},{4,2},{6,4},{1,7},{3,1},{5,3},{7,5},{8,14},{10,8},{12,... | collective-permute-start | bytes 1204232 | tf_op jit(solution)/shard_map/ppermute | solution.py:50
  60.3 2.0 %collective-permute-done.2 = bf16[92,7168]{1,0:T(8,128)(2,1)S(1)} collective-permute-done((bf16[92,7168]{1,0:T(8,128)(2,1)S(1)}, bf16[92,7168]{1,0:T(8,128)(2,1)S(1)}, u32[]{:S(2)}, u32[]{:S(2)}) %collective-permute-start.2) | collective-permute-done | bytes 1318944 | tf_op jit(solution)/shard_map/ppermute | solution.py:50
  62.5 0.1 fusion.24
  62.6 2.9 %copy-done.9 = bf16[512,7168]{1,0:T(8,128)(2,1)} copy-done((bf16[512,7168]{1,0:T(8,128)(2,1)}, bf16[512,7168]{1,0:T(8,128)(2,1)S(1)}, u32[]{:S(2)}) %copy-start.9) | copy-done | bytes 7340056
  65.5 0.3 pad_maximum_fusion
  65.8 2.8 %collective-permute-start.4 = (bf16[256,7168]{1,0:T(8,128)(2,1)S(1)}, bf16[256,7168]{1,0:T(8,128)(2,1)S(1)}, u32[]{:S(2)}, u32[]{:S(2)}) collective-permute-start(bf16[256,7168]{1,0:T(8,128)(2,1)S(1)} %pad_maximum_fusion), channel_id=1, source_target_pairs={{0,1},{1,0},{2,3},{3,2},{4,5},{5,4},{6,7},{7,6},{8,9},{9,8},{10,11... | collective-permute-start | bytes 11010056 | tf_op jit(solution)/shard_map/ppermute | solution.py:54
  68.6 0.2 slice_select_fusion.1
  68.8 0.2 slice_select_fusion
  69.1 4.0 %collective-permute-done.10 = bf16[32,7168]{1,0:T(8,128)(2,1)S(1)} collective-permute-done((bf16[32,7168]{1,0:T(8,128)(2,1)S(1)}, bf16[32,7168]{1,0:T(8,128)(2,1)S(1)}, u32[]{:S(2)}, u32[]{:S(2)}) %collective-permute-start.10) | collective-permute-done | bytes 458784 | tf_op jit(solution)/shard_map/ppermute | solution.py:50
  73.2 0.3 pad_maximum_fusion.1
  73.5 3.6 %collective-permute-start.12 = (bf16[256,7168]{1,0:T(8,128)(2,1)S(1)}, bf16[256,7168]{1,0:T(8,128)(2,1)}, u32[]{:S(2)}, u32[]{:S(2)}) collective-permute-start(bf16[256,7168]{1,0:T(8,128)(2,1)S(1)} %pad_maximum_fusion.1), channel_id=1, source_target_pairs={{0,1},{1,0},{2,3},{3,2},{4,5},{5,4},{6,7},{7,6},{8,9},{9,8},{10,11... | collective-permute-start | bytes 11010056 | tf_op jit(solution)/shard_map/ppermute | solution.py:54
  77.1 2.1 %constant_dynamic-update-slice_fusion = bf16[512,7168]{1,0:T(8,128)(2,1)} fusion(bf16[512,7168]{1,0:T(8,128)(2,1)} %copy-done.9, bf16[256,7168]{1,0:T(8,128)(2,1)S(1)} %collective-permute-done.4), kind=kLoop, calls=%fused_computation.57 | loop fusion | bytes 7340032 | tf_op jit(solution)/shard_map/concatenate | solution.py:109
  79.2 1.3 copy-done.1
  80.5 5.3 %fusion.16 = f32[512,256]{1,0:T(8,128)S(1)} fusion(bf16[512,7168]{1,0:T(8,128)(2,1)} %constant_dynamic-update-slice_fusion, bf16[1,7168,256]{2,1,0:T(8,128)(2,1)S(1)} %copy-done.1), kind=kOutput, calls=%fused_computation.24 | convolution fusion | flops 1879048192 | bytes 11534336 | tf_op jit(solution)/shard_map/dot_general | solution.py:25
  85.8 0.9 copy-done.10
  86.8 2.9 %multiply_convert_fusion.2 = (bf16[512,256]{1,0:T(8,128)(2,1)S(1)}, f32[512,256]{1,0:T(8,128)}) fusion(f32[512,256]{1,0:T(8,128)S(1)} %fusion.16, bf16[512,7168]{1,0:T(8,128)(2,1)S(1)} %copy-done.10, bf16[1,7168,256]{2,1,0:T(8,128)(2,1)S(1)} %copy-done), kind=kOutput, calls=%fused_computation.52 | convolution fusion | flops 1879834624 | bytes 12320768 | tf_op jit(solution)/shard_map/dot_general | solution.py:26
  89.6 2.1 %convolution_convert_fusion = bf16[512,7168]{1,0:T(8,128)(2,1)S(1)} fusion(bf16[512,256]{1,0:T(8,128)(2,1)S(1)} %get-tuple-element.12, bf16[1,256,7168]{2,1,0:T(8,128)(2,1)S(1)} %copy-done.2), kind=kOutput, calls=%fused_computation | convolution fusion | flops 1882718208 | bytes 11272192 | tf_op jit(solution)/shard_map/dot_general | solution.py:29
  91.7 2.1 %slice.143 = bf16[256,7168]{1,0:T(8,128)(2,1)} slice(bf16[512,7168]{1,0:T(8,128)(2,1)S(1)} %convolution_convert_fusion), slice={[256:512], [0:7168]} | slice | bytes 7340032 | tf_op jit(solution)/shard_map/slice | solution.py:117
  93.9 1.4 fusion.31
  95.3 2.3 %constant_dynamic-update-slice_fusion.5 = bf16[512,7168]{1,0:T(8,128)(2,1)S(1)} fusion(bf16[512,7168]{1,0:T(8,128)(2,1)S(1)} %get-tuple-element.40, bf16[256,7168]{1,0:T(8,128)(2,1)} %collective-permute-done.12), kind=kLoop, calls=%fused_computation.62 | loop fusion | bytes 7340032 | tf_op jit(solution)/shard_map/concatenate | solution.py:112
  97.7 4.0 %fusion.4 = bf16[1,256,7168]{2,1,0:T(8,128)(2,1)} fusion(bf16[512,256]{1,0:T(8,128)(2,1)S(1)} %copy-done.6, bf16[512,7168]{1,0:T(8,128)(2,1)S(1)} %constant_dynamic-update-slice_fusion.5), kind=kOutput, calls=%fused_computation.10 | convolution fusion | flops 1880883200 | bytes 11272192 | tf_op jit(solution)/shard_map/dot_general | solution.py:19
  101.7 2.9 %multiply_convert_fusion = (bf16[512,256]{1,0:T(8,128)(2,1)}, bf16[512,256]{1,0:T(8,128)(2,1)S(1)}) fusion(f32[512,256]{1,0:T(8,128)S(1)} %copy-done.13, f32[512,256]{1,0:T(8,128)S(1)} %copy-done.14, bf16[512,7168]{1,0:T(8,128)(2,1)S(1)} %constant_dynamic-update-slice_fusion.5, bf16[1,256,7168]{2,1,0:T(8,128)(2,1)S(1)} %copy-done.2), kind=kOutput, calls=%fused_computation.49 | convolution fusion | flops 1880752128 | bytes 12582912 | tf_op jit(solution)/shard_map/dot_general | solution.py:13
  104.6 1.2 fusion.12
  105.8 2.1 %fusion.1 = bf16[256,7168]{1,0:T(8,128)(2,1)S(1)} fusion(f32[256,7168]{1,0:T(8,128)S(1)} %fusion.12, bf16[1,7168,256]{2,1,0:T(8,128)(2,1)S(1)} %copy-done, bf16[512,256]{1,0:T(8,128)(2,1)} %get-tuple-element.37), kind=kOutput, calls=%fused_computation.4 | convolution fusion | flops 943194112 | bytes 14811136 | tf_op jit(solution)/shard_map/dot_general | solution.py:13
  107.9 1.2 fusion.14
  109.1 0.8 collective-permute-start.13
  109.9 2.1 %fusion = bf16[256,7168]{1,0:T(8,128)(2,1)S(1)} fusion(f32[256,7168]{1,0:T(8,128)S(1)} %fusion.14, bf16[1,7168,256]{2,1,0:T(8,128)(2,1)S(1)} %copy-done, bf16[512,256]{1,0:T(8,128)(2,1)} %get-tuple-element.37), kind=kOutput, calls=%fused_computation.3 | convolution fusion | flops 943194112 | bytes 14811136 | tf_op jit(solution)/shard_map/dot_general | solution.py:13
  112.0 7.1 %fusion.3 = bf16[1,7168,256]{2,1,0:T(8,128)(2,1)} fusion(bf16[512,7168]{1,0:T(8,128)(2,1)} %constant_dynamic-update-slice_fusion, bf16[512,256]{1,0:T(8,128)(2,1)} %get-tuple-element.37), kind=kOutput, calls=%fused_computation.9 | convolution fusion | flops 1880883200 | bytes 11272192 | tf_op jit(solution)/shard_map/dot_general | solution.py:19
  119.0 7.0 %fusion.2 = bf16[1,7168,256]{2,1,0:T(8,128)(2,1)} fusion(bf16[512,7168]{1,0:T(8,128)(2,1)} %constant_dynamic-update-slice_fusion, bf16[512,256]{1,0:T(8,128)(2,1)S(1)} %copy-done.8), kind=kOutput, calls=%fused_computation.8 | convolution fusion | flops 1880883200 | bytes 11272192 | tf_op jit(solution)/shard_map/dot_general | solution.py:19
  126.1 0.2 fusion.32
  126.3 1.4 add_convert_fusion.7
  127.8 0.5 collective-permute-start.6
  128.2 1.1 collective-permute-start.8
  129.3 1.9 fusion.34
  131.2 9.7 %collective-permute-done.8 = bf16[28,7168]{1,0:T(8,128)(2,1)S(1)} collective-permute-done((bf16[28,7168]{1,0:T(8,128)(2,1)S(1)}, bf16[28,7168]{1,0:T(8,128)(2,1)S(1)}, u32[]{:S(2)}, u32[]{:S(2)}) %collective-permute-start.8) | collective-permute-done | bytes 401440 | tf_op jit(solution)/shard_map/ppermute | solution.py:50
  140.9 0.3 add_convert_fusion.5
  141.1 0.3 collective-permute-start.9
  141.4 1.4 add_convert_fusion.3
  142.9 0.3 add_convert_fusion.6
  143.2 2.5 %collective-permute-start.7 = (bf16[60,7168]{1,0:T(8,128)(2,1)S(1)}, bf16[60,7168]{1,0:T(8,128)(2,1)S(1)}, u32[]{:S(2)}, u32[]{:S(2)}) collective-permute-start(bf16[60,7168]{1,0:T(8,128)(2,1)S(1)} %add_convert_fusion.6), channel_id=1, source_target_pairs={{0,6},{2,0},{4,2},{6,4},{1,7},{3,1},{5,3},{7,5},{8,14},{10,8},{12,... | collective-permute-start | bytes 2580488 | tf_op jit(solution)/shard_map/ppermute | solution.py:50
  145.8 1.4 collective-permute-start.16
  147.2 1.9 fusion.33
  149.1 23.5 %collective-permute-done.16 = bf16[28,7168]{1,0:T(8,128)(2,1)S(1)} collective-permute-done((bf16[28,7168]{1,0:T(8,128)(2,1)S(1)}, bf16[28,7168]{1,0:T(8,128)(2,1)S(1)}, u32[]{:S(2)}, u32[]{:S(2)}) %collective-permute-start.16) | collective-permute-done | bytes 401440 | tf_op jit(solution)/shard_map/ppermute | solution.py:50
  172.7 0.3 add_convert_fusion.1
  173.0 0.5 collective-permute-done.14
  173.5 0.3 add_convert_fusion.2
  173.8 3.4 %collective-permute-start.15 = (bf16[60,7168]{1,0:T(8,128)(2,1)S(1)}, bf16[60,7168]{1,0:T(8,128)(2,1)S(1)}, u32[]{:S(2)}, u32[]{:S(2)}) collective-permute-start(bf16[60,7168]{1,0:T(8,128)(2,1)S(1)} %add_convert_fusion.2), channel_id=1, source_target_pairs={{0,6},{2,0},{4,2},{6,4},{1,7},{3,1},{5,3},{7,5},{8,14},{10,8},{12,... | collective-permute-start | bytes 2580488 | tf_op jit(solution)/shard_map/ppermute | solution.py:50
  177.2 1.4 fusion.22
  178.6 15.1 %collective-permute-done.17 = bf16[60,7168]{1,0:T(8,128)(2,1)S(1)} collective-permute-done((bf16[60,7168]{1,0:T(8,128)(2,1)S(1)}, bf16[60,7168]{1,0:T(8,128)(2,1)S(1)}, u32[]{:S(2)}, u32[]{:S(2)}) %collective-permute-start.17) | collective-permute-done | bytes 860192 | tf_op jit(solution)/shard_map/ppermute | solution.py:50
  193.8 0.5 collective-permute-done.15
  194.3 1.4 fusion.23
  (51 shorter events, 0.9 us)
Async XLA Ops:
  4.6 22.7 %collective-permute-start.1 = (bf16[60,7168]{1,0:T(8,128)(2,1)S(1)}, bf16[60,7168]{1,0:T(8,128)(2,1)S(1)}, u32[]{:S(2)}, u32[]{:S(2)}) collective-permute-start(bf16[60,7168]{1,0:T(8,128)(2,1)S(1)} %bitcast.49), channel_id=1, source_target_pairs={{0,6},{2,0},{4,2},{6,4},{1,7},{3,1},{5,3},{7,5},{8,14},{10,8},{12,... | collective-permute-start | bytes 2580488 | tf_op jit(solution)/shard_map/ppermute | solution.py:50
  8.2 22.2 %collective-permute-start = (bf16[60,7168]{1,0:T(8,128)(2,1)S(1)}, bf16[60,7168]{1,0:T(8,128)(2,1)S(1)}, u32[]{:S(2)}, u32[]{:S(2)}) collective-permute-start(bf16[60,7168]{1,0:T(8,128)(2,1)S(1)} %bitcast.50), channel_id=1, source_target_pairs={{0,2},{2,4},{4,6},{6,0},{1,3},{3,5},{5,7},{7,1},{8,10},{10,12},{12... | collective-permute-start | bytes 2580488 | tf_op jit(solution)/shard_map/ppermute | solution.py:50
  30.6 27.5 %collective-permute-start.3 = (bf16[88,7168]{1,0:T(8,128)(2,1)S(1)}, bf16[88,7168]{1,0:T(8,128)(2,1)S(1)}, u32[]{:S(2)}, u32[]{:S(2)}) collective-permute-start(bf16[88,7168]{1,0:T(8,128)(2,1)S(1)} %pad_maximum_fusion.3), channel_id=1, source_target_pairs={{0,6},{2,0},{4,2},{6,4},{1,7},{3,1},{5,3},{7,5},{8,14},{10,8},{12,... | collective-permute-start | bytes 3784712 | tf_op jit(solution)/shard_map/ppermute | solution.py:50
  31.1 31.1 %collective-permute-start.2 = (bf16[92,7168]{1,0:T(8,128)(2,1)S(1)}, bf16[92,7168]{1,0:T(8,128)(2,1)S(1)}, u32[]{:S(2)}, u32[]{:S(2)}) collective-permute-start(bf16[92,7168]{1,0:T(8,128)(2,1)S(1)} %pad_maximum_fusion.2), channel_id=1, source_target_pairs={{0,2},{2,4},{4,6},{6,0},{1,3},{3,5},{5,7},{7,1},{8,10},{10,12},{12... | collective-permute-start | bytes 3956744 | tf_op jit(solution)/shard_map/ppermute | solution.py:50
  58.2 10.8 %collective-permute-start.11 = (bf16[28,7168]{1,0:T(8,128)(2,1)S(1)}, bf16[28,7168]{1,0:T(8,128)(2,1)S(1)}, u32[]{:S(2)}, u32[]{:S(2)}) collective-permute-start(bf16[28,7168]{1,0:T(8,128)(2,1)S(1)} %get-tuple-element.35), channel_id=1, source_target_pairs={{0,6},{2,0},{4,2},{6,4},{1,7},{3,1},{5,3},{7,5},{8,14},{10,8},{12,... | collective-permute-start | bytes 1204232 | tf_op jit(solution)/shard_map/ppermute | solution.py:50
  62.4 10.7 %collective-permute-start.10 = (bf16[32,7168]{1,0:T(8,128)(2,1)S(1)}, bf16[32,7168]{1,0:T(8,128)(2,1)S(1)}, u32[]{:S(2)}, u32[]{:S(2)}) collective-permute-start(bf16[32,7168]{1,0:T(8,128)(2,1)S(1)} %get-tuple-element.31), channel_id=1, source_target_pairs={{0,2},{2,4},{4,6},{6,0},{1,3},{3,5},{5,7},{7,1},{8,10},{10,12},{12... | collective-permute-start | bytes 1376264 | tf_op jit(solution)/shard_map/ppermute | solution.py:50
  62.6 2.9 %copy-start.9 = (bf16[512,7168]{1,0:T(8,128)(2,1)}, bf16[512,7168]{1,0:T(8,128)(2,1)S(1)}, u32[]{:S(2)}) copy-start(bf16[512,7168]{1,0:T(8,128)(2,1)S(1)} %get-tuple-element.46) | copy-start | bytes 22020100
  65.5 3.1 %copy-start.11 = (pred[64]{0:T(512)(128)(4,1)S(1)}, pred[64]{0:T(512)(128)(4,1)}, u32[]{:S(2)}) copy-start(pred[64]{0:T(512)(128)(4,1)} %constant.30.clone.1) | copy-start | bytes 196
  65.8 11.3 %collective-permute-start.4 = (bf16[256,7168]{1,0:T(8,128)(2,1)S(1)}, bf16[256,7168]{1,0:T(8,128)(2,1)S(1)}, u32[]{:S(2)}, u32[]{:S(2)}) collective-permute-start(bf16[256,7168]{1,0:T(8,128)(2,1)S(1)} %pad_maximum_fusion), channel_id=1, source_target_pairs={{0,1},{1,0},{2,3},{3,2},{4,5},{5,4},{6,7},{7,6},{8,9},{9,8},{10,11... | collective-permute-start | bytes 11010056 | tf_op jit(solution)/shard_map/ppermute | solution.py:54
  73.5 21.8 %collective-permute-start.12 = (bf16[256,7168]{1,0:T(8,128)(2,1)S(1)}, bf16[256,7168]{1,0:T(8,128)(2,1)}, u32[]{:S(2)}, u32[]{:S(2)}) collective-permute-start(bf16[256,7168]{1,0:T(8,128)(2,1)S(1)} %pad_maximum_fusion.1), channel_id=1, source_target_pairs={{0,1},{1,0},{2,3},{3,2},{4,5},{5,4},{6,7},{7,6},{8,9},{9,8},{10,11... | collective-permute-start | bytes 11010056 | tf_op jit(solution)/shard_map/ppermute | solution.py:54
  77.1 3.4 %copy-start.1 = (bf16[1,7168,256]{2,1,0:T(8,128)(2,1)S(1)}, bf16[1,7168,256]{2,1,0:T(8,128)(2,1)}, u32[]{:S(2)}) copy-start(bf16[1,7168,256]{2,1,0:T(8,128)(2,1)} %param.9) | copy-start | bytes 11010052
  80.5 5.3 %copy-start = (bf16[1,7168,256]{2,1,0:T(8,128)(2,1)S(1)}, bf16[1,7168,256]{2,1,0:T(8,128)(2,1)}, u32[]{:S(2)}) copy-start(bf16[1,7168,256]{2,1,0:T(8,128)(2,1)} %param.10) | copy-start | bytes 11010052
  80.5 6.3 %copy-start.10 = (bf16[512,7168]{1,0:T(8,128)(2,1)S(1)}, bf16[512,7168]{1,0:T(8,128)(2,1)}, u32[]{:S(2)}) copy-start(bf16[512,7168]{1,0:T(8,128)(2,1)} %constant_dynamic-update-slice_fusion) | copy-start | bytes 22020100
  86.8 2.9 %copy-start.12 = (f32[512,256]{1,0:T(8,128)}, f32[512,256]{1,0:T(8,128)S(1)}, u32[]{:S(2)}) copy-start(f32[512,256]{1,0:T(8,128)S(1)} %fusion.16) | copy-start | bytes 1572868
  86.8 2.9 %copy-start.2 = (bf16[1,256,7168]{2,1,0:T(8,128)(2,1)S(1)}, bf16[1,256,7168]{2,1,0:T(8,128)(2,1)}, u32[]{:S(2)}) copy-start(bf16[1,256,7168]{2,1,0:T(8,128)(2,1)} %param.11) | copy-start | bytes 11010052
  89.6 2.1 %copy-start.5 = (bf16[512,256]{1,0:T(8,128)(2,1)}, bf16[512,256]{1,0:T(8,128)(2,1)S(1)}, u32[]{:S(2)}) copy-start(bf16[512,256]{1,0:T(8,128)(2,1)S(1)} %get-tuple-element.12) | copy-start | bytes 786436
  93.9 32.4 %collective-permute-start.5 = (bf16[256,7168]{1,0:T(8,128)(2,1)}, bf16[256,7168]{1,0:T(8,128)(2,1)}, u32[]{:S(2)}, u32[]{:S(2)}) collective-permute-start(bf16[256,7168]{1,0:T(8,128)(2,1)} %slice.143), channel_id=1, source_target_pairs={{0,1},{1,0},{2,3},{3,2},{4,5},{5,4},{6,7},{7,6},{8,9},{9,8},{10,11... | collective-permute-start | bytes 11010056 | tf_op jit(solution)/shard_map/ppermute | solution.py:54
  95.3 2.3 %copy-start.6 = (bf16[512,256]{1,0:T(8,128)(2,1)S(1)}, bf16[512,256]{1,0:T(8,128)(2,1)}, u32[]{:S(2)}) copy-start(bf16[512,256]{1,0:T(8,128)(2,1)} %copy-done.5) | copy-start | bytes 786436
  97.7 4.1 %copy-start.13 = (f32[512,256]{1,0:T(8,128)S(1)}, f32[512,256]{1,0:T(8,128)}, u32[]{:S(2)}) copy-start(f32[512,256]{1,0:T(8,128)} %copy-done.12) | copy-start | bytes 1572868
  97.7 4.1 %copy-start.14 = (f32[512,256]{1,0:T(8,128)S(1)}, f32[512,256]{1,0:T(8,128)}, u32[]{:S(2)}) copy-start(f32[512,256]{1,0:T(8,128)} %get-tuple-element.10) | copy-start | bytes 1572868
  104.6 1.2 copy-start.7
  105.8 2.2 %copy-start.8 = (bf16[512,256]{1,0:T(8,128)(2,1)S(1)}, bf16[512,256]{1,0:T(8,128)(2,1)}, u32[]{:S(2)}) copy-start(bf16[512,256]{1,0:T(8,128)(2,1)} %copy-done.7) | copy-start | bytes 786436
  109.1 32.3 %collective-permute-start.13 = (bf16[256,7168]{1,0:T(8,128)(2,1)S(1)}, bf16[256,7168]{1,0:T(8,128)(2,1)}, u32[]{:S(2)}, u32[]{:S(2)}) collective-permute-start(bf16[256,7168]{1,0:T(8,128)(2,1)S(1)} %fusion.1), channel_id=1, source_target_pairs={{0,1},{1,0},{2,3},{3,2},{4,5},{5,4},{6,7},{7,6},{8,9},{9,8},{10,11... | collective-permute-start | bytes 11010056 | tf_op jit(solution)/shard_map/ppermute | solution.py:54
  127.7 13.2 %copy-start.3 = (bf16[64,7168]{1,0:T(8,128)(2,1)S(1)}, bf16[64,7168]{1,0:T(8,128)(2,1)}, u32[]{:S(2)}) copy-start(bf16[64,7168]{1,0:T(8,128)(2,1)} %get-tuple-element.18) | copy-start | bytes 2752516
  127.8 15.1 %collective-permute-start.6 = (bf16[32,7168]{1,0:T(8,128)(2,1)S(1)}, bf16[32,7168]{1,0:T(8,128)(2,1)S(1)}, u32[]{:S(2)}, u32[]{:S(2)}) collective-permute-start(bf16[32,7168]{1,0:T(8,128)(2,1)S(1)} %slice.190), channel_id=1, source_target_pairs={{0,6},{2,0},{4,2},{6,4},{1,7},{3,1},{5,3},{7,5},{8,14},{10,8},{12,... | collective-permute-start | bytes 1376264 | tf_op jit(solution)/shard_map/ppermute | solution.py:50
  128.2 12.6 %collective-permute-start.8 = (bf16[28,7168]{1,0:T(8,128)(2,1)S(1)}, bf16[28,7168]{1,0:T(8,128)(2,1)S(1)}, u32[]{:S(2)}, u32[]{:S(2)}) collective-permute-start(bf16[28,7168]{1,0:T(8,128)(2,1)S(1)} %slice.194), channel_id=1, source_target_pairs={{0,2},{2,4},{4,6},{6,0},{1,3},{3,5},{5,7},{7,1},{8,10},{10,12},{12... | collective-permute-start | bytes 1204232 | tf_op jit(solution)/shard_map/ppermute | solution.py:50
  141.1 36.1 %collective-permute-start.9 = (bf16[60,7168]{1,0:T(8,128)(2,1)S(1)}, bf16[60,7168]{1,0:T(8,128)(2,1)S(1)}, u32[]{:S(2)}, u32[]{:S(2)}) collective-permute-start(bf16[60,7168]{1,0:T(8,128)(2,1)S(1)} %add_convert_fusion.5), channel_id=1, source_target_pairs={{0,2},{2,4},{4,6},{6,0},{1,3},{3,5},{5,7},{7,1},{8,10},{10,12},{12... | collective-permute-start | bytes 2580488 | tf_op jit(solution)/shard_map/ppermute | solution.py:50
  143.2 34.1 %collective-permute-start.7 = (bf16[60,7168]{1,0:T(8,128)(2,1)S(1)}, bf16[60,7168]{1,0:T(8,128)(2,1)S(1)}, u32[]{:S(2)}, u32[]{:S(2)}) collective-permute-start(bf16[60,7168]{1,0:T(8,128)(2,1)S(1)} %add_convert_fusion.6), channel_id=1, source_target_pairs={{0,6},{2,0},{4,2},{6,4},{1,7},{3,1},{5,3},{7,5},{8,14},{10,8},{12,... | collective-permute-start | bytes 2580488 | tf_op jit(solution)/shard_map/ppermute | solution.py:50
  145.7 27.8 %collective-permute-start.14 = (bf16[32,7168]{1,0:T(8,128)(2,1)S(1)}, bf16[32,7168]{1,0:T(8,128)(2,1)S(1)}, u32[]{:S(2)}, u32[]{:S(2)}) collective-permute-start(bf16[32,7168]{1,0:T(8,128)(2,1)S(1)} %slice.213), channel_id=1, source_target_pairs={{0,6},{2,0},{4,2},{6,4},{1,7},{3,1},{5,3},{7,5},{8,14},{10,8},{12,... | collective-permute-start | bytes 1376264 | tf_op jit(solution)/shard_map/ppermute | solution.py:50
  145.8 26.8 %collective-permute-start.16 = (bf16[28,7168]{1,0:T(8,128)(2,1)S(1)}, bf16[28,7168]{1,0:T(8,128)(2,1)S(1)}, u32[]{:S(2)}, u32[]{:S(2)}) collective-permute-start(bf16[28,7168]{1,0:T(8,128)(2,1)S(1)} %slice.218), channel_id=1, source_target_pairs={{0,2},{2,4},{4,6},{6,0},{1,3},{3,5},{5,7},{7,1},{8,10},{10,12},{12... | collective-permute-start | bytes 1204232 | tf_op jit(solution)/shard_map/ppermute | solution.py:50
  149.1 28.1 %copy-start.4 = (bf16[64,7168]{1,0:T(8,128)(2,1)S(1)}, bf16[64,7168]{1,0:T(8,128)(2,1)}, u32[]{:S(2)}) copy-start(bf16[64,7168]{1,0:T(8,128)(2,1)} %get-tuple-element.17) | copy-start | bytes 2752516
  172.9 20.8 %collective-permute-start.17 = (bf16[60,7168]{1,0:T(8,128)(2,1)S(1)}, bf16[60,7168]{1,0:T(8,128)(2,1)S(1)}, u32[]{:S(2)}, u32[]{:S(2)}) collective-permute-start(bf16[60,7168]{1,0:T(8,128)(2,1)S(1)} %add_convert_fusion.1), channel_id=1, source_target_pairs={{0,2},{2,4},{4,6},{6,0},{1,3},{3,5},{5,7},{7,1},{8,10},{10,12},{12... | collective-permute-start | bytes 2580488 | tf_op jit(solution)/shard_map/ppermute | solution.py:50
  173.8 20.5 %collective-permute-start.15 = (bf16[60,7168]{1,0:T(8,128)(2,1)S(1)}, bf16[60,7168]{1,0:T(8,128)(2,1)S(1)}, u32[]{:S(2)}, u32[]{:S(2)}) collective-permute-start(bf16[60,7168]{1,0:T(8,128)(2,1)S(1)} %add_convert_fusion.2), channel_id=1, source_target_pairs={{0,6},{2,0},{4,2},{6,4},{1,7},{3,1},{5,3},{7,5},{8,14},{10,8},{12,... | collective-permute-start | bytes 2580488 | tf_op jit(solution)/shard_map/ppermute | solution.py:50

commit v5 on v3

--- a/solution.py
+++ b/solution.py
@@ -26,7 +26,11 @@
     up = jnp.dot(rows, up_w, preferred_element_type=jnp.float32)
     active = jax.nn.silu(gate)
     hidden = (active * up).astype(jnp.bfloat16)
-    out_part = jnp.dot(hidden, down_w, preferred_element_type=jnp.float32).astype(jnp.bfloat16)
+    half = rows.shape[0] // 2
+    out_part = tuple(
+        jnp.dot(hidden[pick], down_w, preferred_element_type=jnp.float32).astype(jnp.bfloat16)
+        for pick in (slice(half, None), slice(None, half))
+    )
     out_part, hidden, gate, up = lax.optimization_barrier((out_part, hidden, gate, up))
     active = jax.nn.silu(gate)
     hidden_grad = contract_last(cot_rows, down_w)
@@ -106,8 +110,7 @@
     out_part, in_part, gate_term, up_term, down_term = expert_work(
         all_rows, all_cot, gate_w, up_w, down_w
     )
-    half = out_part.shape[0] // 2
-    outputs = scatter_rows(out_part[half:], out_part[:half])[:slots]
+    outputs = scatter_rows(*out_part)[:slots]
     input_grads = scatter_rows(*in_part)[:slots]
     gate_grad = gate_term.astype(jnp.bfloat16)
     up_grad = up_term.astype(jnp.bfloat16)

time: 199 us -> 185 us (0.930)
  matrix products: 45.7 us -> 36.6 us
  local copies, waits for them, and re-layouts: 17.4 us -> 9.58 us
  waiting for transfers between devices: 99.6 us -> 104 us
    ppermute x14, waiting for transfers between devices: 99.6 us -> 104 us  [y_shift(): lax.ppermute(value, 'y', [(i, (i + distance) % size) for i in range(size)])]
    dot_general x3, matrix products: 19.6 us -> 16.3 us  [contract_first(): lax.dot_general(left, right, (((0,), (0,)), ((), ())), preferred_element_...]
    unnamed x20 -> x24, local copies, waits for them, and re-layouts: 7.46 us -> 4.31 us
    dot_general x1, matrix products: 5.14 us -> 2.09 us  [expert_work(): up = jnp.dot(rows, up_w, preferred_element_type=jnp.float32)]
    dot_general x5, matrix products: 11.5 us -> 8.64 us  [contract_last(): lax.dot_general(left, right, (((1,), (1,)), ((), ())), preferred_element_...]
    slice x1 -> x0, local copies, waits for them, and re-layouts: 2.27 us -> none  [shards(): outputs = scatter_rows(out_part[half:], out_part[:half])[:slots]]
    dot_general x1 -> x2, matrix products: 4.12 us -> 4.27 us  [expert_work(): jnp.dot(hidden[pick], down_w, preferred_element_type=jnp.float32)]
  transfers between devices with their start and end apart: 18 -> 18, of which waited for: 12 -> 12; matrix products, arithmetic and copies ran while one was open for 35% -> 28% of each run, Pallas kernels for 0% -> 0%
where the time goes in v5:
time: 185 us; the launch traced here: 184 us
  waiting for transfers between devices  104 us (56%)
  matrix products  36.6 us (20%)
  starting transfers between devices  19.6 us (11%)
  other arithmetic  13.3 us (7%)
  local copies, waits for them, and re-layouts  9.58 us (5%)
    ppermute x14, waiting for transfers between devices, y_shift(): lax.ppermute(value, 'y', [(i, (i + distance) % size) for i in range(size)])  104 us
    dot_general x3, matrix products, contract_first(): lax.dot_general(left, right, (((0,), (0,)), ((), ())), preferred_element_...  16.3 us
    ppermute x14, starting transfers between devices, y_shift(): lax.ppermute(value, 'y', [(i, (i + distance) % size) for i in range(size)])  12.8 us
    dot_general x5, matrix products, contract_last(): lax.dot_general(left, right, (((1,), (1,)), ((), ())), preferred_element_...  8.64 us
    ppermute x4, starting transfers between devices, core_swap(): return lax.ppermute(value, 'core', [(0, 1), (1, 0)])  6.78 us
    dot_general x1, matrix products, expert_work(): gate = jnp.dot(rows, gate_w, preferred_element_type=jnp.float32)  5.29 us
    unnamed x24, local copies, waits for them, and re-layouts  4.31 us
    dot_general x2, matrix products, expert_work(): jnp.dot(hidden[pick], down_w, preferred_element_type=jnp.float32)  4.27 us
  transfers between devices with their start and end apart: 18, of which 12 were waited for; matrix products, arithmetic and copies ran while one was open for 28% of the time, Pallas kernels for 0%

profile of v5, /device:TPU:1, one launch (start us, length us, event | category | flops | bytes accessed | tf_op | source)
XLA Modules:
  0.0 184.3 jit_solution(14670370877327709877)
XLA Ops:
  0.7 0.8 select_reduce_fusion
  1.5 0.6 fusion.27
  2.8 1.8 constant_dynamic-update-slice_fusion.9
  4.6 3.6 %collective-permute-start.1 = (bf16[64,7168]{1,0:T(8,128)(2,1)S(1)}, bf16[64,7168]{1,0:T(8,128)(2,1)S(1)}, u32[]{:S(2)}, u32[]{:S(2)}) collective-permute-start(bf16[64,7168]{1,0:T(8,128)(2,1)S(1)} %get-tuple-element.50), channel_id=1, source_target_pairs={{0,6},{2,0},{4,2},{6,4},{1,7},{3,1},{5,3},{7,5},{8,14},{10,8},{12,... | collective-permute-start | bytes 2752520 | tf_op jit(solution)/shard_map/ppermute | solution.py:54
  8.2 0.1 constant_dynamic-update-slice_fusion.6
  8.3 18.9 %collective-permute-done.1 = bf16[64,7168]{1,0:T(8,128)(2,1)S(1)} collective-permute-done((bf16[64,7168]{1,0:T(8,128)(2,1)S(1)}, bf16[64,7168]{1,0:T(8,128)(2,1)S(1)}, u32[]{:S(2)}, u32[]{:S(2)}) %collective-permute-start.1) | collective-permute-done | bytes 917536 | tf_op jit(solution)/shard_map/ppermute | solution.py:54
  27.3 3.1 %collective-permute-done = bf16[64,7168]{1,0:T(8,128)(2,1)S(1)} collective-permute-done((bf16[64,7168]{1,0:T(8,128)(2,1)S(1)}, bf16[64,7168]{1,0:T(8,128)(2,1)S(1)}, u32[]{:S(2)}, u32[]{:S(2)}) %collective-permute-start) | collective-permute-done | bytes 917536 | tf_op jit(solution)/shard_map/ppermute | solution.py:54
  30.4 0.3 pad_maximum_fusion
  30.7 0.4 collective-permute-start.3
  31.1 1.1 collective-permute-start.2
  32.3 0.1 constant_dynamic-update-slice_fusion.1
  32.4 0.1 constant_dynamic-update-slice_fusion
  32.6 29.7 %collective-permute-done.2 = bf16[96,7168]{1,0:T(8,128)(2,1)S(1)} collective-permute-done((bf16[96,7168]{1,0:T(8,128)(2,1)S(1)}, bf16[96,7168]{1,0:T(8,128)(2,1)S(1)}, u32[]{:S(2)}, u32[]{:S(2)}) %collective-permute-start.2) | collective-permute-done | bytes 1376288 | tf_op jit(solution)/shard_map/ppermute | solution.py:54
  62.3 0.1 fusion.29
  62.4 0.1 fusion.28
  62.5 0.2 collective-permute-start.11
  62.7 1.3 collective-permute-start.10
  64.1 1.4 copy-done.5
  65.4 2.7 %collective-permute-start.4 = (bf16[256,7168]{1,0:T(8,128)(2,1)S(1)}, bf16[256,7168]{1,0:T(8,128)(2,1)S(1)}, u32[]{:S(2)}, u32[]{:S(2)}) collective-permute-start(bf16[256,7168]{1,0:T(8,128)(2,1)S(1)} %get-tuple-element.29), channel_id=1, source_target_pairs={{0,1},{1,0},{2,3},{3,2},{4,5},{5,4},{6,7},{7,6},{8,9},{9,8},{10,11... | collective-permute-start | bytes 11010056 | tf_op jit(solution)/shard_map/ppermute | solution.py:58
  68.1 0.1 slice_dynamic-update-slice_fusion.3
  68.2 0.1 slice_dynamic-update-slice_fusion.1
  68.3 5.0 %collective-permute-done.10 = bf16[32,7168]{1,0:T(8,128)(2,1)S(1)} collective-permute-done((bf16[32,7168]{1,0:T(8,128)(2,1)S(1)}, bf16[32,7168]{1,0:T(8,128)(2,1)S(1)}, u32[]{:S(2)}, u32[]{:S(2)}) %collective-permute-start.10) | collective-permute-done | bytes 458784 | tf_op jit(solution)/shard_map/ppermute | solution.py:54
  73.5 3.6 %collective-permute-start.12 = (bf16[256,7168]{1,0:T(8,128)(2,1)S(1)}, bf16[256,7168]{1,0:T(8,128)(2,1)S(1)}, u32[]{:S(2)}, u32[]{:S(2)}) collective-permute-start(bf16[256,7168]{1,0:T(8,128)(2,1)S(1)} %get-tuple-element.45), channel_id=1, source_target_pairs={{0,1},{1,0},{2,3},{3,2},{4,5},{5,4},{6,7},{7,6},{8,9},{9,8},{10,11... | collective-permute-start | bytes 11010056 | tf_op jit(solution)/shard_map/ppermute | solution.py:58
  77.1 2.1 %constant_dynamic-update-slice_fusion.3 = bf16[512,7168]{1,0:T(8,128)(2,1)} fusion(bf16[512,7168]{1,0:T(8,128)(2,1)} %copy-done.5, bf16[256,7168]{1,0:T(8,128)(2,1)S(1)} %collective-permute-done.4), kind=kLoop, calls=%fused_computation.61 | loop fusion | bytes 7340032 | tf_op jit(solution)/shard_map/concatenate | solution.py:106
  79.2 1.3 copy-done.4
  80.5 5.3 %fusion.17 = f32[512,256]{1,0:T(8,128)S(1)} fusion(bf16[512,7168]{1,0:T(8,128)(2,1)} %constant_dynamic-update-slice_fusion.3, bf16[1,7168,256]{2,1,0:T(8,128)(2,1)S(1)} %copy-done.4), kind=kOutput, calls=%fused_computation.24 | convolution fusion | flops 1879048192 | bytes 11534336 | tf_op jit(solution)/shard_map/dot_general | solution.py:25
  85.8 1.0 copy-done.6
  86.8 2.1 %multiply_convert_fusion.2 = (bf16[512,256]{1,0:T(8,128)(2,1)S(1)}, f32[512,256]{1,0:T(8,128)S(1)}) fusion(f32[512,256]{1,0:T(8,128)S(1)} %fusion.17, bf16[512,7168]{1,0:T(8,128)(2,1)S(1)} %copy-done.6, bf16[1,7168,256]{2,1,0:T(8,128)(2,1)S(1)} %copy-done.1), kind=kOutput, calls=%fused_computation.47 | convolution fusion | flops 1879834624 | bytes 12320768 | tf_op jit(solution)/shard_map/dot_general | solution.py:26
  88.9 1.1 convolution_convert_fusion.3
  90.0 3.1 %convolution_convert_fusion.4 = bf16[256,7168]{1,0:T(8,128)(2,1)} fusion(bf16[1,256,7168]{2,1,0:T(8,128)(2,1)S(1)} %copy-done, bf16[512,256]{1,0:T(8,128)(2,1)S(1)} %get-tuple-element.14), kind=kOutput, calls=%fused_computation.8 | convolution fusion | flops 941359104 | bytes 7471104 | tf_op jit(solution)/shard_map/dot_general | solution.py:31
  93.2 0.2 constant_dynamic-update-slice_fusion.10
  93.4 2.2 %multiply_convert_fusion = (bf16[512,256]{1,0:T(8,128)(2,1)S(1)}, bf16[512,256]{1,0:T(8,128)(2,1)S(1)}) fusion(f32[512,256]{1,0:T(8,128)S(1)} %fusion.17, f32[512,256]{1,0:T(8,128)S(1)} %get-tuple-element.12, bf16[512,7168]{1,0:T(8,128)(2,1)S(1)} %constant_dynamic-update-slice_fusion.10, bf16[1,256,7168]{2,1,0:T(8,128)(2,1)S(1)} %copy-done), kind=kOutput, calls=%fused_computation.44 | convolution fusion | flops 1880752128 | bytes 12582912 | tf_op jit(solution)/shard_map/dot_general | solution.py:13
  95.6 1.1 fusion.13
  96.8 3.0 %fusion.1 = bf16[256,7168]{1,0:T(8,128)(2,1)} fusion(f32[256,7168]{1,0:T(8,128)S(1)} %fusion.13, bf16[1,7168,256]{2,1,0:T(8,128)(2,1)S(1)} %copy-done.1, bf16[512,256]{1,0:T(8,128)(2,1)S(1)} %get-tuple-element.33), kind=kOutput, calls=%fused_computation.3 | convolution fusion | flops 943194112 | bytes 14811136 | tf_op jit(solution)/shard_map/dot_general | solution.py:13
  99.8 0.5 collective-permute-start.13
  100.3 1.1 fusion.15
  101.4 1.2 fusion
  102.6 8.4 %fusion.3 = bf16[1,7168,256]{2,1,0:T(8,128)(2,1)} fusion(bf16[512,7168]{1,0:T(8,128)(2,1)} %constant_dynamic-update-slice_fusion.3, bf16[512,256]{1,0:T(8,128)(2,1)S(1)} %get-tuple-element.33), kind=kOutput, calls=%fused_computation.10 | convolution fusion | flops 1880883200 | bytes 11272192 | tf_op jit(solution)/shard_map/dot_general | solution.py:19
  111.0 4.0 %fusion.2 = bf16[1,7168,256]{2,1,0:T(8,128)(2,1)} fusion(bf16[512,7168]{1,0:T(8,128)(2,1)S(1)} %bitcast.49, bf16[512,256]{1,0:T(8,128)(2,1)S(1)} %get-tuple-element.34), kind=kOutput, calls=%fused_computation.9 | convolution fusion | flops 1880883200 | bytes 11272192 | tf_op jit(solution)/shard_map/dot_general | solution.py:19
  115.0 3.9 %fusion.4 = bf16[1,256,7168]{2,1,0:T(8,128)(2,1)} fusion(bf16[512,256]{1,0:T(8,128)(2,1)S(1)} %get-tuple-element.14, bf16[512,7168]{1,0:T(8,128)(2,1)S(1)} %constant_dynamic-update-slice_fusion.10), kind=kOutput, calls=%fused_computation.11 | convolution fusion | flops 1880883200 | bytes 11272192 | tf_op jit(solution)/shard_map/dot_general | solution.py:19
  119.0 1.4 add_convert_fusion.7
  120.4 0.1 collective-permute-start.6
  120.5 1.5 collective-permute-start.8
  122.0 1.2 slice.156
  123.2 1.4 add_convert_fusion.3
  124.7 1.4 collective-permute-start.14
  126.0 0.2 collective-permute-start.16
  126.2 1.2 slice.175
  127.5 5.1 %collective-permute-done.6 = bf16[32,7168]{1,0:T(8,128)(2,1)S(1)} collective-permute-done((bf16[32,7168]{1,0:T(8,128)(2,1)S(1)}, bf16[32,7168]{1,0:T(8,128)(2,1)S(1)}, u32[]{:S(2)}, u32[]{:S(2)}) %collective-permute-start.6) | collective-permute-done | bytes 458784 | tf_op jit(solution)/shard_map/ppermute | solution.py:54
  132.6 1.2 collective-permute-done.8
  133.7 2.1 %add_convert_fusion.6 = (bf16[64,7168]{1,0:T(8,128)(2,1)S(1)}, bf16[64,7168]{1,0:T(8,128)(2,1)S(1)}) fusion(bf16[256,7168]{1,0:T(8,128)(2,1)} %collective-permute-done.5, bf16[32,7168]{1,0:T(8,128)(2,1)S(1)} %collective-permute-done.6, bf16[256,7168]{1,0:T(8,128)(2,1)S(1)} %convolution_convert_fusion.3, bf16[32,7168]{1,0:T(8,128)(2,1)S(1)} %collective-permute-done.8), kind=kLoop, calls=%fused_computation.32 | loop fusion | flops 5505024 | bytes 6422528 | tf_op jit(solution)/shard_map/convert_element_type | solution.py:74
  135.8 0.2 collective-permute-start.7
  136.0 1.3 collective-permute-start.9
  137.4 5.0 %collective-permute-done.14 = bf16[32,7168]{1,0:T(8,128)(2,1)S(1)} collective-permute-done((bf16[32,7168]{1,0:T(8,128)(2,1)S(1)}, bf16[32,7168]{1,0:T(8,128)(2,1)S(1)}, u32[]{:S(2)}, u32[]{:S(2)}) %collective-permute-start.14) | collective-permute-done | bytes 458784 | tf_op jit(solution)/shard_map/ppermute | solution.py:54
  142.4 1.2 collective-permute-done.16
  143.6 2.1 %add_convert_fusion.2 = (bf16[64,7168]{1,0:T(8,128)(2,1)S(1)}, bf16[64,7168]{1,0:T(8,128)(2,1)S(1)}) fusion(bf16[256,7168]{1,0:T(8,128)(2,1)} %collective-permute-done.13, bf16[256,7168]{1,0:T(8,128)(2,1)S(1)} %fusion, bf16[32,7168]{1,0:T(8,128)(2,1)S(1)} %collective-permute-done.14, bf16[32,7168]{1,0:T(8,128)(2,1)S(1)} %collective-permute-done.16), kind=kLoop, calls=%fused_computation.28 | loop fusion | flops 5505024 | bytes 6422528 | tf_op jit(solution)/shard_map/convert_element_type | solution.py:74
  145.7 0.2 collective-permute-start.15
  145.9 1.3 collective-permute-start.17
  147.2 14.9 %collective-permute-done.7 = bf16[64,7168]{1,0:T(8,128)(2,1)S(1)} collective-permute-done((bf16[64,7168]{1,0:T(8,128)(2,1)S(1)}, bf16[64,7168]{1,0:T(8,128)(2,1)S(1)}, u32[]{:S(2)}, u32[]{:S(2)}) %collective-permute-start.7) | collective-permute-done | bytes 917536 | tf_op jit(solution)/shard_map/ppermute | solution.py:54
  162.1 1.2 collective-permute-done.9
  163.2 1.4 fusion.19
  164.6 17.1 %collective-permute-done.15 = bf16[64,7168]{1,0:T(8,128)(2,1)S(1)} collective-permute-done((bf16[64,7168]{1,0:T(8,128)(2,1)S(1)}, bf16[64,7168]{1,0:T(8,128)(2,1)S(1)}, u32[]{:S(2)}, u32[]{:S(2)}) %collective-permute-start.15) | collective-permute-done | bytes 917536 | tf_op jit(solution)/shard_map/ppermute | solution.py:54
  181.7 1.2 collective-permute-done.17
  182.9 1.4 fusion.20
  (36 shorter events, 0.4 us)
Async XLA Ops:
  4.6 22.7 %collective-permute-start.1 = (bf16[64,7168]{1,0:T(8,128)(2,1)S(1)}, bf16[64,7168]{1,0:T(8,128)(2,1)S(1)}, u32[]{:S(2)}, u32[]{:S(2)}) collective-permute-start(bf16[64,7168]{1,0:T(8,128)(2,1)S(1)} %get-tuple-element.50), channel_id=1, source_target_pairs={{0,6},{2,0},{4,2},{6,4},{1,7},{3,1},{5,3},{7,5},{8,14},{10,8},{12,... | collective-permute-start | bytes 2752520 | tf_op jit(solution)/shard_map/ppermute | solution.py:54
  8.2 22.2 %collective-permute-start = (bf16[64,7168]{1,0:T(8,128)(2,1)S(1)}, bf16[64,7168]{1,0:T(8,128)(2,1)S(1)}, u32[]{:S(2)}, u32[]{:S(2)}) collective-permute-start(bf16[64,7168]{1,0:T(8,128)(2,1)S(1)} %get-tuple-element.50), channel_id=1, source_target_pairs={{0,2},{2,4},{4,6},{6,0},{1,3},{3,5},{5,7},{7,1},{8,10},{10,12},{12... | collective-permute-start | bytes 2752520 | tf_op jit(solution)/shard_map/ppermute | solution.py:54
  30.7 31.7 %collective-permute-start.3 = (bf16[96,7168]{1,0:T(8,128)(2,1)S(1)}, bf16[96,7168]{1,0:T(8,128)(2,1)S(1)}, u32[]{:S(2)}, u32[]{:S(2)}) collective-permute-start(bf16[96,7168]{1,0:T(8,128)(2,1)S(1)} %get-tuple-element.43), channel_id=1, source_target_pairs={{0,6},{2,0},{4,2},{6,4},{1,7},{3,1},{5,3},{7,5},{8,14},{10,8},{12,... | collective-permute-start | bytes 4128776 | tf_op jit(solution)/shard_map/ppermute | solution.py:54
  31.1 31.1 %collective-permute-start.2 = (bf16[96,7168]{1,0:T(8,128)(2,1)S(1)}, bf16[96,7168]{1,0:T(8,128)(2,1)S(1)}, u32[]{:S(2)}, u32[]{:S(2)}) collective-permute-start(bf16[96,7168]{1,0:T(8,128)(2,1)S(1)} %get-tuple-element.44), channel_id=1, source_target_pairs={{0,2},{2,4},{4,6},{6,0},{1,3},{3,5},{5,7},{7,1},{8,10},{10,12},{12... | collective-permute-start | bytes 4128776 | tf_op jit(solution)/shard_map/ppermute | solution.py:54
  62.5 2.9 %copy-start.5 = (bf16[512,7168]{1,0:T(8,128)(2,1)}, bf16[512,7168]{1,0:T(8,128)(2,1)S(1)}, u32[]{:S(2)}) copy-start(bf16[512,7168]{1,0:T(8,128)(2,1)S(1)} %get-tuple-element.28) | copy-start | bytes 22020100
  62.5 10.9 %collective-permute-start.11 = (bf16[32,7168]{1,0:T(8,128)(2,1)S(1)}, bf16[32,7168]{1,0:T(8,128)(2,1)S(1)}, u32[]{:S(2)}, u32[]{:S(2)}) collective-permute-start(bf16[32,7168]{1,0:T(8,128)(2,1)S(1)} %get-tuple-element.27), channel_id=1, source_target_pairs={{0,6},{2,0},{4,2},{6,4},{1,7},{3,1},{5,3},{7,5},{8,14},{10,8},{12,... | collective-permute-start | bytes 1376264 | tf_op jit(solution)/shard_map/ppermute | solution.py:54
  62.7 10.6 %collective-permute-start.10 = (bf16[32,7168]{1,0:T(8,128)(2,1)S(1)}, bf16[32,7168]{1,0:T(8,128)(2,1)S(1)}, u32[]{:S(2)}, u32[]{:S(2)}) collective-permute-start(bf16[32,7168]{1,0:T(8,128)(2,1)S(1)} %get-tuple-element.30), channel_id=1, source_target_pairs={{0,2},{2,4},{4,6},{6,0},{1,3},{3,5},{5,7},{7,1},{8,10},{10,12},{12... | collective-permute-start | bytes 1376264 | tf_op jit(solution)/shard_map/ppermute | solution.py:54
  65.4 11.7 %collective-permute-start.4 = (bf16[256,7168]{1,0:T(8,128)(2,1)S(1)}, bf16[256,7168]{1,0:T(8,128)(2,1)S(1)}, u32[]{:S(2)}, u32[]{:S(2)}) collective-permute-start(bf16[256,7168]{1,0:T(8,128)(2,1)S(1)} %get-tuple-element.29), channel_id=1, source_target_pairs={{0,1},{1,0},{2,3},{3,2},{4,5},{5,4},{6,7},{7,6},{8,9},{9,8},{10,11... | collective-permute-start | bytes 11010056 | tf_op jit(solution)/shard_map/ppermute | solution.py:58
  73.5 19.7 %collective-permute-start.12 = (bf16[256,7168]{1,0:T(8,128)(2,1)S(1)}, bf16[256,7168]{1,0:T(8,128)(2,1)S(1)}, u32[]{:S(2)}, u32[]{:S(2)}) collective-permute-start(bf16[256,7168]{1,0:T(8,128)(2,1)S(1)} %get-tuple-element.45), channel_id=1, source_target_pairs={{0,1},{1,0},{2,3},{3,2},{4,5},{5,4},{6,7},{7,6},{8,9},{9,8},{10,11... | collective-permute-start | bytes 11010056 | tf_op jit(solution)/shard_map/ppermute | solution.py:58
  77.1 3.4 %copy-start.4 = (bf16[1,7168,256]{2,1,0:T(8,128)(2,1)S(1)}, bf16[1,7168,256]{2,1,0:T(8,128)(2,1)}, u32[]{:S(2)}) copy-start(bf16[1,7168,256]{2,1,0:T(8,128)(2,1)} %param.9) | copy-start | bytes 11010052
  80.5 5.3 %copy-start.1 = (bf16[1,7168,256]{2,1,0:T(8,128)(2,1)S(1)}, bf16[1,7168,256]{2,1,0:T(8,128)(2,1)}, u32[]{:S(2)}) copy-start(bf16[1,7168,256]{2,1,0:T(8,128)(2,1)} %param.10) | copy-start | bytes 11010052
  80.5 6.3 %copy-start.6 = (bf16[512,7168]{1,0:T(8,128)(2,1)S(1)}, bf16[512,7168]{1,0:T(8,128)(2,1)}, u32[]{:S(2)}) copy-start(bf16[512,7168]{1,0:T(8,128)(2,1)} %constant_dynamic-update-slice_fusion.3) | copy-start | bytes 22020100
  86.8 2.1 %copy-start = (bf16[1,256,7168]{2,1,0:T(8,128)(2,1)S(1)}, bf16[1,256,7168]{2,1,0:T(8,128)(2,1)}, u32[]{:S(2)}) copy-start(bf16[1,256,7168]{2,1,0:T(8,128)(2,1)} %param.11) | copy-start | bytes 11010052
  90.0 43.7 %copy-start.2 = (bf16[256,7168]{1,0:T(8,128)(2,1)}, bf16[256,7168]{1,0:T(8,128)(2,1)S(1)}, u32[]{:S(2)}) copy-start(bf16[256,7168]{1,0:T(8,128)(2,1)S(1)} %convolution_convert_fusion.3) | copy-start | bytes 11010052
  93.2 25.8 %collective-permute-start.5 = (bf16[256,7168]{1,0:T(8,128)(2,1)}, bf16[256,7168]{1,0:T(8,128)(2,1)}, u32[]{:S(2)}, u32[]{:S(2)}) collective-permute-start(bf16[256,7168]{1,0:T(8,128)(2,1)} %convolution_convert_fusion.4), channel_id=1, source_target_pairs={{0,1},{1,0},{2,3},{3,2},{4,5},{5,4},{6,7},{7,6},{8,9},{9,8},{10,11... | collective-permute-start | bytes 11010056 | tf_op jit(solution)/shard_map/ppermute | solution.py:58
  99.8 23.4 %collective-permute-start.13 = (bf16[256,7168]{1,0:T(8,128)(2,1)}, bf16[256,7168]{1,0:T(8,128)(2,1)}, u32[]{:S(2)}, u32[]{:S(2)}) collective-permute-start(bf16[256,7168]{1,0:T(8,128)(2,1)} %fusion.1), channel_id=1, source_target_pairs={{0,1},{1,0},{2,3},{3,2},{4,5},{5,4},{6,7},{7,6},{8,9},{9,8},{10,11... | collective-permute-start | bytes 11010056 | tf_op jit(solution)/shard_map/ppermute | solution.py:58
  102.6 41.0 %copy-start.3 = (bf16[256,7168]{1,0:T(8,128)(2,1)}, bf16[256,7168]{1,0:T(8,128)(2,1)S(1)}, u32[]{:S(2)}) copy-start(bf16[256,7168]{1,0:T(8,128)(2,1)S(1)} %fusion) | copy-start | bytes 11010052
  102.6 8.4 %slice-start.2 = ((s8[7340032]{0:T(1024)(128)(4,1)}), s8[4194304]{0:T(1024)(128)(4,1)S(1)}, s32[]{:S(2)}) async-start(s8[7340032]{0:T(1024)(128)(4,1)} %bitcast.48), calls=%async_computation.2 | async-start | bytes 8388608
  102.6 8.4 %slice-start.3 = ((s8[7340032]{0:T(1024)(128)(4,1)}), s8[3145728]{0:T(1024)(128)(4,1)S(1)}, s32[]{:S(2)}) async-start(s8[7340032]{0:T(1024)(128)(4,1)} %bitcast.48), calls=%async_computation.3 | async-start | bytes 6291456
  120.4 12.1 %collective-permute-start.6 = (bf16[32,7168]{1,0:T(8,128)(2,1)S(1)}, bf16[32,7168]{1,0:T(8,128)(2,1)S(1)}, u32[]{:S(2)}, u32[]{:S(2)}) collective-permute-start(bf16[32,7168]{1,0:T(8,128)(2,1)S(1)} %get-tuple-element.37), channel_id=1, source_target_pairs={{0,6},{2,0},{4,2},{6,4},{1,7},{3,1},{5,3},{7,5},{8,14},{10,8},{12,... | collective-permute-start | bytes 1376264 | tf_op jit(solution)/shard_map/ppermute | solution.py:54
  120.5 13.2 %collective-permute-start.8 = (bf16[32,7168]{1,0:T(8,128)(2,1)S(1)}, bf16[32,7168]{1,0:T(8,128)(2,1)S(1)}, u32[]{:S(2)}, u32[]{:S(2)}) collective-permute-start(bf16[32,7168]{1,0:T(8,128)(2,1)S(1)} %get-tuple-element.38), channel_id=1, source_target_pairs={{0,2},{2,4},{4,6},{6,0},{1,3},{3,5},{5,7},{7,1},{8,10},{10,12},{12... | collective-permute-start | bytes 1376264 | tf_op jit(solution)/shard_map/ppermute | solution.py:54
  124.7 17.7 %collective-permute-start.14 = (bf16[32,7168]{1,0:T(8,128)(2,1)S(1)}, bf16[32,7168]{1,0:T(8,128)(2,1)S(1)}, u32[]{:S(2)}, u32[]{:S(2)}) collective-permute-start(bf16[32,7168]{1,0:T(8,128)(2,1)S(1)} %get-tuple-element.35), channel_id=1, source_target_pairs={{0,6},{2,0},{4,2},{6,4},{1,7},{3,1},{5,3},{7,5},{8,14},{10,8},{12,... | collective-permute-start | bytes 1376264 | tf_op jit(solution)/shard_map/ppermute | solution.py:54
  126.0 17.5 %collective-permute-start.16 = (bf16[32,7168]{1,0:T(8,128)(2,1)S(1)}, bf16[32,7168]{1,0:T(8,128)(2,1)S(1)}, u32[]{:S(2)}, u32[]{:S(2)}) collective-permute-start(bf16[32,7168]{1,0:T(8,128)(2,1)S(1)} %get-tuple-element.36), channel_id=1, source_target_pairs={{0,2},{2,4},{4,6},{6,0},{1,3},{3,5},{5,7},{7,1},{8,10},{10,12},{12... | collective-permute-start | bytes 1376264 | tf_op jit(solution)/shard_map/ppermute | solution.py:54
  135.8 27.4 %slice-start = ((bf16[256,7168]{1,0:T(8,128)(2,1)}), bf16[64,7168]{1,0:T(8,128)(2,1)S(1)}, s32[]{:S(2)}) async-start(bf16[256,7168]{1,0:T(8,128)(2,1)} %copy-done.2), calls=%async_computation | async-start | bytes 1835008 | tf_op jit(solution)/shard_map/slice | solution.py:66
  135.8 26.2 %collective-permute-start.7 = (bf16[64,7168]{1,0:T(8,128)(2,1)S(1)}, bf16[64,7168]{1,0:T(8,128)(2,1)S(1)}, u32[]{:S(2)}, u32[]{:S(2)}) collective-permute-start(bf16[64,7168]{1,0:T(8,128)(2,1)S(1)} %get-tuple-element.21), channel_id=1, source_target_pairs={{0,6},{2,0},{4,2},{6,4},{1,7},{3,1},{5,3},{7,5},{8,14},{10,8},{12,... | collective-permute-start | bytes 2752520 | tf_op jit(solution)/shard_map/ppermute | solution.py:54
  136.0 27.2 %collective-permute-start.9 = (bf16[64,7168]{1,0:T(8,128)(2,1)S(1)}, bf16[64,7168]{1,0:T(8,128)(2,1)S(1)}, u32[]{:S(2)}, u32[]{:S(2)}) collective-permute-start(bf16[64,7168]{1,0:T(8,128)(2,1)S(1)} %get-tuple-element.22), channel_id=1, source_target_pairs={{0,2},{2,4},{4,6},{6,0},{1,3},{3,5},{5,7},{7,1},{8,10},{10,12},{12... | collective-permute-start | bytes 2752520 | tf_op jit(solution)/shard_map/ppermute | solution.py:54
  145.6 37.2 %slice-start.1 = ((bf16[256,7168]{1,0:T(8,128)(2,1)}), bf16[64,7168]{1,0:T(8,128)(2,1)S(1)}, s32[]{:S(2)}) async-start(bf16[256,7168]{1,0:T(8,128)(2,1)} %copy-done.3), calls=%async_computation.1 | async-start | bytes 1835008 | tf_op jit(solution)/shard_map/slice | solution.py:66
  145.7 36.1 %collective-permute-start.15 = (bf16[64,7168]{1,0:T(8,128)(2,1)S(1)}, bf16[64,7168]{1,0:T(8,128)(2,1)S(1)}, u32[]{:S(2)}, u32[]{:S(2)}) collective-permute-start(bf16[64,7168]{1,0:T(8,128)(2,1)S(1)} %get-tuple-element.19), channel_id=1, source_target_pairs={{0,6},{2,0},{4,2},{6,4},{1,7},{3,1},{5,3},{7,5},{8,14},{10,8},{12,... | collective-permute-start | bytes 2752520 | tf_op jit(solution)/shard_map/ppermute | solution.py:54
  145.9 37.0 %collective-permute-start.17 = (bf16[64,7168]{1,0:T(8,128)(2,1)S(1)}, bf16[64,7168]{1,0:T(8,128)(2,1)S(1)}, u32[]{:S(2)}, u32[]{:S(2)}) collective-permute-start(bf16[64,7168]{1,0:T(8,128)(2,1)S(1)} %get-tuple-element.20), channel_id=1, source_target_pairs={{0,2},{2,4},{4,6},{6,0},{1,3},{3,5},{5,7},{7,1},{8,10},{10,12},{12... | collective-permute-start | bytes 2752520 | tf_op jit(solution)/shard_map/ppermute | solution.py:54

commit v6 on v3

--- a/solution.py
+++ b/solution.py
@@ -57,11 +57,13 @@
 def scatter_rows(other, mine):
     slots = mine.shape[0] // 4
     cut = slots // 2
-    got = core_swap(other)
-    own, prev, nxt, far = (
+    got_far = core_swap(other[3 * slots:])
+    got = core_swap(other[:3 * slots])
+    far = mine[3 * slots:].astype(jnp.float32) + got_far.astype(jnp.float32)
+    own, prev, nxt = (
         mine[k * slots:(k + 1) * slots].astype(jnp.float32)
         + got[k * slots:(k + 1) * slots].astype(jnp.float32)
-        for k in range(4)
+        for k in range(3)
     )
     back_prev = y_shift(far[:cut].astype(jnp.bfloat16), -1)
     back_next = y_shift(far[cut:].astype(jnp.bfloat16), 1)

time: 199 us -> 207 us (1.040)
  waiting for transfers between devices: 99.6 us -> 103 us
  local copies, waits for them, and re-layouts: 17.4 us -> 20.7 us
    ppermute x14, waiting for transfers between devices: 99.6 us -> 103 us  [y_shift(): lax.ppermute(value, 'y', [(i, (i + distance) % size) for i in range(size)])]
    slice x1 -> x3, local copies, waits for them, and re-layouts: 2.27 us -> 4.45 us  [the longest x2 3.47 us: scatter_rows(): got = core_swap(other[:3 * slots])]
    unnamed x20 -> x24, local copies, waits for them, and re-layouts: 7.46 us -> 8.89 us
    ppermute x4 -> x6, starting transfers between devices: 7.5 us -> 7.77 us  [core_swap(): return lax.ppermute(value, 'core', [(0, 1), (1, 0)])]
  transfers between devices with their start and end apart: 18 -> 20, of which waited for: 12 -> 12; matrix products, arithmetic and copies ran while one was open for 35% -> 34% of each run, Pallas kernels for 0% -> 0%
where the time goes in v6:
time: 207 us; the launch traced here: 205 us
  waiting for transfers between devices  103 us (50%)
  matrix products  46.6 us (23%)
  local copies, waits for them, and re-layouts  20.7 us (10%)
  starting transfers between devices  20.5 us (10%)
  other arithmetic  12.9 us (6%)
    ppermute x14, waiting for transfers between devices, y_shift(): lax.ppermute(value, 'y', [(i, (i + distance) % size) for i in range(size)])  103 us
    dot_general x3, matrix products, contract_first(): lax.dot_general(left, right, (((0,), (0,)), ((), ())), preferred_element_...  19.6 us
    ppermute x14, starting transfers between devices, y_shift(): lax.ppermute(value, 'y', [(i, (i + distance) % size) for i in range(size)])  12.8 us
    dot_general x5, matrix products, contract_last(): lax.dot_general(left, right, (((1,), (1,)), ((), ())), preferred_element_...  12.5 us
    unnamed x24, local copies, waits for them, and re-layouts  8.89 us
    ppermute x6, starting transfers between devices, core_swap(): return lax.ppermute(value, 'core', [(0, 1), (1, 0)])  7.77 us
    dot_general x1, matrix products, expert_work(): gate = jnp.dot(rows, gate_w, preferred_element_type=jnp.float32)  5.29 us
    dot_general x1, matrix products, expert_work(): up = jnp.dot(rows, up_w, preferred_element_type=jnp.float32)  5.14 us
  transfers between devices with their start and end apart: 20, of which 12 were waited for; matrix products, arithmetic and copies ran while one was open for 34% of the time, Pallas kernels for 0%

profile of v6, /device:TPU:1, one launch (start us, length us, event | category | flops | bytes accessed | tf_op | source)
XLA Modules:
  0.0 205.4 jit_solution(10134322456301829813)
XLA Ops:
  0.7 0.8 select_reduce_fusion
  1.5 0.6 fusion.24
  2.8 2.9 %constant_dynamic-update-slice_fusion.9 = (bf16[256,7168]{1,0:T(8,128)(2,1)}, bf16[64,7168]{1,0:T(8,128)(2,1)S(1)}, bf16[256,7168]{1,0:T(8,128)(2,1)S(1)}, bf16[64,7168]{1,0:T(8,128)(2,1)S(1)}) fusion(bf16[60,7168]{1,0:T(8,128)(2,1)} %bitcast.47, pred[64]{0:T(512)(128)(4,1)S(1)} %iota_compare_fusion.1, bf16[60,7168]{1,0:T(8,128)(2,1)} %bitcast.48), kind=kLoop, calls=%fused_computation.63 | loop fusion | flops 917502 | bytes 5390400
  5.7 3.6 %collective-permute-start.1 = (bf16[64,7168]{1,0:T(8,128)(2,1)S(1)}, bf16[64,7168]{1,0:T(8,128)(2,1)S(1)}, u32[]{:S(2)}, u32[]{:S(2)}) collective-permute-start(bf16[64,7168]{1,0:T(8,128)(2,1)S(1)} %get-tuple-element.50), channel_id=1, source_target_pairs={{0,6},{2,0},{4,2},{6,4},{1,7},{3,1},{5,3},{7,5},{8,14},{10,8},{12,... | collective-permute-start | bytes 2752520 | tf_op jit(solution)/shard_map/ppermute | solution.py:50
  9.2 1.1 constant_dynamic-update-slice_fusion.6
  10.3 18.0 %collective-permute-done.1 = bf16[64,7168]{1,0:T(8,128)(2,1)S(1)} collective-permute-done((bf16[64,7168]{1,0:T(8,128)(2,1)S(1)}, bf16[64,7168]{1,0:T(8,128)(2,1)S(1)}, u32[]{:S(2)}, u32[]{:S(2)}) %collective-permute-start.1) | collective-permute-done | bytes 917536 | tf_op jit(solution)/shard_map/ppermute | solution.py:50
  28.3 3.1 %collective-permute-done = bf16[64,7168]{1,0:T(8,128)(2,1)S(1)} collective-permute-done((bf16[64,7168]{1,0:T(8,128)(2,1)S(1)}, bf16[64,7168]{1,0:T(8,128)(2,1)S(1)}, u32[]{:S(2)}, u32[]{:S(2)}) %collective-permute-start) | collective-permute-done | bytes 917536 | tf_op jit(solution)/shard_map/ppermute | solution.py:50
  31.4 0.3 pad_maximum_fusion
  31.7 0.4 collective-permute-start.3
  32.1 1.1 collective-permute-start.2
  33.3 1.1 constant_dynamic-update-slice_fusion.1
  34.4 1.1 constant_dynamic-update-slice_fusion
  35.4 27.8 %collective-permute-done.2 = bf16[96,7168]{1,0:T(8,128)(2,1)S(1)} collective-permute-done((bf16[96,7168]{1,0:T(8,128)(2,1)S(1)}, bf16[96,7168]{1,0:T(8,128)(2,1)S(1)}, u32[]{:S(2)}, u32[]{:S(2)}) %collective-permute-start.2) | collective-permute-done | bytes 1376288 | tf_op jit(solution)/shard_map/ppermute | solution.py:50
  63.3 0.9 fusion.27
  64.2 0.9 fusion.26
  65.0 1.5 collective-permute-start.11
  66.5 3.2 %collective-permute-start.4 = (bf16[256,7168]{1,0:T(8,128)(2,1)S(1)}, bf16[256,7168]{1,0:T(8,128)(2,1)S(1)}, u32[]{:S(2)}, u32[]{:S(2)}) collective-permute-start(bf16[256,7168]{1,0:T(8,128)(2,1)S(1)} %get-tuple-element.29), channel_id=1, source_target_pairs={{0,1},{1,0},{2,3},{3,2},{4,5},{5,4},{6,7},{7,6},{8,9},{9,8},{10,11... | collective-permute-start | bytes 11010056 | tf_op jit(solution)/shard_map/ppermute | solution.py:54
  69.7 1.1 slice_dynamic-update-slice_fusion.3
  70.8 1.1 slice_dynamic-update-slice_fusion.1
  71.9 3.8 %collective-permute-done.11 = bf16[32,7168]{1,0:T(8,128)(2,1)S(1)} collective-permute-done((bf16[32,7168]{1,0:T(8,128)(2,1)S(1)}, bf16[32,7168]{1,0:T(8,128)(2,1)S(1)}, u32[]{:S(2)}, u32[]{:S(2)}) %collective-permute-start.11) | collective-permute-done | bytes 458784 | tf_op jit(solution)/shard_map/ppermute | solution.py:50
  75.7 0.8 constant_dynamic-update-slice_fusion.8
  76.5 0.8 constant_dynamic-update-slice_fusion.7
  77.3 3.5 %collective-permute-start.13 = (bf16[256,7168]{1,0:T(8,128)(2,1)}, bf16[256,7168]{1,0:T(8,128)(2,1)S(1)}, u32[]{:S(2)}, u32[]{:S(2)}) collective-permute-start(bf16[256,7168]{1,0:T(8,128)(2,1)} %get-tuple-element.45), channel_id=1, source_target_pairs={{0,1},{1,0},{2,3},{3,2},{4,5},{5,4},{6,7},{7,6},{8,9},{9,8},{10,11... | collective-permute-start | bytes 11010056 | tf_op jit(solution)/shard_map/ppermute | solution.py:54
  80.8 2.1 %constant_dynamic-update-slice_fusion.3 = bf16[512,7168]{1,0:T(8,128)(2,1)} fusion(bf16[512,7168]{1,0:T(8,128)(2,1)} %get-tuple-element.28, bf16[256,7168]{1,0:T(8,128)(2,1)S(1)} %collective-permute-done.4), kind=kLoop, calls=%fused_computation.57 | loop fusion | bytes 7340032 | tf_op jit(solution)/shard_map/concatenate | solution.py:104
  82.9 1.3 copy-done.2
  84.2 5.3 %fusion.16 = f32[512,256]{1,0:T(8,128)S(1)} fusion(bf16[512,7168]{1,0:T(8,128)(2,1)} %constant_dynamic-update-slice_fusion.3, bf16[1,7168,256]{2,1,0:T(8,128)(2,1)S(1)} %copy-done.2), kind=kOutput, calls=%fused_computation.22 | convolution fusion | flops 1879048192 | bytes 11534336 | tf_op jit(solution)/shard_map/dot_general | solution.py:25
  89.5 5.1 %multiply_convert_fusion.2 = (bf16[512,256]{1,0:T(8,128)(2,1)S(1)}, f32[512,256]{1,0:T(8,128)S(1)}) fusion(f32[512,256]{1,0:T(8,128)S(1)} %fusion.16, bf16[512,7168]{1,0:T(8,128)(2,1)} %constant_dynamic-update-slice_fusion.3, bf16[1,7168,256]{2,1,0:T(8,128)(2,1)S(1)} %copy-done), kind=kOutput, calls=%fused_computation.45 | convolution fusion | flops 1879834624 | bytes 12320768 | tf_op jit(solution)/shard_map/dot_general | solution.py:26
  94.7 4.1 %convolution_convert_fusion = bf16[512,7168]{1,0:T(8,128)(2,1)S(1)} fusion(bf16[512,256]{1,0:T(8,128)(2,1)S(1)} %get-tuple-element.12, bf16[1,256,7168]{2,1,0:T(8,128)(2,1)} %param.11), kind=kOutput, calls=%fused_computation | convolution fusion | flops 1882718208 | bytes 11272192 | tf_op jit(solution)/shard_map/dot_general | solution.py:29
  98.8 1.7 slice.127
  100.5 1.0 fusion.25
  101.5 0.5 collective-permute-start.5
  102.3 7.0 %multiply_convert_fusion = (bf16[512,256]{1,0:T(8,128)(2,1)S(1)}, bf16[512,256]{1,0:T(8,128)(2,1)S(1)}) fusion(f32[512,256]{1,0:T(8,128)S(1)} %fusion.16, f32[512,256]{1,0:T(8,128)S(1)} %get-tuple-element.10, bf16[512,7168]{1,0:T(8,128)(2,1)S(1)} %constant_dynamic-update-slice_fusion.10, bf16[1,256,7168]{2,1,0:T(8,128)(2,1)} %param.11), kind=kOutput, calls=%fused_computation.42 | convolution fusion | flops 1880752128 | bytes 12582912 | tf_op jit(solution)/shard_map/dot_general | solution.py:13
  109.3 7.2 %fusion.3 = bf16[1,7168,256]{2,1,0:T(8,128)(2,1)} fusion(bf16[512,7168]{1,0:T(8,128)(2,1)} %constant_dynamic-update-slice_fusion.3, bf16[512,256]{1,0:T(8,128)(2,1)S(1)} %get-tuple-element.33), kind=kOutput, calls=%fused_computation.9 | convolution fusion | flops 1880883200 | bytes 11272192 | tf_op jit(solution)/shard_map/dot_general | solution.py:19
  116.5 1.1 fusion.12
  117.6 2.1 %fusion.1 = bf16[256,7168]{1,0:T(8,128)(2,1)S(1)} fusion(f32[256,7168]{1,0:T(8,128)S(1)} %fusion.12, bf16[1,7168,256]{2,1,0:T(8,128)(2,1)S(1)} %copy-done, bf16[512,256]{1,0:T(8,128)(2,1)} %copy-done.5), kind=kOutput, calls=%fused_computation.4 | convolution fusion | flops 943194112 | bytes 14811136 | tf_op jit(solution)/shard_map/dot_general | solution.py:13
  119.7 1.0 slice.185
  120.7 1.8 slice.180
  122.4 1.1 fusion.14
  123.6 0.3 slice-done.1
  123.9 1.2 slice-done.2
  125.0 4.0 %fusion.4 = bf16[1,256,7168]{2,1,0:T(8,128)(2,1)} fusion(bf16[512,256]{1,0:T(8,128)(2,1)S(1)} %get-tuple-element.12, bf16[512,7168]{1,0:T(8,128)(2,1)S(1)} %bitcast.46), kind=kOutput, calls=%fused_computation.10 | convolution fusion | flops 1880883200 | bytes 11272192 | tf_op jit(solution)/shard_map/dot_general | solution.py:19
  129.0 0.5 collective-permute-start.14
  129.6 1.2 fusion
  130.7 8.4 %fusion.2 = bf16[1,7168,256]{2,1,0:T(8,128)(2,1)} fusion(bf16[512,7168]{1,0:T(8,128)(2,1)} %constant_dynamic-update-slice_fusion.3, bf16[512,256]{1,0:T(8,128)(2,1)S(1)} %get-tuple-element.34), kind=kOutput, calls=%fused_computation.8 | convolution fusion | flops 1880883200 | bytes 11272192 | tf_op jit(solution)/shard_map/dot_general | solution.py:19
  139.1 1.4 add_convert_fusion.7
  140.7 1.5 collective-permute-start.9
  142.1 1.4 add_convert_fusion.3
  143.6 1.4 collective-permute-start.16
  144.9 7.8 %collective-permute-done.7 = bf16[32,7168]{1,0:T(8,128)(2,1)S(1)} collective-permute-done((bf16[32,7168]{1,0:T(8,128)(2,1)S(1)}, bf16[32,7168]{1,0:T(8,128)(2,1)S(1)}, u32[]{:S(2)}, u32[]{:S(2)}) %collective-permute-start.7) | collective-permute-done | bytes 458784 | tf_op jit(solution)/shard_map/ppermute | solution.py:50
  153.0 1.0 collective-permute-done.9
  154.0 2.1 %add_convert_fusion.6 = (bf16[64,7168]{1,0:T(8,128)(2,1)S(1)}, bf16[64,7168]{1,0:T(8,128)(2,1)S(1)}) fusion(bf16[192,7168]{1,0:T(8,128)(2,1)} %collective-permute-done.5, bf16[32,7168]{1,0:T(8,128)(2,1)S(1)} %collective-permute-done.7, bf16[512,7168]{1,0:T(8,128)(2,1)S(1)} %convolution_convert_fusion, bf16[32,7168]{1,0:T(8,128)(2,1)S(1)} %collective-permute-done.9), kind=kLoop, calls=%fused_computation.30 | loop fusion | flops 5505024 | bytes 6422528 | tf_op jit(solution)/shard_map/convert_element_type | solution.py:72
  156.1 1.5 collective-permute-start.8
  157.6 1.2 slice.162
  158.9 3.7 %collective-permute-done.16 = bf16[32,7168]{1,0:T(8,128)(2,1)S(1)} collective-permute-done((bf16[32,7168]{1,0:T(8,128)(2,1)S(1)}, bf16[32,7168]{1,0:T(8,128)(2,1)S(1)}, u32[]{:S(2)}, u32[]{:S(2)}) %collective-permute-start.16) | collective-permute-done | bytes 458784 | tf_op jit(solution)/shard_map/ppermute | solution.py:50
  162.5 2.1 %collective-permute-done.18 = bf16[32,7168]{1,0:T(8,128)(2,1)S(1)} collective-permute-done((bf16[32,7168]{1,0:T(8,128)(2,1)S(1)}, bf16[32,7168]{1,0:T(8,128)(2,1)S(1)}, u32[]{:S(2)}, u32[]{:S(2)}) %collective-permute-start.18) | collective-permute-done | bytes 458784 | tf_op jit(solution)/shard_map/ppermute | solution.py:50
  164.7 0.6 add_convert_fusion.2
  165.3 0.9 collective-permute-start.17
  166.2 0.6 collective-permute-start.19
  166.9 15.3 %collective-permute-done.8 = bf16[64,7168]{1,0:T(8,128)(2,1)S(1)} collective-permute-done((bf16[64,7168]{1,0:T(8,128)(2,1)S(1)}, bf16[64,7168]{1,0:T(8,128)(2,1)S(1)}, u32[]{:S(2)}, u32[]{:S(2)}) %collective-permute-start.8) | collective-permute-done | bytes 917536 | tf_op jit(solution)/shard_map/ppermute | solution.py:50
  182.2 2.1 %collective-permute-done.10 = bf16[64,7168]{1,0:T(8,128)(2,1)S(1)} collective-permute-done((bf16[64,7168]{1,0:T(8,128)(2,1)S(1)}, bf16[64,7168]{1,0:T(8,128)(2,1)S(1)}, u32[]{:S(2)}, u32[]{:S(2)}) %collective-permute-start.10) | collective-permute-done | bytes 917536 | tf_op jit(solution)/shard_map/ppermute | solution.py:50
  184.3 1.4 fusion.18
  185.7 16.1 %collective-permute-done.17 = bf16[64,7168]{1,0:T(8,128)(2,1)S(1)} collective-permute-done((bf16[64,7168]{1,0:T(8,128)(2,1)S(1)}, bf16[64,7168]{1,0:T(8,128)(2,1)S(1)}, u32[]{:S(2)}, u32[]{:S(2)}) %collective-permute-start.17) | collective-permute-done | bytes 917536 | tf_op jit(solution)/shard_map/ppermute | solution.py:50
  201.9 2.1 %collective-permute-done.19 = bf16[64,7168]{1,0:T(8,128)(2,1)S(1)} collective-permute-done((bf16[64,7168]{1,0:T(8,128)(2,1)S(1)}, bf16[64,7168]{1,0:T(8,128)(2,1)S(1)}, u32[]{:S(2)}, u32[]{:S(2)}) %collective-permute-start.19) | collective-permute-done | bytes 917536 | tf_op jit(solution)/shard_map/ppermute | solution.py:50
  204.0 1.4 fusion.19
  (42 shorter events, 0.9 us)
Async XLA Ops:
  5.7 22.6 %collective-permute-start.1 = (bf16[64,7168]{1,0:T(8,128)(2,1)S(1)}, bf16[64,7168]{1,0:T(8,128)(2,1)S(1)}, u32[]{:S(2)}, u32[]{:S(2)}) collective-permute-start(bf16[64,7168]{1,0:T(8,128)(2,1)S(1)} %get-tuple-element.50), channel_id=1, source_target_pairs={{0,6},{2,0},{4,2},{6,4},{1,7},{3,1},{5,3},{7,5},{8,14},{10,8},{12,... | collective-permute-start | bytes 2752520 | tf_op jit(solution)/shard_map/ppermute | solution.py:50
  9.2 22.2 %collective-permute-start = (bf16[64,7168]{1,0:T(8,128)(2,1)S(1)}, bf16[64,7168]{1,0:T(8,128)(2,1)S(1)}, u32[]{:S(2)}, u32[]{:S(2)}) collective-permute-start(bf16[64,7168]{1,0:T(8,128)(2,1)S(1)} %get-tuple-element.50), channel_id=1, source_target_pairs={{0,2},{2,4},{4,6},{6,0},{1,3},{3,5},{5,7},{7,1},{8,10},{10,12},{12... | collective-permute-start | bytes 2752520 | tf_op jit(solution)/shard_map/ppermute | solution.py:50
  31.7 32.4 %collective-permute-start.3 = (bf16[96,7168]{1,0:T(8,128)(2,1)S(1)}, bf16[96,7168]{1,0:T(8,128)(2,1)S(1)}, u32[]{:S(2)}, u32[]{:S(2)}) collective-permute-start(bf16[96,7168]{1,0:T(8,128)(2,1)S(1)} %get-tuple-element.43), channel_id=1, source_target_pairs={{0,6},{2,0},{4,2},{6,4},{1,7},{3,1},{5,3},{7,5},{8,14},{10,8},{12,... | collective-permute-start | bytes 4128776 | tf_op jit(solution)/shard_map/ppermute | solution.py:50
  32.1 31.1 %collective-permute-start.2 = (bf16[96,7168]{1,0:T(8,128)(2,1)S(1)}, bf16[96,7168]{1,0:T(8,128)(2,1)S(1)}, u32[]{:S(2)}, u32[]{:S(2)}) collective-permute-start(bf16[96,7168]{1,0:T(8,128)(2,1)S(1)} %get-tuple-element.44), channel_id=1, source_target_pairs={{0,2},{2,4},{4,6},{6,0},{1,3},{3,5},{5,7},{7,1},{8,10},{10,12},{12... | collective-permute-start | bytes 4128776 | tf_op jit(solution)/shard_map/ppermute | solution.py:50
  65.0 11.5 %collective-permute-start.12 = (bf16[32,7168]{1,0:T(8,128)(2,1)S(1)}, bf16[32,7168]{1,0:T(8,128)(2,1)S(1)}, u32[]{:S(2)}, u32[]{:S(2)}) collective-permute-start(bf16[32,7168]{1,0:T(8,128)(2,1)S(1)} %get-tuple-element.27), channel_id=1, source_target_pairs={{0,6},{2,0},{4,2},{6,4},{1,7},{3,1},{5,3},{7,5},{8,14},{10,8},{12,... | collective-permute-start | bytes 1376264 | tf_op jit(solution)/shard_map/ppermute | solution.py:50
  65.0 10.6 %collective-permute-start.11 = (bf16[32,7168]{1,0:T(8,128)(2,1)S(1)}, bf16[32,7168]{1,0:T(8,128)(2,1)S(1)}, u32[]{:S(2)}, u32[]{:S(2)}) collective-permute-start(bf16[32,7168]{1,0:T(8,128)(2,1)S(1)} %get-tuple-element.30), channel_id=1, source_target_pairs={{0,2},{2,4},{4,6},{6,0},{1,3},{3,5},{5,7},{7,1},{8,10},{10,12},{12... | collective-permute-start | bytes 1376264 | tf_op jit(solution)/shard_map/ppermute | solution.py:50
  66.5 14.3 %collective-permute-start.4 = (bf16[256,7168]{1,0:T(8,128)(2,1)S(1)}, bf16[256,7168]{1,0:T(8,128)(2,1)S(1)}, u32[]{:S(2)}, u32[]{:S(2)}) collective-permute-start(bf16[256,7168]{1,0:T(8,128)(2,1)S(1)} %get-tuple-element.29), channel_id=1, source_target_pairs={{0,1},{1,0},{2,3},{3,2},{4,5},{5,4},{6,7},{7,6},{8,9},{9,8},{10,11... | collective-permute-start | bytes 11010056 | tf_op jit(solution)/shard_map/ppermute | solution.py:54
  77.3 24.7 %collective-permute-start.13 = (bf16[256,7168]{1,0:T(8,128)(2,1)}, bf16[256,7168]{1,0:T(8,128)(2,1)S(1)}, u32[]{:S(2)}, u32[]{:S(2)}) collective-permute-start(bf16[256,7168]{1,0:T(8,128)(2,1)} %get-tuple-element.45), channel_id=1, source_target_pairs={{0,1},{1,0},{2,3},{3,2},{4,5},{5,4},{6,7},{7,6},{8,9},{9,8},{10,11... | collective-permute-start | bytes 11010056 | tf_op jit(solution)/shard_map/ppermute | solution.py:54
  80.8 3.4 %copy-start.2 = (bf16[1,7168,256]{2,1,0:T(8,128)(2,1)S(1)}, bf16[1,7168,256]{2,1,0:T(8,128)(2,1)}, u32[]{:S(2)}) copy-start(bf16[1,7168,256]{2,1,0:T(8,128)(2,1)} %param.9) | copy-start | bytes 11010052
  84.2 5.3 %copy-start = (bf16[1,7168,256]{2,1,0:T(8,128)(2,1)S(1)}, bf16[1,7168,256]{2,1,0:T(8,128)(2,1)}, u32[]{:S(2)}) copy-start(bf16[1,7168,256]{2,1,0:T(8,128)(2,1)} %param.10) | copy-start | bytes 11010052
  101.5 37.6 %collective-permute-start.6 = (bf16[64,7168]{1,0:T(8,128)(2,1)}, bf16[64,7168]{1,0:T(8,128)(2,1)}, u32[]{:S(2)}, u32[]{:S(2)}) collective-permute-start(bf16[64,7168]{1,0:T(8,128)(2,1)} %get-tuple-element.20), channel_id=1, source_target_pairs={{0,1},{1,0},{2,3},{3,2},{4,5},{5,4},{6,7},{7,6},{8,9},{9,8},{10,11... | collective-permute-start | bytes 2752520 | tf_op jit(solution)/shard_map/ppermute | solution.py:54
  101.5 52.5 %collective-permute-start.5 = (bf16[192,7168]{1,0:T(8,128)(2,1)}, bf16[192,7168]{1,0:T(8,128)(2,1)}, u32[]{:S(2)}, u32[]{:S(2)}) collective-permute-start(bf16[192,7168]{1,0:T(8,128)(2,1)} %slice.127), channel_id=1, source_target_pairs={{0,1},{1,0},{2,3},{3,2},{4,5},{5,4},{6,7},{7,6},{8,9},{9,8},{10,11... | collective-permute-start | bytes 8257544 | tf_op jit(solution)/shard_map/ppermute | solution.py:54
  102.3 7.0 %copy-start.3 = (bf16[512,7168]{1,0:T(8,128)(2,1)}, bf16[512,7168]{1,0:T(8,128)(2,1)S(1)}, u32[]{:S(2)}) copy-start(bf16[512,7168]{1,0:T(8,128)(2,1)S(1)} %constant_dynamic-update-slice_fusion.10) | copy-start | bytes 22020100
  109.3 7.2 %copy-start.5 = (bf16[512,256]{1,0:T(8,128)(2,1)}, bf16[512,256]{1,0:T(8,128)(2,1)S(1)}, u32[]{:S(2)}) copy-start(bf16[512,256]{1,0:T(8,128)(2,1)S(1)} %get-tuple-element.33) | copy-start | bytes 786436
  120.7 3.2 %slice-start.1 = ((s8[7340032]{0:T(1024)(128)(4,1)}), s8[4194304]{0:T(1024)(128)(4,1)S(1)}, s32[]{:S(2)}) async-start(s8[7340032]{0:T(1024)(128)(4,1)} %bitcast.45), calls=%async_computation.1 | async-start | bytes 8388608
  122.4 2.6 %slice-start.2 = ((s8[7340032]{0:T(1024)(128)(4,1)}), s8[3145728]{0:T(1024)(128)(4,1)S(1)}, s32[]{:S(2)}) async-start(s8[7340032]{0:T(1024)(128)(4,1)} %bitcast.45), calls=%async_computation.2 | async-start | bytes 6291456
  125.0 4.5 %copy-start.6 = (bf16[512,256]{1,0:T(8,128)(2,1)S(1)}, bf16[512,256]{1,0:T(8,128)(2,1)}, u32[]{:S(2)}) copy-start(bf16[512,256]{1,0:T(8,128)(2,1)} %copy-done.5) | copy-start | bytes 786436
  129.0 13.1 %collective-permute-start.15 = (bf16[64,7168]{1,0:T(8,128)(2,1)}, bf16[64,7168]{1,0:T(8,128)(2,1)}, u32[]{:S(2)}, u32[]{:S(2)}) collective-permute-start(bf16[64,7168]{1,0:T(8,128)(2,1)} %slice.185), channel_id=1, source_target_pairs={{0,1},{1,0},{2,3},{3,2},{4,5},{5,4},{6,7},{7,6},{8,9},{9,8},{10,11... | collective-permute-start | bytes 2752520 | tf_op jit(solution)/shard_map/ppermute | solution.py:54
  129.0 35.6 %collective-permute-start.14 = (bf16[192,7168]{1,0:T(8,128)(2,1)}, bf16[192,7168]{1,0:T(8,128)(2,1)S(1)}, u32[]{:S(2)}, u32[]{:S(2)}) collective-permute-start(bf16[192,7168]{1,0:T(8,128)(2,1)} %slice.180), channel_id=1, source_target_pairs={{0,1},{1,0},{2,3},{3,2},{4,5},{5,4},{6,7},{7,6},{8,9},{9,8},{10,11... | collective-permute-start | bytes 8257544 | tf_op jit(solution)/shard_map/ppermute | solution.py:54
  130.7 34.0 %copy-start.1 = (bf16[256,7168]{1,0:T(8,128)(2,1)}, bf16[256,7168]{1,0:T(8,128)(2,1)S(1)}, u32[]{:S(2)}) copy-start(bf16[256,7168]{1,0:T(8,128)(2,1)S(1)} %fusion) | copy-start | bytes 11010052
  140.6 12.1 %collective-permute-start.7 = (bf16[32,7168]{1,0:T(8,128)(2,1)S(1)}, bf16[32,7168]{1,0:T(8,128)(2,1)S(1)}, u32[]{:S(2)}, u32[]{:S(2)}) collective-permute-start(bf16[32,7168]{1,0:T(8,128)(2,1)S(1)} %get-tuple-element.37), channel_id=1, source_target_pairs={{0,6},{2,0},{4,2},{6,4},{1,7},{3,1},{5,3},{7,5},{8,14},{10,8},{12,... | collective-permute-start | bytes 1376264 | tf_op jit(solution)/shard_map/ppermute | solution.py:50
  140.7 13.4 %collective-permute-start.9 = (bf16[32,7168]{1,0:T(8,128)(2,1)S(1)}, bf16[32,7168]{1,0:T(8,128)(2,1)S(1)}, u32[]{:S(2)}, u32[]{:S(2)}) collective-permute-start(bf16[32,7168]{1,0:T(8,128)(2,1)S(1)} %get-tuple-element.38), channel_id=1, source_target_pairs={{0,2},{2,4},{4,6},{6,0},{1,3},{3,5},{5,7},{7,1},{8,10},{10,12},{12... | collective-permute-start | bytes 1376264 | tf_op jit(solution)/shard_map/ppermute | solution.py:50
  143.6 19.0 %collective-permute-start.16 = (bf16[32,7168]{1,0:T(8,128)(2,1)S(1)}, bf16[32,7168]{1,0:T(8,128)(2,1)S(1)}, u32[]{:S(2)}, u32[]{:S(2)}) collective-permute-start(bf16[32,7168]{1,0:T(8,128)(2,1)S(1)} %get-tuple-element.35), channel_id=1, source_target_pairs={{0,6},{2,0},{4,2},{6,4},{1,7},{3,1},{5,3},{7,5},{8,14},{10,8},{12,... | collective-permute-start | bytes 1376264 | tf_op jit(solution)/shard_map/ppermute | solution.py:50
  152.7 12.0 %collective-permute-start.18 = (bf16[32,7168]{1,0:T(8,128)(2,1)S(1)}, bf16[32,7168]{1,0:T(8,128)(2,1)S(1)}, u32[]{:S(2)}, u32[]{:S(2)}) collective-permute-start(bf16[32,7168]{1,0:T(8,128)(2,1)S(1)} %get-tuple-element.36), channel_id=1, source_target_pairs={{0,2},{2,4},{4,6},{6,0},{1,3},{3,5},{5,7},{7,1},{8,10},{10,12},{12... | collective-permute-start | bytes 1376264 | tf_op jit(solution)/shard_map/ppermute | solution.py:50
  156.1 26.1 %collective-permute-start.8 = (bf16[64,7168]{1,0:T(8,128)(2,1)S(1)}, bf16[64,7168]{1,0:T(8,128)(2,1)S(1)}, u32[]{:S(2)}, u32[]{:S(2)}) collective-permute-start(bf16[64,7168]{1,0:T(8,128)(2,1)S(1)} %get-tuple-element.17), channel_id=1, source_target_pairs={{0,6},{2,0},{4,2},{6,4},{1,7},{3,1},{5,3},{7,5},{8,14},{10,8},{12,... | collective-permute-start | bytes 2752520 | tf_op jit(solution)/shard_map/ppermute | solution.py:50
  157.5 26.8 %collective-permute-start.10 = (bf16[64,7168]{1,0:T(8,128)(2,1)S(1)}, bf16[64,7168]{1,0:T(8,128)(2,1)S(1)}, u32[]{:S(2)}, u32[]{:S(2)}) collective-permute-start(bf16[64,7168]{1,0:T(8,128)(2,1)S(1)} %get-tuple-element.18), channel_id=1, source_target_pairs={{0,2},{2,4},{4,6},{6,0},{1,3},{3,5},{5,7},{7,1},{8,10},{10,12},{12... | collective-permute-start | bytes 2752520 | tf_op jit(solution)/shard_map/ppermute | solution.py:50
  164.7 2.2 %copy-start.4 = (bf16[192,7168]{1,0:T(8,128)(2,1)}, bf16[192,7168]{1,0:T(8,128)(2,1)S(1)}, u32[]{:S(2)}) copy-start(bf16[192,7168]{1,0:T(8,128)(2,1)S(1)} %collective-permute-done.14) | copy-start | bytes 8257540
  165.3 38.7 %slice-start = ((bf16[256,7168]{1,0:T(8,128)(2,1)}), bf16[64,7168]{1,0:T(8,128)(2,1)S(1)}, s32[]{:S(2)}) async-start(bf16[256,7168]{1,0:T(8,128)(2,1)} %copy-done.1), calls=%async_computation | async-start | bytes 1835008 | tf_op jit(solution)/shard_map/slice | solution.py:64
  165.3 36.5 %collective-permute-start.17 = (bf16[64,7168]{1,0:T(8,128)(2,1)S(1)}, bf16[64,7168]{1,0:T(8,128)(2,1)S(1)}, u32[]{:S(2)}, u32[]{:S(2)}) collective-permute-start(bf16[64,7168]{1,0:T(8,128)(2,1)S(1)} %get-tuple-element.21), channel_id=1, source_target_pairs={{0,6},{2,0},{4,2},{6,4},{1,7},{3,1},{5,3},{7,5},{8,14},{10,8},{12,... | collective-permute-start | bytes 2752520 | tf_op jit(solution)/shard_map/ppermute | solution.py:50
  166.2 37.8 %collective-permute-start.19 = (bf16[64,7168]{1,0:T(8,128)(2,1)S(1)}, bf16[64,7168]{1,0:T(8,128)(2,1)S(1)}, u32[]{:S(2)}, u32[]{:S(2)}) collective-permute-start(bf16[64,7168]{1,0:T(8,128)(2,1)S(1)} %get-tuple-element.22), channel_id=1, source_target_pairs={{0,2},{2,4},{4,6},{6,0},{1,3},{3,5},{5,7},{7,1},{8,10},{10,12},{12... | collective-permute-start | bytes 2752520 | tf_op jit(solution)/shard_map/ppermute | solution.py:50
  182.2 21.8 %slice-start.3 = ((bf16[192,7168]{1,0:T(8,128)(2,1)}), bf16[64,7168]{1,0:T(8,128)(2,1)S(1)}, s32[]{:S(2)}) async-start(bf16[192,7168]{1,0:T(8,128)(2,1)} %copy-done.4), calls=%async_computation.3 | async-start | bytes 1835008 | tf_op jit(solution)/shard_map/slice | solution.py:65
